TPU v7x, 256 devices: a whole 4x4x8 slice. The times are simulated.
256 devices in a mesh: ax: 32 (over y, z_hi, core), rad: 8 (over z_lo, x).
Axes of the slice: x: 4, y: 4, z: 8 (z_hi: 4, z_lo: 2; z = z_hi * 2 + z_lo), core: 2. Of those that a mesh axis runs over, the one named last changes fastest.
Arguments:
- state: float32 [512, 256, 5, 384], P('ax', 'rad'), may hold values from -6 to 6
- metric: float32 [512, 256, 384], P('ax', 'rad'), may hold values from 0.25 to 4
- deriv: float32 [512, 512], replicated, may hold values from -0.25 to 0.25
- filt_corr: float32 [512, 512], replicated, may hold values from -0.25 to 0.25
- jac_axial: float32 [5, 5], replicated, may hold values from -3 to 3
- jac_radial: float32 [5, 5], replicated, may hold values from -3 to 3
Outputs:
- advanced: float32 [512, 256, 5, 384], P('ax', 'rad')
All inputs are finite; a program needn't handle non-finite values.
Results may differ from a plain program's by a relative error of at most 0.000084.
Values sent between devices are 32-bit elements; how exact they have to be, the bound alone decides.
No kernel may reach another device: no remote copies, remote signals or barrier semaphores. Data moves between devices by JAX's collectives and lax.ppermute only.
A program may use at most 128 MiB of HBM per device.

v0:
```python
import jax
import jax.numpy as jnp
from jax import lax
from jax.sharding import PartitionSpec as P

section_step = 0.25
viscosity = 0.5


def extended(x, sides, width):
    for axis, dim in sides:
        peers, length = (lax.axis_size(axis), x.shape[dim])
        up = [(i, (i + 1) % peers) for i in range(peers - 1)]
        down = [(j, i) for i, j in up]
        last = lax.slice_in_dim(x, length - width, length, axis=dim)
        leading = lax.slice_in_dim(x, 0, width, axis=dim)
        before = lax.ppermute(last, axis, up)
        after = lax.ppermute(leading, axis, down)
        x = jnp.concatenate([before, x, after], axis=dim)
    return x


def axial_viscous(padded):
    field = padded[:, :, :5]
    weight = padded[:, :, 5:]
    centre = field[1:-1]
    upper = 0.5 * (weight[1:-1] + weight[2:])
    lower = 0.5 * (weight[1:-1] + weight[:-2])
    return upper * (field[2:] - centre) - lower * (centre - field[:-2])


def radial_terms(padded, jac_radial):
    field = padded[:, :, :5]
    weight = padded[:, :, 5:]
    centre = field[:, 1:-1]
    upper = 0.5 * (weight[:, 1:-1] + weight[:, 2:])
    lower = 0.5 * (weight[:, 1:-1] + weight[:, :-2])
    flux = upper * (field[:, 2:] - centre) - lower * (centre - field[:, :-2])
    spread = 0.5 * (field[:, 2:] - field[:, :-2])
    mixed = jnp.einsum("xrka,kv->xrva", spread, jac_radial, precision=lax.Precision.HIGHEST)
    return mixed + viscosity * flux


def body(state, metric, deriv, filt_corr, jac_axial, jac_radial):
    weight = metric.reshape(metric.shape[0], metric.shape[1], 1, metric.shape[2])
    packed = jnp.concatenate([state, weight], axis=2)
    lines = lax.all_to_all(state, "ax", split_axis=1, concat_axis=0, tiled=True)
    flat = lines.reshape(lines.shape[0], -1)
    slope = jnp.dot(
        deriv, flat, precision=lax.Precision.HIGHEST, preferred_element_type=jnp.float32
    ).reshape(lines.shape)
    smooth = jnp.dot(
        filt_corr, flat, precision=lax.Precision.HIGHEST, preferred_element_type=jnp.float32
    ).reshape(lines.shape)
    mixed = jnp.einsum("xrka,kv->xrva", slope, jac_axial, precision=lax.Precision.HIGHEST)
    returned = lax.all_to_all(
        lines - smooth + section_step * mixed, "ax", split_axis=0, concat_axis=1, tiled=True
    )
    padded = extended(packed, (("ax", 0), ("rad", 1)), 1)
    local = viscosity * axial_viscous(padded[:, 1:-1]) + radial_terms(padded[1:-1], jac_radial)
    return returned + section_step * local


def solution(mesh):
    in_specs = (P("ax", "rad", None, None), P("ax", "rad", None), P(), P(), P(), P())
    out_specs = P("ax", "rad", None, None)
    return jax.shard_map(body, mesh=mesh, in_specs=in_specs, out_specs=out_specs, check_vma=False)
```

profile of v0, /device:TPU:40, one launch (start us, length us, event | category | flops | bytes accessed | tf_op | source)
XLA Modules:
  0.0 317.8 jit_solution(8941002510085099346)
XLA Ops:
  0.0 4.5 %copy.61 = f32[16,32,5,384]{3,0,2,1:T(8,128)S(1)} copy(f32[16,32,5,384]{3,1,2,0:T(8,128)} %param.6) | data formatting | bytes 7864320 | tf_op args[0]
  4.5 100.4 %all_to_all.36 = f32[16,32,5,384]{3,0,2,1:T(8,128)S(1)} all-to-all(f32[16,32,5,384]{3,0,2,1:T(8,128)S(1)} %copy.61), channel_id=1, replica_groups=mesh['ax'=32,'rad'=8] {'ax'}, dimensions={1} | all-to-all | bytes 7864320 | tf_op jit(solution)/shard_map/all_to_all | solution.py:47
  104.9 2.2 copy.62
  108.9 2.8 copy.86
  111.7 5.9 %copy.64 = f32[1920,512]{1,0:T(8,128)} copy(f32[1920,512]{0,1:T(8,128)} %bitcast.56) | data formatting | bytes 7864320 | tf_op jit(solution)/shard_map/dot_general | solution.py:52
  117.7 9.2 %fusion.19 = f32[512,5,384]{2,0,1:T(8,128)S(1)} fusion(f32[5,384,512]{2,1,0:T(8,128)} %bitcast.50, f32[512,512]{1,0:T(8,128)S(1)} %copy-done), kind=kOutput, calls=%fused_computation.26 | convolution fusion | flops 6039797760 | bytes 8912896 | tf_op jit(solution)/shard_map/dot_general | solution.py:49
  126.9 8.8 %fusion.9 = f32[512,384,5]{1,2,0:T(8,128)S(1)} fusion(f32[512,5,384]{2,0,1:T(8,128)S(1)} %fusion.19, f32[5,5]{1,0:T(8,128)S(1)} %copy-done.10), kind=kOutput, calls=%fused_computation.16 | convolution fusion | flops 58982400 | bytes 7864420 | tf_op jit(solution)/shard_map/xrka,kv->xrva/dot_general | solution.py:55
  135.7 8.0 %bitcast_add_fusion.1 = f32[512,1,5,384]{3,0,2,1:T(8,128)S(1)} fusion(f32[512,384,5]{1,2,0:T(8,128)S(1)} %fusion.9, f32[512,5,384]{2,0,1:T(8,128)S(1)} %bitcast.54, f32[5,384,512]{2,1,0:T(8,128)S(1)} %bitcast.51, f32[512,512]{1,0:T(8,128)S(1)} %copy-done.5), kind=kOutput, calls=%fused_computation.23 | convolution fusion | flops 6042746880 | bytes 16777216 | tf_op jit(solution)/shard_map/dot_general | solution.py:52
  143.7 6.2 %copy.68 = f32[512,1,5,384]{3,1,2,0:T(1,128)} copy(f32[512,1,5,384]{3,0,2,1:T(8,128)S(1)} %bitcast_add_fusion.1) | data formatting | bytes 7864320 | tf_op jit(solution)/shard_map/add | solution.py:57
  149.9 6.3 %all-to-all-start.1 = ((f32[512,1,5,384]{3,1,2,0:T(1,128)}), f32[512,1,5,384]{3,1,2,0:T(1,128)}, u32[]{:S(2)}, u32[]{:S(2)}) async-start(f32[512,1,5,384]{3,1,2,0:T(1,128)} %copy.68), calls=%async_computation.1 | async-start | bytes 7864320 | tf_op jit(solution)/shard_map/all_to_all | solution.py:56
  156.3 4.8 %copy.71 = f32[16,32,5,384]{3,2,1,0:T(8,128)S(1)} copy(f32[16,32,5,384]{3,1,2,0:T(8,128)} %param.6) | data formatting | bytes 7864320 | tf_op args[0]
  161.8 5.2 %collective-permute-start = (f32[1,32,6,384]{3,2,1,0:T(8,128)S(1)}, f32[1,32,6,384]{3,2,1,0:T(8,128)S(1)}, u32[]{:S(2)}, u32[]{:S(2)}) collective-permute-start(f32[1,32,6,384]{3,2,1,0:T(8,128)S(1)} %get-tuple-element.13), channel_id=1, source_target_pairs={{8,0},{16,8},{24,16},{32,24},{40,32},{48,40},{56,48},{64,56},{72,6... | collective-permute-start | bytes 884744 | tf_op jit(solution)/shard_map/ppermute | solution.py:18
  167.0 1.9 collective-permute-start.1
  168.9 81.6 %collective-permute-done = f32[1,32,6,384]{3,2,1,0:T(8,128)S(1)} collective-permute-done((f32[1,32,6,384]{3,2,1,0:T(8,128)S(1)}, f32[1,32,6,384]{3,2,1,0:T(8,128)S(1)}, u32[]{:S(2)}, u32[]{:S(2)}) %collective-permute-start) | collective-permute-done | bytes 294944 | tf_op jit(solution)/shard_map/ppermute | solution.py:18
  250.5 3.9 %collective-permute-done.1 = f32[1,32,6,384]{3,2,1,0:T(8,128)S(1)} collective-permute-done((f32[1,32,6,384]{3,2,1,0:T(8,128)S(1)}, f32[1,32,6,384]{3,2,1,0:T(8,128)S(1)}, u32[]{:S(2)}, u32[]{:S(2)}) %collective-permute-start.1) | collective-permute-done | bytes 294944 | tf_op jit(solution)/shard_map/ppermute | solution.py:17
  254.5 1.9 collective-permute-start.2
  256.4 3.9 %collective-permute-start.3 = (f32[18,1,6,384]{3,2,1,0:T(8,128)S(1)}, f32[18,1,6,384]{3,2,1,0:T(8,128)S(1)}, u32[]{:S(2)}, u32[]{:S(2)}) collective-permute-start(f32[18,1,6,384]{3,2,1,0:T(8,128)S(1)} %get-tuple-element.10), channel_id=1, source_target_pairs={{0,1},{1,2},{2,3},{3,4},{4,5},{5,6},{6,7},{8,9},{9,10},{10,11},{11... | collective-permute-start | bytes 497672 | tf_op jit(solution)/shard_map/ppermute | solution.py:17
  260.4 2.0 collective-permute-done.2
  262.3 4.0 %collective-permute-done.3 = f32[18,1,6,384]{3,2,1,0:T(8,128)S(1)} collective-permute-done((f32[18,1,6,384]{3,2,1,0:T(8,128)S(1)}, f32[18,1,6,384]{3,2,1,0:T(8,128)S(1)}, u32[]{:S(2)}, u32[]{:S(2)}) %collective-permute-start.3) | collective-permute-done | bytes 165920 | tf_op jit(solution)/shard_map/ppermute | solution.py:17
  266.4 9.1 %fusion.23 = (f32[16,32,1,384]{3,2,1,0:T(1,128)S(1)}, f32[16,32,1,384]{3,2,1,0:T(1,128)S(1)}, f32[16,32,1,384]{3,2,1,0:T(1,128)S(1)}, f32[16,32,1,384]{3,2,1,0:T(1,128)S(1)}) fusion(f32[16,32,1,384]{3,2,1,0:T(1,128)S(1)} %reshape.23, f32[18,1,6,384]{3,2,1,0:T(8,128)S(1)} %collective-permute-done.2, f32[1,32,6,384]{3,2,1,0:T(8,128)S(1)} %collective-permute-done, ...), kind=kLoop, calls=%fused_computation.32 | loop fusion | flops 3932160 | bytes 8785920 | tf_op jit(solution)/shard_map/mul | solution.py:36
  277.8 6.8 %pad_maximum_fusion = (f32[18,33,6,384]{3,2,1,0:T(8,128)}, f32[18,33,6,384]{3,2,1,0:T(8,128)}) fusion(f32[18,1,6,384]{3,2,1,0:T(8,128)S(1)} %collective-permute-done.2, f32[1,32,6,384]{3,2,1,0:T(8,128)S(1)} %collective-permute-done, f32[16,32,1,384]{3,2,1,0:T(1,128)S(1)} %reshape.23, f32[16,32,5,384]{3,2,1,0:T(8,128)S(1)} %copy.71, ...), kind=kLoop, calls=%fused_computation | loop fusion | flops 10948608 | bytes 16588800 | tf_op jit(solution)/shard_map/concatenate | solution.py:19
  284.6 4.4 %copy.69 = f32[512,1,5,384]{3,0,2,1:T(8,128)} copy(f32[512,1,5,384]{3,1,2,0:T(1,128)} %all-to-all-done.1) | data formatting | bytes 7864320 | tf_op jit(solution)/shard_map/all_to_all | solution.py:56
  289.1 23.0 %fusion.6 = f32[16,32,5,384]{3,2,1,0:T(8,128)} fusion(f32[16,32,5,384]{3,2,1,0:T(8,128)} %copy-done.2, f32[1,32,6,384]{3,2,1,0:T(8,128)S(1)} %collective-permute-done.1, f32[16,32,1,384]{3,2,1,0:T(1,128)S(1)} %reshape.23, f32[1,32,6,384]{3,2,1,0:T(8,128)S(1)} %collective-permute-done, f32[32,16,1,5,384]{4,1,0,3,2:T(8,128)} %bitcast.57, ...), kind=kOutput, calls=%fused_computation.9 | convolution fusion | flops 80609280 | bytes 43843684 | tf_op jit(solution)/shard_map/xrka,kv->xrva/dot_general | solution.py:40
  312.1 5.4 %copy.77 = f32[16,32,5,384]{3,1,2,0:T(8,128)} copy(f32[16,32,5,384]{3,2,1,0:T(8,128)} %fusion.6) | data formatting | bytes 7864320 | tf_op jit(solution)/shard_map/add | solution.py:61
  (31 shorter events, 4.9 us)
Async XLA Ops:
  0.0 117.7 %copy-start = (f32[512,512]{1,0:T(8,128)S(1)}, f32[512,512]{1,0:T(8,128)}, u32[]{:S(2)}) copy-start(f32[512,512]{1,0:T(8,128)} %param.8) | copy-start | bytes 3145732
  117.6 9.2 %copy-start.10 = (f32[5,5]{1,0:T(8,128)S(1)}, f32[5,5]{1,0:T(8,128)}, u32[]{:S(2)}) copy-start(f32[5,5]{1,0:T(8,128)} %param.10) | copy-start | bytes 304
  126.9 8.8 %copy-start.3 = (f32[1920,512]{1,0:T(8,128)S(1)}, f32[1920,512]{1,0:T(8,128)}, u32[]{:S(2)}) copy-start(f32[1920,512]{1,0:T(8,128)} %copy.64) | copy-start | bytes 11796484
  126.9 8.8 %copy-start.4 = (f32[32,16,1,5,384]{4,1,0,3,2:T(8,128)S(1)}, f32[32,16,1,5,384]{4,1,0,3,2:T(8,128)}, u32[]{:S(2)}) copy-start(f32[32,16,1,5,384]{4,1,0,3,2:T(8,128)} %copy.62) | copy-start | bytes 11796484
  126.9 8.8 %copy-start.5 = (f32[512,512]{1,0:T(8,128)S(1)}, f32[512,512]{1,0:T(8,128)}, u32[]{:S(2)}) copy-start(f32[512,512]{1,0:T(8,128)} %param.9) | copy-start | bytes 3145732
  149.9 134.7 %all-to-all-start.1 = ((f32[512,1,5,384]{3,1,2,0:T(1,128)}), f32[512,1,5,384]{3,1,2,0:T(1,128)}, u32[]{:S(2)}, u32[]{:S(2)}) async-start(f32[512,1,5,384]{3,1,2,0:T(1,128)} %copy.68), calls=%async_computation.1 | async-start | bytes 7864320 | tf_op jit(solution)/shard_map/all_to_all | solution.py:56
  156.2 4.8 %copy-start.6 = (f32[16,32,384]{2,1,0:T(8,128)S(1)}, f32[16,32,384]{2,1,0:T(8,128)}, u32[]{:S(2)}) copy-start(f32[16,32,384]{2,1,0:T(8,128)} %param.7) | copy-start | bytes 2359300
  161.0 116.8 %copy-start.2 = (f32[16,32,5,384]{3,2,1,0:T(8,128)}, f32[16,32,5,384]{3,2,1,0:T(8,128)S(1)}, u32[]{:S(2)}) copy-start(f32[16,32,5,384]{3,2,1,0:T(8,128)S(1)} %copy.71) | copy-start | bytes 11796484
  161.8 88.7 %collective-permute-start = (f32[1,32,6,384]{3,2,1,0:T(8,128)S(1)}, f32[1,32,6,384]{3,2,1,0:T(8,128)S(1)}, u32[]{:S(2)}, u32[]{:S(2)}) collective-permute-start(f32[1,32,6,384]{3,2,1,0:T(8,128)S(1)} %get-tuple-element.13), channel_id=1, source_target_pairs={{8,0},{16,8},{24,16},{32,24},{40,32},{48,40},{56,48},{64,56},{72,6... | collective-permute-start | bytes 884744 | tf_op jit(solution)/shard_map/ppermute | solution.py:18
  167.0 87.4 %collective-permute-start.1 = (f32[1,32,6,384]{3,2,1,0:T(8,128)S(1)}, f32[1,32,6,384]{3,2,1,0:T(8,128)S(1)}, u32[]{:S(2)}, u32[]{:S(2)}) collective-permute-start(f32[1,32,6,384]{3,2,1,0:T(8,128)S(1)} %get-tuple-element.14), channel_id=1, source_target_pairs={{0,8},{8,16},{16,24},{24,32},{32,40},{40,48},{48,56},{56,64},{64,7... | collective-permute-start | bytes 884744 | tf_op jit(solution)/shard_map/ppermute | solution.py:17
  254.5 7.8 %collective-permute-start.2 = (f32[18,1,6,384]{3,2,1,0:T(8,128)S(1)}, f32[18,1,6,384]{3,2,1,0:T(8,128)S(1)}, u32[]{:S(2)}, u32[]{:S(2)}) collective-permute-start(f32[18,1,6,384]{3,2,1,0:T(8,128)S(1)} %get-tuple-element.9), channel_id=1, source_target_pairs={{1,0},{2,1},{3,2},{4,3},{5,4},{6,5},{7,6},{9,8},{10,9},{11,10},{12... | collective-permute-start | bytes 497672 | tf_op jit(solution)/shard_map/ppermute | solution.py:18
  256.4 9.9 %collective-permute-start.3 = (f32[18,1,6,384]{3,2,1,0:T(8,128)S(1)}, f32[18,1,6,384]{3,2,1,0:T(8,128)S(1)}, u32[]{:S(2)}, u32[]{:S(2)}) collective-permute-start(f32[18,1,6,384]{3,2,1,0:T(8,128)S(1)} %get-tuple-element.10), channel_id=1, source_target_pairs={{0,1},{1,2},{2,3},{3,4},{4,5},{5,6},{6,7},{8,9},{9,10},{10,11},{11... | collective-permute-start | bytes 497672 | tf_op jit(solution)/shard_map/ppermute | solution.py:17
  284.6 4.5 %copy-start.11 = (f32[5,5]{1,0:T(8,128)S(1)}, f32[5,5]{1,0:T(8,128)}, u32[]{:S(2)}) copy-start(f32[5,5]{1,0:T(8,128)} %param.11) | copy-start | bytes 304
  284.6 4.5 %copy-start.7 = (f32[16,32,384]{2,1,0:T(8,128)S(1)}, f32[16,32,384]{2,1,0:T(8,128)}, u32[]{:S(2)}) copy-start(f32[16,32,384]{2,1,0:T(8,128)} %get-tuple-element.16) | copy-start | bytes 2359300
  284.6 4.5 %copy-start.8 = (f32[16,32,384]{2,1,0:T(8,128)S(1)}, f32[16,32,384]{2,1,0:T(8,128)}, u32[]{:S(2)}) copy-start(f32[16,32,384]{2,1,0:T(8,128)} %get-tuple-element.17) | copy-start | bytes 2359300
  284.6 4.5 %copy-start.9 = (f32[16,32,384]{2,1,0:T(8,128)S(1)}, f32[16,32,384]{2,1,0:T(8,128)}, u32[]{:S(2)}) copy-start(f32[16,32,384]{2,1,0:T(8,128)} %get-tuple-element.18) | copy-start | bytes 2359300
  289.1 28.4 %copy-start.1 = (f32[512,512]{1,0:T(8,128)S(1)}, f32[512,512]{1,0:T(8,128)}, u32[]{:S(2)}) copy-start(f32[512,512]{1,0:T(8,128)} %param.8) | copy-start | bytes 3145732
where the time goes:
time: 323 us; the launch traced here: 318 us
  blocking collectives  100 us (31%)
  waiting for transfers between devices  91.5 us (28%)
  matrix products  49 us (15%)
  local copies, waits for them, and re-layouts  40.9 us (13%)
  starting transfers between devices  19.3 us (6%)
  other arithmetic  16.2 us (5%)
    all_to_all x1, blocking collectives, body(): lines = lax.all_to_all(state, 'ax', split_axis=1, concat_axis=0, tiled=True)  100 us
    ppermute x2, waiting for transfers between devices, extended(): after = lax.ppermute(leading, axis, down)  83.6 us
    dot_general x1, matrix products, radial_terms(): jnp.einsum('xrka,kv->xrva', spread, jac_radial, precision=lax.Precision.H...  23 us
    unnamed x29, local copies, waits for them, and re-layouts  14.4 us
    dot_general x1, matrix products, body(): jnp.dot(deriv, flat, precision=lax.Precision.HIGHEST, preferred_element_t...  9.21 us
    mul x1, other arithmetic, radial_terms(): upper = 0.5 * (weight[:, 1:-1] + weight[:, 2:])  9.14 us
    dot_general x1, matrix products, body(): jnp.einsum('xrka,kv->xrva', slope, jac_axial, precision=lax.Precision.HIG...  8.78 us
    dot_general x1, matrix products, body(): jnp.dot(filt_corr, flat, precision=lax.Precision.HIGHEST, preferred_eleme...  7.98 us
  transfers between devices with their start and end apart: 5, of which 4 were waited for; matrix products, arithmetic and copies ran while one was open for 7% of the time, Pallas kernels for 0%

commit v1 on v0

--- a/solution.py
+++ b/solution.py
@@ -1,10 +1,15 @@
+import functools
+
 import jax
 import jax.numpy as jnp
 from jax import lax
+from jax.experimental import pallas as pl
+from jax.experimental.pallas import tpu as pltpu
 from jax.sharding import PartitionSpec as P
 
 section_step = 0.25
 viscosity = 0.5
+CHUNK = 128
 
 
 def extended(x, sides, width):
@@ -41,24 +46,58 @@
     return mixed + viscosity * flux
 
 
+def line_kernel(jac_ref, lines_ref, mats_ref, out_ref):
+    S, V, XL, C = lines_ref.shape
+    nx = S * XL
+    cols = [lines_ref[:, v, :, :].reshape(nx, C) for v in range(V)]
+    wide = jnp.concatenate(cols, axis=1)
+    prod = jnp.dot(
+        mats_ref[...], wide, precision=lax.Precision.HIGHEST, preferred_element_type=jnp.float32
+    )
+    smooth = prod[:nx]
+    slope = prod[nx:]
+    for v in range(V):
+        mix = jac_ref[0, v] * slope[:, 0:C]
+        for k in range(1, V):
+            mix = mix + jac_ref[k, v] * slope[:, k * C:(k + 1) * C]
+        res = cols[v] - smooth[:, v * C:(v + 1) * C] + section_step * mix
+        out_ref[:, v, :, :] = res.reshape(S, XL, C)
+
+
+def line_section(lines, mats, jac_axial):
+    S, V, XL, C = lines.shape
+    return pl.pallas_call(
+        line_kernel,
+        out_shape=jax.ShapeDtypeStruct(lines.shape, lines.dtype),
+        in_specs=[
+            pl.BlockSpec(memory_space=pltpu.SMEM),
+            pl.BlockSpec(memory_space=pltpu.VMEM),
+            pl.BlockSpec(memory_space=pltpu.VMEM),
+        ],
+        out_specs=pl.BlockSpec(memory_space=pltpu.VMEM),
+        compiler_params=pltpu.CompilerParams(vmem_limit_bytes=48 * 1024 * 1024),
+    )(jac_axial, lines, mats)
+
+
 def body(state, metric, deriv, filt_corr, jac_axial, jac_radial):
+    nx, nr, nv, na = state.shape
+    peers = lax.axis_size("ax")
+    assert nr == peers
+    mats = jnp.concatenate([filt_corr, deriv], axis=0)
+    send = jnp.transpose(state, (1, 2, 0, 3))
+    chunk = CHUNK if na % CHUNK == 0 else na
+    rets = []
+    for c in range(na // chunk):
+        piece = send[:, :, :, c * chunk:(c + 1) * chunk]
+        lines = lax.all_to_all(piece, "ax", split_axis=0, concat_axis=0, tiled=True)
+        res = line_section(lines, mats, jac_axial)
+        rets.append(lax.all_to_all(res, "ax", split_axis=0, concat_axis=0, tiled=True))
+    ret = jnp.concatenate(rets, axis=3)
     weight = metric.reshape(metric.shape[0], metric.shape[1], 1, metric.shape[2])
     packed = jnp.concatenate([state, weight], axis=2)
-    lines = lax.all_to_all(state, "ax", split_axis=1, concat_axis=0, tiled=True)
-    flat = lines.reshape(lines.shape[0], -1)
-    slope = jnp.dot(
-        deriv, flat, precision=lax.Precision.HIGHEST, preferred_element_type=jnp.float32
-    ).reshape(lines.shape)
-    smooth = jnp.dot(
-        filt_corr, flat, precision=lax.Precision.HIGHEST, preferred_element_type=jnp.float32
-    ).reshape(lines.shape)
-    mixed = jnp.einsum("xrka,kv->xrva", slope, jac_axial, precision=lax.Precision.HIGHEST)
-    returned = lax.all_to_all(
-        lines - smooth + section_step * mixed, "ax", split_axis=0, concat_axis=1, tiled=True
-    )
     padded = extended(packed, (("ax", 0), ("rad", 1)), 1)
     local = viscosity * axial_viscous(padded[:, 1:-1]) + radial_terms(padded[1:-1], jac_radial)
-    return returned + section_step * local
+    return jnp.transpose(ret, (2, 0, 1, 3)) + section_step * local
 
 
 def solution(mesh):

time: 323 us -> 290 us (0.90)
  the two profiles are of different devices: /device:TPU:40 before, /device:TPU:6 now
where the time goes in v1:
time: 290 us; the launch traced here: 289 us
  blocking collectives  84.4 us (29%)
  waiting for transfers between devices  74.9 us (26%)
  starting transfers between devices  49.4 us (17%)
  other arithmetic  26.5 us (9%)
  local copies, waits for them, and re-layouts  23.9 us (8%)
  Pallas kernels  19.9 us (7%)
  matrix products  9.22 us (3%)
    all_to_all x2, blocking collectives, body(): lines = lax.all_to_all(piece, 'ax', split_axis=0, concat_axis=0, tiled=True)  84.4 us
    all_to_all x3, waiting for transfers between devices, body(): lax.all_to_all(res, 'ax', split_axis=0, concat_axis=0, tiled=True)  31.8 us
    all_to_all x3, starting transfers between devices, body(): lax.all_to_all(res, 'ax', split_axis=0, concat_axis=0, tiled=True)  28.7 us
    ppermute x2, waiting for transfers between devices, extended(): after = lax.ppermute(leading, axis, down)  24.8 us
    pallas_call x3, Pallas kernels, line_section(): pl.pallas_call(line_kernel, out_shape=jax.ShapeDtypeStruct(lines.shape, l...  19.9 us
    all_to_all x1, waiting for transfers between devices, body(): lines = lax.all_to_all(piece, 'ax', split_axis=0, concat_axis=0, tiled=True)  18.4 us
    unnamed x27, local copies, waits for them, and re-layouts  18 us
    add x1, other arithmetic, body(): return jnp.transpose(ret, (2, 0, 1, 3)) + section_step * local  14.2 us
  transfers between devices with their start and end apart: 8, of which 4 were waited for; matrix products, arithmetic and copies ran while one was open for 9% of the time, Pallas kernels for 7%

profile of v1, /device:TPU:6, one launch (start us, length us, event | category | flops | bytes accessed | tf_op | source)
XLA Modules:
  0.0 288.5 jit_solution(14140340123160529538)
XLA Ops:
  0.0 4.4 %copy.27 = f32[16,32,5,384]{3,0,2,1:T(8,128)S(1)} copy(f32[16,32,5,384]{3,1,2,0:T(8,128)} %param.6) | data formatting | bytes 7864320 | tf_op args[0]
  6.8 46.7 %all_to_all.30.lines_ref = f32[32,5,16,128]{3,2,1,0:T(8,128)} all-to-all(f32[32,5,16,128]{3,2,1,0:T(8,128)S(1)} %get-tuple-element.15), channel_id=1, replica_groups=mesh['ax'=32,'rad'=8] {'ax'}, dimensions={0} | all-to-all | bytes 2621440 | tf_op jit(solution)/shard_map/all_to_all | solution.py:92
  53.5 37.6 %all_to_all.31.lines_ref = f32[32,5,16,128]{3,2,1,0:T(8,128)} all-to-all(f32[32,5,16,128]{3,2,1,0:T(8,128)S(1)} %get-tuple-element.16), channel_id=1, replica_groups=mesh['ax'=32,'rad'=8] {'ax'}, dimensions={0} | all-to-all | bytes 2621440 | tf_op jit(solution)/shard_map/all_to_all | solution.py:92
  91.1 5.2 %all-to-all-start.2 = ((f32[32,5,16,128]{3,2,1,0:T(8,128)}), f32[32,5,16,128]{3,2,1,0:T(8,128)S(1)}, u32[]{:S(2)}, u32[]{:S(2)}) async-start(f32[32,5,16,128]{3,2,1,0:T(8,128)} %get-tuple-element.17), calls=%async_computation.2 | async-start | bytes 2621440 | tf_op jit(solution)/shard_map/all_to_all | solution.py:92
  100.3 6.3 %shard_map.64 = f32[32,5,16,128]{3,2,1,0:T(8,128)S(1)} custom-call(f32[5,5]{1,0:T(8,128)S(1)} %copy-done.5, f32[32,5,16,128]{3,2,1,0:T(8,128)S(1)} %copy-done.3, f32[1024,512]{1,0:T(8,128)S(1)} %constant_dynamic-update-slice_fusion.mats_ref), custom_call_target="tpu_custom_call" | custom-call | tf_op jit(solution)/shard_map/pallas_call | solution.py:69
  107.7 18.4 %all-to-all-done.2.lines_ref = f32[32,5,16,128]{3,2,1,0:T(8,128)S(1)} async-done(((f32[32,5,16,128]{3,2,1,0:T(8,128)}), f32[32,5,16,128]{3,2,1,0:T(8,128)S(1)}, u32[]{:S(2)}, u32[]{:S(2)}) %all-to-all-start.2) | async-done | bytes 1310752 | tf_op jit(solution)/shard_map/all_to_all | solution.py:92
  126.0 9.5 %all-to-all-start.1 = ((f32[32,5,16,128]{3,2,1,0:T(8,128)}), f32[32,5,16,128]{3,2,1,0:T(8,128)}, u32[]{:S(2)}, u32[]{:S(2)}) async-start(f32[32,5,16,128]{3,2,1,0:T(8,128)} %copy-done.4), calls=%async_computation.1 | async-start | bytes 2621440 | tf_op jit(solution)/shard_map/all_to_all | solution.py:94
  136.9 6.3 %shard_map.66 = f32[32,5,16,128]{3,2,1,0:T(8,128)S(1)} custom-call(f32[5,5]{1,0:T(8,128)S(1)} %copy-done.5, f32[32,5,16,128]{3,2,1,0:T(8,128)S(1)} %copy-done.2, f32[1024,512]{1,0:T(8,128)S(1)} %constant_dynamic-update-slice_fusion.mats_ref), custom_call_target="tpu_custom_call" | custom-call | tf_op jit(solution)/shard_map/pallas_call | solution.py:69
  144.3 20.8 %all-to-all-done.1 = f32[32,5,16,128]{3,2,1,0:T(8,128)} async-done(((f32[32,5,16,128]{3,2,1,0:T(8,128)}), f32[32,5,16,128]{3,2,1,0:T(8,128)}, u32[]{:S(2)}, u32[]{:S(2)}) %all-to-all-start.1) | async-done | bytes 1310752 | tf_op jit(solution)/shard_map/all_to_all | solution.py:94
  165.1 9.8 %all-to-all-start.5 = ((f32[32,5,16,128]{3,2,1,0:T(8,128)}), f32[32,5,16,128]{3,2,1,0:T(8,128)}, u32[]{:S(2)}, u32[]{:S(2)}) async-start(f32[32,5,16,128]{3,2,1,0:T(8,128)} %copy-done.1), calls=%async_computation.5 | async-start | bytes 2621440 | tf_op jit(solution)/shard_map/all_to_all | solution.py:94
  177.3 3.5 %pad_maximum_fusion.6 = (f32[1,32,6,384]{3,0,2,1:T(1,128)}, f32[1,32,6,384]{3,0,2,1:T(1,128)}) fusion(f32[16,32,1,384]{3,0,2,1:T(8,128)S(1)} %bitcast.26, f32[16,32,5,384]{3,0,2,1:T(8,128)} %copy-done.6), kind=kLoop, calls=%fused_computation.34 | loop fusion | flops 147456 | bytes 5308416 | tf_op jit(solution)/shard_map/slice | solution.py:21
  182.1 3.8 %collective-permute-start.1 = (f32[1,32,6,384]{3,0,2,1:T(1,128)}, f32[1,32,6,384]{3,0,2,1:T(1,128)}, u32[]{:S(2)}, u32[]{:S(2)}) collective-permute-start(f32[1,32,6,384]{3,0,2,1:T(1,128)} %get-tuple-element.14), channel_id=1, source_target_pairs={{0,8},{8,16},{16,24},{24,32},{32,40},{40,48},{48,56},{56,64},{64,7... | collective-permute-start | bytes 884744 | tf_op jit(solution)/shard_map/ppermute | solution.py:22
  185.8 7.4 %shard_map.65 = f32[32,5,16,128]{3,2,1,0:T(8,128)} custom-call(f32[5,5]{1,0:T(8,128)S(1)} %copy-done.5, f32[32,5,16,128]{3,2,1,0:T(8,128)S(1)} %all-to-all-done.2.lines_ref, f32[1024,512]{1,0:T(8,128)S(1)} %constant_dynamic-update-slice_fusion.mats_ref), custom_call_target="tpu_custom_call" | custom-call | tf_op jit(solution)/shard_map/pallas_call | solution.py:69
  193.2 11.0 %all-to-all-done.5 = f32[32,5,16,128]{3,2,1,0:T(8,128)} async-done(((f32[32,5,16,128]{3,2,1,0:T(8,128)}), f32[32,5,16,128]{3,2,1,0:T(8,128)}, u32[]{:S(2)}, u32[]{:S(2)}) %all-to-all-start.5) | async-done | bytes 1310752 | tf_op jit(solution)/shard_map/all_to_all | solution.py:94
  204.2 9.4 %all-to-all-start.3 = ((f32[32,5,16,128]{3,2,1,0:T(8,128)}), f32[32,5,16,128]{3,2,1,0:T(8,128)S(1)}, u32[]{:S(2)}, u32[]{:S(2)}) async-start(f32[32,5,16,128]{3,2,1,0:T(8,128)} %shard_map.65), calls=%async_computation.3 | async-start | bytes 2621440 | tf_op jit(solution)/shard_map/all_to_all | solution.py:94
  214.9 2.9 collective-permute-start.2
  217.8 7.6 %collective-permute-start.3 = (f32[18,1,6,384]{3,0,2,1:T(8,128)S(1)}, f32[18,1,6,384]{3,0,2,1:T(8,128)S(1)}, u32[]{:S(2)}, u32[]{:S(2)}) collective-permute-start(f32[18,1,6,384]{3,0,2,1:T(8,128)S(1)} %get-tuple-element.10), channel_id=1, source_target_pairs={{0,1},{1,2},{2,3},{3,4},{4,5},{5,6},{6,7},{8,9},{9,10},{10,11},{11... | collective-permute-start | bytes 497672 | tf_op jit(solution)/shard_map/ppermute | solution.py:22
  225.4 24.8 %collective-permute-done.2 = f32[18,1,6,384]{3,0,2,1:T(8,128)S(1)} collective-permute-done((f32[18,1,6,384]{3,0,2,1:T(8,128)S(1)}, f32[18,1,6,384]{3,0,2,1:T(8,128)S(1)}, u32[]{:S(2)}, u32[]{:S(2)}) %collective-permute-start.2) | collective-permute-done | bytes 165920 | tf_op jit(solution)/shard_map/ppermute | solution.py:23
  250.1 2.6 fusion.14
  252.8 4.0 %pad_maximum_fusion = (f32[18,33,6,384]{3,0,2,1:T(8,128)S(1)}, f32[18,33,6,384]{3,0,2,1:T(8,128)S(1)}) fusion(f32[18,1,6,384]{3,0,2,1:T(8,128)S(1)} %collective-permute-done.2, f32[1,32,6,384]{3,0,2,1:T(1,128)} %collective-permute-done, f32[16,32,1,384]{3,0,2,1:T(8,128)S(1)} %bitcast.29, f32[16,32,5,384]{3,0,2,1:T(8,128)S(1)} %copy-done.7, ...), kind=kLoop, calls=%fused_computation | loop fusion | flops 10948608 | bytes 16588800 | tf_op jit(solution)/shard_map/concatenate | solution.py:24
  256.8 2.9 %copy-done.9 = f32[18,33,6,384]{3,0,2,1:T(8,128)} copy-done((f32[18,33,6,384]{3,0,2,1:T(8,128)}, f32[18,33,6,384]{3,0,2,1:T(8,128)S(1)}, u32[]{:S(2)}) %copy-start.9) | copy-done | bytes 5474328
  261.9 9.2 %fusion = f32[16,32,384,5]{2,3,1,0:T(8,128)} fusion(f32[16,32,5,384]{3,0,2,1:T(8,128)S(1)} %subtract_multiply_fusion, f32[5,5]{1,0:T(8,128)S(1)} %copy-done), kind=kOutput, calls=%fused_computation.2 | convolution fusion | flops 58982400 | bytes 7864420 | tf_op jit(solution)/shard_map/xrka,kv->xrva/dot_general | solution.py:45
  271.2 14.2 %fusion.8 = f32[16,32,5,384]{3,0,2,1:T(8,128)S(1)} fusion(f32[16,32,5,384]{3,0,2,1:T(8,128)} %copy-done.6, f32[1,32,6,384]{3,0,2,1:T(1,128)} %collective-permute-done.1, f32[16,32,1,384]{3,0,2,1:T(8,128)S(1)} %bitcast.30, f32[1,32,6,384]{3,0,2,1:T(1,128)} %collective-permute-done, f32[32,5,16,128]{3,2,1,0:T(8,128)} %all-to-all-done.5, ...), kind=kLoop, calls=%fused_computation.11 | loop fusion | flops 21626880 | bytes 28114944 | tf_op jit(solution)/shard_map/add | solution.py:100
  285.4 3.1 %copy.17 = f32[16,32,5,384]{3,1,2,0:T(8,128)} copy(f32[16,32,5,384]{3,0,2,1:T(8,128)S(1)} %fusion.8) | data formatting | bytes 7864320 | tf_op jit(solution)/shard_map/add | solution.py:100
  (34 shorter events, 17.0 us)
Async XLA Ops:
  0.0 261.9 %copy-start = (f32[5,5]{1,0:T(8,128)S(1)}, f32[5,5]{1,0:T(8,128)}, u32[]{:S(2)}) copy-start(f32[5,5]{1,0:T(8,128)} %param.11) | copy-start | bytes 304
  4.4 2.4 copy-start.6
  91.1 7.8 %copy-start.5 = (f32[5,5]{1,0:T(8,128)S(1)}, f32[5,5]{1,0:T(8,128)}, u32[]{:S(2)}) copy-start(f32[5,5]{1,0:T(8,128)} %jac_ref.5) | copy-start | bytes 304
  91.1 34.9 %all-to-all-start.2 = ((f32[32,5,16,128]{3,2,1,0:T(8,128)}), f32[32,5,16,128]{3,2,1,0:T(8,128)S(1)}, u32[]{:S(2)}, u32[]{:S(2)}) async-start(f32[32,5,16,128]{3,2,1,0:T(8,128)} %get-tuple-element.17), calls=%async_computation.2 | async-start | bytes 2621440 | tf_op jit(solution)/shard_map/all_to_all | solution.py:92
  99.0 1.3 copy-start.3
  106.6 1.1 copy-start.4
  126.0 39.0 %all-to-all-start.1 = ((f32[32,5,16,128]{3,2,1,0:T(8,128)}), f32[32,5,16,128]{3,2,1,0:T(8,128)}, u32[]{:S(2)}, u32[]{:S(2)}) async-start(f32[32,5,16,128]{3,2,1,0:T(8,128)} %copy-done.4), calls=%async_computation.1 | async-start | bytes 2621440 | tf_op jit(solution)/shard_map/all_to_all | solution.py:94
  135.6 1.3 copy-start.2
  143.2 1.1 copy-start.1
  165.1 39.1 %all-to-all-start.5 = ((f32[32,5,16,128]{3,2,1,0:T(8,128)}), f32[32,5,16,128]{3,2,1,0:T(8,128)}, u32[]{:S(2)}, u32[]{:S(2)}) async-start(f32[32,5,16,128]{3,2,1,0:T(8,128)} %copy-done.1), calls=%async_computation.5 | async-start | bytes 2621440 | tf_op jit(solution)/shard_map/all_to_all | solution.py:94
  176.5 0.9 copy-start.10
  180.8 32.8 %collective-permute-start = (f32[1,32,6,384]{3,0,2,1:T(1,128)}, f32[1,32,6,384]{3,0,2,1:T(1,128)}, u32[]{:S(2)}, u32[]{:S(2)}) collective-permute-start(f32[1,32,6,384]{3,0,2,1:T(1,128)} %get-tuple-element.13), channel_id=1, source_target_pairs={{8,0},{16,8},{24,16},{32,24},{40,32},{48,40},{56,48},{64,56},{72,6... | collective-permute-start | bytes 884744 | tf_op jit(solution)/shard_map/ppermute | solution.py:23
  182.1 31.5 %collective-permute-start.1 = (f32[1,32,6,384]{3,0,2,1:T(1,128)}, f32[1,32,6,384]{3,0,2,1:T(1,128)}, u32[]{:S(2)}, u32[]{:S(2)}) collective-permute-start(f32[1,32,6,384]{3,0,2,1:T(1,128)} %get-tuple-element.14), channel_id=1, source_target_pairs={{0,8},{8,16},{16,24},{24,32},{32,40},{40,48},{48,56},{56,64},{64,7... | collective-permute-start | bytes 884744 | tf_op jit(solution)/shard_map/ppermute | solution.py:22
  193.2 56.9 %copy-start.11 = (f32[16,32,384]{2,0,1:T(8,128)S(1)}, f32[16,32,384]{2,0,1:T(8,128)}, u32[]{:S(2)}) copy-start(f32[16,32,384]{2,0,1:T(8,128)} %copy-done.10) | copy-start | bytes 2359300
  204.2 67.0 %all-to-all-start.3 = ((f32[32,5,16,128]{3,2,1,0:T(8,128)}), f32[32,5,16,128]{3,2,1,0:T(8,128)S(1)}, u32[]{:S(2)}, u32[]{:S(2)}) async-start(f32[32,5,16,128]{3,2,1,0:T(8,128)} %shard_map.65), calls=%async_computation.3 | async-start | bytes 2621440 | tf_op jit(solution)/shard_map/all_to_all | solution.py:94
  213.6 36.5 %copy-start.7 = (f32[16,32,5,384]{3,0,2,1:T(8,128)S(1)}, f32[16,32,5,384]{3,0,2,1:T(8,128)}, u32[]{:S(2)}) copy-start(f32[16,32,5,384]{3,0,2,1:T(8,128)} %copy-done.6) | copy-start | bytes 11796484
  214.9 35.2 %collective-permute-start.2 = (f32[18,1,6,384]{3,0,2,1:T(8,128)S(1)}, f32[18,1,6,384]{3,0,2,1:T(8,128)S(1)}, u32[]{:S(2)}, u32[]{:S(2)}) collective-permute-start(f32[18,1,6,384]{3,0,2,1:T(8,128)S(1)} %get-tuple-element.9), channel_id=1, source_target_pairs={{1,0},{2,1},{3,2},{4,3},{5,4},{6,5},{7,6},{9,8},{10,9},{11,10},{12... | collective-permute-start | bytes 497672 | tf_op jit(solution)/shard_map/ppermute | solution.py:23
  217.8 32.4 %collective-permute-start.3 = (f32[18,1,6,384]{3,0,2,1:T(8,128)S(1)}, f32[18,1,6,384]{3,0,2,1:T(8,128)S(1)}, u32[]{:S(2)}, u32[]{:S(2)}) collective-permute-start(f32[18,1,6,384]{3,0,2,1:T(8,128)S(1)} %get-tuple-element.10), channel_id=1, source_target_pairs={{0,1},{1,2},{2,3},{3,4},{4,5},{5,6},{6,7},{8,9},{9,10},{10,11},{11... | collective-permute-start | bytes 497672 | tf_op jit(solution)/shard_map/ppermute | solution.py:22
  256.7 2.9 %copy-start.9 = (f32[18,33,6,384]{3,0,2,1:T(8,128)}, f32[18,33,6,384]{3,0,2,1:T(8,128)S(1)}, u32[]{:S(2)}) copy-start(f32[18,33,6,384]{3,0,2,1:T(8,128)S(1)} %get-tuple-element.8) | copy-start | bytes 16422916
  256.8 5.2 %copy-start.8 = (f32[18,33,6,384]{3,0,2,1:T(8,128)}, f32[18,33,6,384]{3,0,2,1:T(8,128)S(1)}, u32[]{:S(2)}) copy-start(f32[18,33,6,384]{3,0,2,1:T(8,128)S(1)} %get-tuple-element.7) | copy-start | bytes 16422916

commit v2 on v1

--- a/solution.py
+++ b/solution.py
@@ -9,7 +9,6 @@
 
 section_step = 0.25
 viscosity = 0.5
-CHUNK = 128
 
 
 def extended(x, sides, width):
@@ -42,8 +41,14 @@
     lower = 0.5 * (weight[:, 1:-1] + weight[:, :-2])
     flux = upper * (field[:, 2:] - centre) - lower * (centre - field[:, :-2])
     spread = 0.5 * (field[:, 2:] - field[:, :-2])
-    mixed = jnp.einsum("xrka,kv->xrva", spread, jac_radial, precision=lax.Precision.HIGHEST)
-    return mixed + viscosity * flux
+    nv = spread.shape[2]
+    mixed = []
+    for v in range(nv):
+        acc = jac_radial[0, v] * spread[:, :, 0]
+        for k in range(1, nv):
+            acc = acc + jac_radial[k, v] * spread[:, :, k]
+        mixed.append(acc)
+    return jnp.stack(mixed, axis=2) + viscosity * flux
 
 
 def line_kernel(jac_ref, lines_ref, mats_ref, out_ref):
@@ -85,18 +90,14 @@
     assert nr == peers
     mats = jnp.concatenate([filt_corr, deriv], axis=0)
     send = jnp.transpose(state, (1, 2, 0, 3))
-    chunk = CHUNK if na % CHUNK == 0 else na
-    rets = []
-    for c in range(na // chunk):
-        piece = send[:, :, :, c * chunk:(c + 1) * chunk]
-        lines = lax.all_to_all(piece, "ax", split_axis=0, concat_axis=0, tiled=True)
-        res = line_section(lines, mats, jac_axial)
-        rets.append(lax.all_to_all(res, "ax", split_axis=0, concat_axis=0, tiled=True))
-    ret = jnp.concatenate(rets, axis=3)
+    lines = lax.all_to_all(send, "ax", split_axis=0, concat_axis=0, tiled=True)
     weight = metric.reshape(metric.shape[0], metric.shape[1], 1, metric.shape[2])
     packed = jnp.concatenate([state, weight], axis=2)
     padded = extended(packed, (("ax", 0), ("rad", 1)), 1)
     local = viscosity * axial_viscous(padded[:, 1:-1]) + radial_terms(padded[1:-1], jac_radial)
+    lines, local = lax.optimization_barrier((lines, local))
+    res = line_section(lines, mats, jac_axial)
+    ret = lax.all_to_all(res, "ax", split_axis=0, concat_axis=0, tiled=True)
     return jnp.transpose(ret, (2, 0, 1, 3)) + section_step * local
 
 

time: 290 us -> 289 us (level)
  blocking collectives: 84.4 us -> 118 us
  starting transfers between devices: 49.4 us -> 24.2 us
  other arithmetic: 26.5 us -> 46.7 us
  local copies, waits for them, and re-layouts: 23.9 us -> 12.7 us
  matrix products: 9.22 us -> 0 us
  waiting for transfers between devices: 74.9 us -> 71 us
  Pallas kernels: 19.9 us -> 16.3 us
    all_to_all x4 -> x1, waiting for transfers between devices: 50.2 us -> 0.01 us  [body(): lines = lax.all_to_all(send, 'ax', split_axis=0, concat_axis=0, tiled=True)]
    ppermute x2, waiting for transfers between devices: 24.8 us -> 70.6 us  [extended(): after = lax.ppermute(leading, axis, down)]
    all_to_all x2 -> x1, blocking collectives: 84.4 us -> 118 us  [body(): ret = lax.all_to_all(res, 'ax', split_axis=0, concat_axis=0, tiled=True)]
    all_to_all x4 -> x1, starting transfers between devices: 33.9 us -> 11.7 us  [body(): lines = lax.all_to_all(send, 'ax', split_axis=0, concat_axis=0, tiled=True)]
    unnamed x0 -> x5, other arithmetic: none -> 17.4 us
    add x1, other arithmetic: 14.2 us -> 0.5 us  [body(): return jnp.transpose(ret, (2, 0, 1, 3)) + section_step * local]
    unnamed x27 -> x22, local copies, waits for them, and re-layouts: 18 us -> 8.26 us
    dot_general x1 -> x0, matrix products: 9.22 us -> none  [radial_terms(): jnp.einsum('xrka,kv->xrva', spread, jac_radial, precision=lax.Precision.H...]
  transfers between devices with their start and end apart: 8 -> 5, of which waited for: 4 -> 2; matrix products, arithmetic and copies ran while one was open for 9% -> 17% of each run, Pallas kernels for 7% -> 0%
where the time goes in v2:
time: 289 us
  blocking collectives  118 us (41%)
  waiting for transfers between devices  71 us (25%)
  other arithmetic  46.7 us (16%)
  starting transfers between devices  24.2 us (8%)
  Pallas kernels  16.3 us (6%)
  local copies, waits for them, and re-layouts  12.7 us (4%)
    all_to_all x1, blocking collectives, body(): ret = lax.all_to_all(res, 'ax', split_axis=0, concat_axis=0, tiled=True)  118 us
    ppermute x2, waiting for transfers between devices, extended(): after = lax.ppermute(leading, axis, down)  70.6 us
    unnamed x5, other arithmetic  17.4 us
    pallas_call x1, Pallas kernels, line_section(): pl.pallas_call(line_kernel, out_shape=jax.ShapeDtypeStruct(lines.shape, l...  16.3 us
    all_to_all x1, starting transfers between devices, body(): lines = lax.all_to_all(send, 'ax', split_axis=0, concat_axis=0, tiled=True)  11.7 us
    add x1, other arithmetic, body(): viscosity * axial_viscous(padded[:, 1:-1])  8.56 us
    ppermute x2, starting transfers between devices, extended(): before = lax.ppermute(last, axis, up)  8.26 us
    unnamed x22, local copies, waits for them, and re-layouts  8.26 us
  transfers between devices with their start and end apart: 5, of which 2 were waited for; matrix products, arithmetic and copies ran while one was open for 17% of the time, Pallas kernels for 0%

profile of v2, /device:TPU:6, one launch (start us, length us, event | category | flops | bytes accessed | tf_op | source)
XLA Modules:
  0.0 288.7 jit_solution(26128029895042346)
XLA Ops:
  0.0 6.3 %copy.19 = f32[16,32,5,384]{3,0,2,1:T(8,128)} copy(f32[16,32,5,384]{3,1,2,0:T(8,128)} %param.6) | data formatting | bytes 7864320 | tf_op args[0]
  6.3 11.7 %all-to-all-start = ((f32[32,5,16,384]{3,2,1,0:T(8,128)}), f32[32,5,16,384]{3,2,1,0:T(8,128)}, u32[]{:S(2)}, u32[]{:S(2)}) async-start(f32[32,5,16,384]{3,2,1,0:T(8,128)} %bitcast.40), calls=%async_computation | async-start | bytes 7864320 | tf_op jit(solution)/shard_map/all_to_all | solution.py:93
  18.6 2.9 pad_maximum_fusion.7
  21.4 1.4 collective-permute-start
  22.9 3.0 %collective-permute-start.1 = (f32[1,32,6,384]{3,0,2,1:T(1,128)S(1)}, f32[1,32,6,384]{3,0,2,1:T(1,128)S(1)}, u32[]{:S(2)}, u32[]{:S(2)}) collective-permute-start(f32[1,32,6,384]{3,0,2,1:T(1,128)S(1)} %get-tuple-element.18), channel_id=1, source_target_pairs={{0,8},{8,16},{16,24},{24,32},{32,40},{40,48},{48,56},{56,64},{64,7... | collective-permute-start | bytes 884744 | tf_op jit(solution)/shard_map/ppermute | solution.py:21
  25.9 0.7 fusion.16
  27.2 2.7 collective-permute-start.2
  29.9 5.2 %collective-permute-start.3 = (f32[18,1,6,384]{3,0,2,1:T(8,128)S(1)}, f32[18,1,6,384]{3,0,2,1:T(8,128)S(1)}, u32[]{:S(2)}, u32[]{:S(2)}) collective-permute-start(f32[18,1,6,384]{3,0,2,1:T(8,128)S(1)} %get-tuple-element.14), channel_id=1, source_target_pairs={{0,1},{1,2},{2,3},{3,4},{4,5},{5,6},{6,7},{8,9},{9,10},{10,11},{11... | collective-permute-start | bytes 497672 | tf_op jit(solution)/shard_map/ppermute | solution.py:21
  35.1 0.6 fusion.17
  35.9 70.6 %collective-permute-done.2 = f32[18,1,6,384]{3,0,2,1:T(8,128)S(1)} collective-permute-done((f32[18,1,6,384]{3,0,2,1:T(8,128)S(1)}, f32[18,1,6,384]{3,0,2,1:T(8,128)S(1)}, u32[]{:S(2)}, u32[]{:S(2)}) %collective-permute-start.2) | collective-permute-done | bytes 165920 | tf_op jit(solution)/shard_map/ppermute | solution.py:22
  106.5 5.0 %pad_maximum_fusion = (f32[18,33,6,384]{3,0,2,1:T(8,128)S(1)}, f32[18,33,6,384]{3,0,2,1:T(8,128)}) fusion(f32[18,1,6,384]{3,0,2,1:T(8,128)S(1)} %collective-permute-done.2, f32[1,32,6,384]{3,0,2,1:T(1,128)S(1)} %collective-permute-done, f32[16,32,1,384]{3,0,2,1:T(8,128)S(1)} %bitcast.45, f32[16,32,5,384]{3,0,2,1:T(8,128)S(1)} %copy-done.1, ...), kind=kLoop, calls=%fused_computation | loop fusion | flops 10948608 | bytes 16588800 | tf_op jit(solution)/shard_map/concatenate | solution.py:23
  111.5 6.1 %subtract_multiply_fusion = f32[16,32,5,384]{3,0,2,1:T(8,128)S(1)} fusion(f32[18,33,6,384]{3,0,2,1:T(8,128)} %get-tuple-element.12, f32[18,33,6,384]{3,0,2,1:T(8,128)S(1)} %get-tuple-element.11), kind=kLoop, calls=%fused_computation.14 | loop fusion | flops 1966080 | bytes 11796480 | tf_op jit(solution)/shard_map/mul | solution.py:43
  117.6 4.3 %add_dynamic-update-slice_fusion.4 = f32[16,32,5,384]{3,0,2,1:T(8,128)} fusion(f32[16,32,5,384]{3,0,2,1:T(8,128)S(1)} %subtract_multiply_fusion, f32[]{:T(128)} %bitcast.8, f32[]{:T(128)} %bitcast.7, f32[]{:T(128)} %bitcast.6, f32[]{:T(128)} %bitcast.5, f32[]{:T(128)} %bitcast.4), kind=kLoop, calls=%fused_computation.33 | loop fusion | flops 1769471 | bytes 4718612
  121.9 4.4 %add_dynamic-update-slice_fusion.3 = f32[16,32,5,384]{3,0,2,1:T(8,128)} fusion(f32[16,32,5,384]{3,0,2,1:T(8,128)} %add_dynamic-update-slice_fusion.4, f32[16,32,5,384]{3,0,2,1:T(8,128)S(1)} %subtract_multiply_fusion, f32[]{:T(128)} %bitcast.13, f32[]{:T(128)} %bitcast.12, f32[]{:T(128)} %bitcast.11, f32[]{:T(128)} %bitcast.10, f32[]{:T(128)} %bitcast.9), kind=kLoop, calls=%fused_computation.32 | loop fusion | flops 1769472 | bytes 4721152
  126.2 4.3 %add_dynamic-update-slice_fusion.2 = f32[16,32,5,384]{3,0,2,1:T(8,128)} fusion(f32[16,32,5,384]{3,0,2,1:T(8,128)} %add_dynamic-update-slice_fusion.3, f32[16,32,5,384]{3,0,2,1:T(8,128)S(1)} %subtract_multiply_fusion, f32[]{:T(128)} %bitcast.18, f32[]{:T(128)} %bitcast.17, f32[]{:T(128)} %bitcast.16, f32[]{:T(128)} %bitcast.15, f32[]{:T(128)} %bitcast.14), kind=kLoop, calls=%fused_computation.31 | loop fusion | flops 1769472 | bytes 4721152
  130.5 4.4 %add_dynamic-update-slice_fusion.1 = f32[16,32,5,384]{3,0,2,1:T(8,128)} fusion(f32[16,32,5,384]{3,0,2,1:T(8,128)} %add_dynamic-update-slice_fusion.2, f32[16,32,5,384]{3,0,2,1:T(8,128)S(1)} %subtract_multiply_fusion, f32[]{:T(128)} %bitcast.23, f32[]{:T(128)} %bitcast.22, f32[]{:T(128)} %bitcast.21, f32[]{:T(128)} %bitcast.20, f32[]{:T(128)} %bitcast.19), kind=kLoop, calls=%fused_computation.30 | loop fusion | flops 1769472 | bytes 4721152
  135.0 4.5 %add_dynamic-update-slice_fusion = f32[16,32,5,384]{3,0,2,1:T(8,128)} fusion(f32[16,32,5,384]{3,0,2,1:T(8,128)} %add_dynamic-update-slice_fusion.1, f32[16,32,5,384]{3,0,2,1:T(8,128)S(1)} %subtract_multiply_fusion, f32[]{:T(128)} %bitcast.28, f32[]{:T(128)} %bitcast.27, f32[]{:T(128)} %bitcast.26, f32[]{:T(128)} %bitcast.25, f32[]{:T(128)} %bitcast.24), kind=kLoop, calls=%fused_computation.29 | loop fusion | flops 1769472 | bytes 4721152 | tf_op jit(solution)/shard_map/stack | solution.py:51
  139.5 1.6 fusion.10
  141.1 1.4 slice-done.1
  142.5 8.6 %fusion.4 = f32[16,32,5,384]{3,0,2,1:T(8,128)} fusion(f32[16,32,5,384]{3,0,2,1:T(8,128)S(1)} %copy-done.1, f32[1,32,6,384]{3,0,2,1:T(1,128)S(1)} %collective-permute-done.1, f32[16,32,1,384]{3,0,2,1:T(8,128)S(1)} %bitcast.47, f32[1,32,6,384]{3,0,2,1:T(1,128)S(1)} %collective-permute-done, f32[16,32,5,384]{3,0,2,1:T(8,128)} %add_dynamic-update-slice_fusion, ...), kind=kLoop, calls=%fused_computation.7 | loop fusion | flops 17694720 | bytes 24182784 | tf_op jit(solution)/shard_map/add | solution.py:97
  151.1 16.3 %shard_map.64 = f32[32,5,16,384]{3,2,1,0:T(8,128)S(1)} custom-call(f32[5,5]{1,0:T(8,128)S(1)} %copy-done, f32[32,5,16,384]{3,2,1,0:T(8,128)} %all-to-all-done.lines_ref, f32[1024,512]{1,0:T(8,128)S(1)} %pad_maximum_fusion.5.mats_ref), custom_call_target="tpu_custom_call" | custom-call | tf_op jit(solution)/shard_map/pallas_call | solution.py:74
  167.4 117.7 %all_to_all.10 = f32[32,5,16,384]{3,2,1,0:T(8,128)S(1)} all-to-all(f32[32,5,16,384]{3,2,1,0:T(8,128)S(1)} %shard_map.64), channel_id=1, replica_groups=mesh['ax'=32,'rad'=8] {'ax'}, dimensions={0} | all-to-all | bytes 7864320 | tf_op jit(solution)/shard_map/all_to_all | solution.py:100
  285.0 0.5 bitcast_add_fusion
  285.5 3.1 %copy.14 = f32[16,32,5,384]{3,1,2,0:T(8,128)} copy(f32[16,32,5,384]{3,0,2,1:T(8,128)S(1)} %bitcast_add_fusion) | data formatting | bytes 7864320 | tf_op jit(solution)/shard_map/add | solution.py:101
  (27 shorter events, 1.2 us)
Async XLA Ops:
  6.3 11.7 %copy-start.6 = (f32[16,32,384]{2,1,0:T(8,128)S(1)}, f32[16,32,384]{2,1,0:T(8,128)}, u32[]{:S(2)}) copy-start(f32[16,32,384]{2,1,0:T(8,128)} %param.7) | copy-start | bytes 2359300
  6.3 144.7 %all-to-all-start = ((f32[32,5,16,384]{3,2,1,0:T(8,128)}), f32[32,5,16,384]{3,2,1,0:T(8,128)}, u32[]{:S(2)}, u32[]{:S(2)}) async-start(f32[32,5,16,384]{3,2,1,0:T(8,128)} %bitcast.40), calls=%async_computation | async-start | bytes 7864320 | tf_op jit(solution)/shard_map/all_to_all | solution.py:93
  18.1 7.9 %copy-start.7 = (f32[5,5]{1,0:T(8,128)S(1)}, f32[5,5]{1,0:T(8,128)}, u32[]{:S(2)}) copy-start(f32[5,5]{1,0:T(8,128)} %param.11) | copy-start | bytes 304
  18.1 9.0 %copy-start.1 = (f32[16,32,5,384]{3,0,2,1:T(8,128)S(1)}, f32[16,32,5,384]{3,0,2,1:T(8,128)}, u32[]{:S(2)}) copy-start(f32[16,32,5,384]{3,0,2,1:T(8,128)} %copy.19) | copy-start | bytes 11796484
  21.4 14.3 %copy-start.4 = (f32[512,512]{1,0:T(8,128)S(1)}, f32[512,512]{1,0:T(8,128)}, u32[]{:S(2)}) copy-start(f32[512,512]{1,0:T(8,128)} %param.8) | copy-start | bytes 3145732
  21.4 14.3 %copy-start.5 = (f32[512,512]{1,0:T(8,128)S(1)}, f32[512,512]{1,0:T(8,128)}, u32[]{:S(2)}) copy-start(f32[512,512]{1,0:T(8,128)} %param.9) | copy-start | bytes 3145732
  21.4 5.2 %collective-permute-start = (f32[1,32,6,384]{3,0,2,1:T(1,128)S(1)}, f32[1,32,6,384]{3,0,2,1:T(1,128)S(1)}, u32[]{:S(2)}, u32[]{:S(2)}) collective-permute-start(f32[1,32,6,384]{3,0,2,1:T(1,128)S(1)} %get-tuple-element.17), channel_id=1, source_target_pairs={{8,0},{16,8},{24,16},{32,24},{40,32},{48,40},{56,48},{64,56},{72,6... | collective-permute-start | bytes 884744 | tf_op jit(solution)/shard_map/ppermute | solution.py:22
  22.9 4.2 %collective-permute-start.1 = (f32[1,32,6,384]{3,0,2,1:T(1,128)S(1)}, f32[1,32,6,384]{3,0,2,1:T(1,128)S(1)}, u32[]{:S(2)}, u32[]{:S(2)}) collective-permute-start(f32[1,32,6,384]{3,0,2,1:T(1,128)S(1)} %get-tuple-element.18), channel_id=1, source_target_pairs={{0,8},{8,16},{16,24},{24,32},{32,40},{40,48},{48,56},{56,64},{64,7... | collective-permute-start | bytes 884744 | tf_op jit(solution)/shard_map/ppermute | solution.py:21
  27.2 79.3 %collective-permute-start.2 = (f32[18,1,6,384]{3,0,2,1:T(8,128)S(1)}, f32[18,1,6,384]{3,0,2,1:T(8,128)S(1)}, u32[]{:S(2)}, u32[]{:S(2)}) collective-permute-start(f32[18,1,6,384]{3,0,2,1:T(8,128)S(1)} %get-tuple-element.13), channel_id=1, source_target_pairs={{1,0},{2,1},{3,2},{4,3},{5,4},{6,5},{7,6},{9,8},{10,9},{11,10},{12... | collective-permute-start | bytes 497672 | tf_op jit(solution)/shard_map/ppermute | solution.py:22
  29.9 76.6 %collective-permute-start.3 = (f32[18,1,6,384]{3,0,2,1:T(8,128)S(1)}, f32[18,1,6,384]{3,0,2,1:T(8,128)S(1)}, u32[]{:S(2)}, u32[]{:S(2)}) collective-permute-start(f32[18,1,6,384]{3,0,2,1:T(8,128)S(1)} %get-tuple-element.14), channel_id=1, source_target_pairs={{0,1},{1,2},{2,3},{3,4},{4,5},{5,6},{6,7},{8,9},{9,10},{10,11},{11... | collective-permute-start | bytes 497672 | tf_op jit(solution)/shard_map/ppermute | solution.py:21
  111.5 6.1 %copy-start.2 = (f32[18,33,6,384]{3,0,2,1:T(8,128)}, f32[18,33,6,384]{3,0,2,1:T(8,128)S(1)}, u32[]{:S(2)}) copy-start(f32[18,33,6,384]{3,0,2,1:T(8,128)S(1)} %get-tuple-element.11) | copy-start | bytes 16422916
  135.0 6.1 %slice-start = ((s8[7299072]{0:T(1024)(128)(4,1)}), s8[3104768]{0:T(1024)(128)(4,1)S(1)}, s32[]{:S(2)}) async-start(s8[7299072]{0:T(1024)(128)(4,1)} %bitcast.41), calls=%async_computation.2 | async-start | bytes 6209536
  139.5 3.0 %slice-start.1 = ((s8[7299072]{0:T(1024)(128)(4,1)}), s8[4194304]{0:T(1024)(128)(4,1)S(1)}, s32[]{:S(2)}) async-start(s8[7299072]{0:T(1024)(128)(4,1)} %bitcast.41), calls=%async_computation.3 | async-start | bytes 8388608
  142.5 8.6 %copy-start = (f32[5,5]{1,0:T(8,128)S(1)}, f32[5,5]{1,0:T(8,128)}, u32[]{:S(2)}) copy-start(f32[5,5]{1,0:T(8,128)} %jac_ref.1) | copy-start | bytes 304
  167.4 117.7 %copy-start.3 = (f32[16,32,5,384]{3,0,2,1:T(8,128)S(1)}, f32[16,32,5,384]{3,0,2,1:T(8,128)}, u32[]{:S(2)}) copy-start(f32[16,32,5,384]{3,0,2,1:T(8,128)} %fusion.4) | copy-start | bytes 11796484

commit v3 on v2

--- a/solution.py
+++ b/solution.py
@@ -9,6 +9,7 @@
 
 section_step = 0.25
 viscosity = 0.5
+CHUNK = 128
 
 
 def extended(x, sides, width):
@@ -90,14 +91,28 @@
     assert nr == peers
     mats = jnp.concatenate([filt_corr, deriv], axis=0)
     send = jnp.transpose(state, (1, 2, 0, 3))
-    lines = lax.all_to_all(send, "ax", split_axis=0, concat_axis=0, tiled=True)
+    chunk = CHUNK if na % CHUNK == 0 else na
+    count = na // chunk
+
+    def exchange(x):
+        return lax.all_to_all(x, "ax", split_axis=0, concat_axis=0, tiled=True)
+
+    lines = [exchange(send[..., c * chunk:(c + 1) * chunk]) for c in range(count)]
     weight = metric.reshape(metric.shape[0], metric.shape[1], 1, metric.shape[2])
     packed = jnp.concatenate([state, weight], axis=2)
     padded = extended(packed, (("ax", 0), ("rad", 1)), 1)
     local = viscosity * axial_viscous(padded[:, 1:-1]) + radial_terms(padded[1:-1], jac_radial)
-    lines, local = lax.optimization_barrier((lines, local))
-    res = line_section(lines, mats, jac_axial)
-    ret = lax.all_to_all(res, "ax", split_axis=0, concat_axis=0, tiled=True)
+    res = [line_section(lines[0], mats, jac_axial)]
+    for c in range(1, count):
+        nxt, prev = lax.optimization_barrier((lines[c], res[-1]))
+        res[-1] = prev
+        res.append(line_section(nxt, mats, jac_axial))
+    rets = [exchange(res[0])]
+    for c in range(1, count):
+        prev, cur = lax.optimization_barrier((rets[-1], res[c]))
+        rets[-1] = prev
+        rets.append(exchange(cur))
+    ret = jnp.concatenate(rets, axis=3)
     return jnp.transpose(ret, (2, 0, 1, 3)) + section_step * local
 
 

time: 289 us -> 289 us (level)
  starting transfers between devices: 24.2 us -> 70.8 us
  blocking collectives: 118 us -> 84.4 us
  waiting for transfers between devices: 71 us -> 45 us
  local copies, waits for them, and re-layouts: 12.7 us -> 25.3 us
  other arithmetic: 46.7 us -> 43.1 us
    ppermute x2, waiting for transfers between devices: 70.6 us -> 0.01 us  [extended(): after = lax.ppermute(leading, axis, down)]
    all_to_all x1 -> x4, starting transfers between devices: 11.7 us -> 58.6 us  [exchange(): return lax.all_to_all(x, 'ax', split_axis=0, concat_axis=0, tiled=True)]
    all_to_all x1 -> x4, waiting for transfers between devices: 0.01 us -> 43.8 us  [exchange(): return lax.all_to_all(x, 'ax', split_axis=0, concat_axis=0, tiled=True)]
    all_to_all x1 -> x2, blocking collectives: 118 us -> 84.4 us  [exchange(): return lax.all_to_all(x, 'ax', split_axis=0, concat_axis=0, tiled=True)]
    add x1, other arithmetic: 0.5 us -> 12.6 us  [body(): return jnp.transpose(ret, (2, 0, 1, 3)) + section_step * local]
    unnamed x22 -> x41, local copies, waits for them, and re-layouts: 8.26 us -> 18 us
    add x1 -> x0, other arithmetic: 8.56 us -> none  [body(): viscosity * axial_viscous(padded[:, 1:-1])]
    mul x1, other arithmetic: 6.08 us -> 1.01 us  [radial_terms(): spread = 0.5 * (field[:, 2:] - field[:, :-2])]
  transfers between devices with their start and end apart: 5 -> 8, of which waited for: 2 -> 5; matrix products, arithmetic and copies ran while one was open for 17% -> 13% of each run, Pallas kernels for 0% -> 7%
where the time goes in v3:
time: 289 us; the launch traced here: 288 us
  blocking collectives  84.4 us (29%)
  starting transfers between devices  70.8 us (24%)
  waiting for transfers between devices  45 us (16%)
  other arithmetic  43.1 us (15%)
  local copies, waits for them, and re-layouts  25.3 us (9%)
  Pallas kernels  18.8 us (7%)
    all_to_all x2, blocking collectives, exchange(): return lax.all_to_all(x, 'ax', split_axis=0, concat_axis=0, tiled=True)  84.4 us
    all_to_all x4, starting transfers between devices, exchange(): return lax.all_to_all(x, 'ax', split_axis=0, concat_axis=0, tiled=True)  58.6 us
    all_to_all x4, waiting for transfers between devices, exchange(): return lax.all_to_all(x, 'ax', split_axis=0, concat_axis=0, tiled=True)  43.8 us
    pallas_call x3, Pallas kernels, line_section(): pl.pallas_call(line_kernel, out_shape=jax.ShapeDtypeStruct(lines.shape, l...  18.8 us
    unnamed x41, local copies, waits for them, and re-layouts  18 us
    unnamed x4, other arithmetic  13.9 us
    add x1, other arithmetic, body(): return jnp.transpose(ret, (2, 0, 1, 3)) + section_step * local  12.6 us
    ppermute x2, starting transfers between devices, extended(): before = lax.ppermute(last, axis, up)  8.26 us
  transfers between devices with their start and end apart: 8, of which 5 were waited for; matrix products, arithmetic and copies ran while one was open for 13% of the time, Pallas kernels for 7%

profile of v3, /device:TPU:6, one launch (start us, length us, event | category | flops | bytes accessed | tf_op | source)
XLA Modules:
  0.0 287.7 jit_solution(4376277313699861883)
XLA Ops:
  0.0 4.4 %copy.19 = f32[16,32,5,384]{3,0,2,1:T(8,128)S(1)} copy(f32[16,32,5,384]{3,1,2,0:T(8,128)} %param.6) | data formatting | bytes 7864320 | tf_op args[0]
  6.8 46.7 %all_to_all.30.lines_ref = f32[32,5,16,128]{3,2,1,0:T(8,128)} all-to-all(f32[32,5,16,128]{3,2,1,0:T(8,128)S(1)} %get-tuple-element.32), channel_id=1, replica_groups=mesh['ax'=32,'rad'=8] {'ax'}, dimensions={0} | all-to-all | bytes 2621440 | tf_op jit(solution)/shard_map/all_to_all | solution.py:98
  53.5 37.6 %all_to_all.31.lines_ref = f32[32,5,16,128]{3,2,1,0:T(8,128)} all-to-all(f32[32,5,16,128]{3,2,1,0:T(8,128)S(1)} %get-tuple-element.33), channel_id=1, replica_groups=mesh['ax'=32,'rad'=8] {'ax'}, dimensions={0} | all-to-all | bytes 2621440 | tf_op jit(solution)/shard_map/all_to_all | solution.py:98
  91.1 5.2 %all-to-all-start.3 = ((f32[32,5,16,128]{3,2,1,0:T(8,128)}), f32[32,5,16,128]{3,2,1,0:T(8,128)S(1)}, u32[]{:S(2)}, u32[]{:S(2)}) async-start(f32[32,5,16,128]{3,2,1,0:T(8,128)} %get-tuple-element.31), calls=%async_computation.3 | async-start | bytes 2621440 | tf_op jit(solution)/shard_map/all_to_all | solution.py:98
  100.3 6.2 %shard_map.64 = f32[32,5,16,128]{3,2,1,0:T(8,128)S(1)} custom-call(f32[5,5]{1,0:T(8,128)S(1)} %copy-done.5, f32[32,5,16,128]{3,2,1,0:T(8,128)S(1)} %copy-done.3, f32[1024,512]{1,0:T(8,128)S(1)} %constant_dynamic-update-slice_fusion.mats_ref), custom_call_target="tpu_custom_call" | custom-call | tf_op jit(solution)/shard_map/pallas_call | solution.py:75
  107.6 18.4 %all-to-all-done.3.lines_ref = f32[32,5,16,128]{3,2,1,0:T(8,128)S(1)} async-done(((f32[32,5,16,128]{3,2,1,0:T(8,128)}), f32[32,5,16,128]{3,2,1,0:T(8,128)S(1)}, u32[]{:S(2)}, u32[]{:S(2)}) %all-to-all-start.3) | async-done | bytes 1310752 | tf_op jit(solution)/shard_map/all_to_all | solution.py:98
  126.0 9.5 %all-to-all-start.2 = ((f32[32,5,16,128]{3,2,1,0:T(8,128)}), f32[32,5,16,128]{3,2,1,0:T(8,128)}, u32[]{:S(2)}, u32[]{:S(2)}) async-start(f32[32,5,16,128]{3,2,1,0:T(8,128)} %copy-done.4), calls=%async_computation.2 | async-start | bytes 2621440 | tf_op jit(solution)/shard_map/all_to_all | solution.py:98
  136.9 6.2 %shard_map.65 = f32[32,5,16,128]{3,2,1,0:T(8,128)S(1)} custom-call(f32[5,5]{1,0:T(8,128)S(1)} %copy-done.5, f32[32,5,16,128]{3,2,1,0:T(8,128)S(1)} %copy-done.2, f32[1024,512]{1,0:T(8,128)S(1)} %constant_dynamic-update-slice_fusion.mats_ref), custom_call_target="tpu_custom_call" | custom-call | tf_op jit(solution)/shard_map/pallas_call | solution.py:75
  144.2 20.8 %all-to-all-done.2 = f32[32,5,16,128]{3,2,1,0:T(8,128)} async-done(((f32[32,5,16,128]{3,2,1,0:T(8,128)}), f32[32,5,16,128]{3,2,1,0:T(8,128)}, u32[]{:S(2)}, u32[]{:S(2)}) %all-to-all-start.2) | async-done | bytes 1310752 | tf_op jit(solution)/shard_map/all_to_all | solution.py:98
  165.1 9.8 %all-to-all-start.4 = ((f32[32,5,16,128]{3,2,1,0:T(8,128)}), f32[32,5,16,128]{3,2,1,0:T(8,128)}, u32[]{:S(2)}, u32[]{:S(2)}) async-start(f32[32,5,16,128]{3,2,1,0:T(8,128)} %copy-done), calls=%async_computation.4 | async-start | bytes 2621440 | tf_op jit(solution)/shard_map/all_to_all | solution.py:98
  176.6 2.9 %pad_maximum_fusion.6 = (f32[1,32,6,384]{3,0,2,1:T(1,128)S(1)}, f32[1,32,6,384]{3,0,2,1:T(1,128)S(1)}) fusion(f32[16,32,1,384]{3,0,2,1:T(8,128)S(1)} %bitcast.44, f32[16,32,5,384]{3,0,2,1:T(8,128)} %copy-done.6), kind=kLoop, calls=%fused_computation.36 | loop fusion | flops 147456 | bytes 5308416 | tf_op jit(solution)/shard_map/slice | solution.py:21
  180.8 3.0 %collective-permute-start.1 = (f32[1,32,6,384]{3,0,2,1:T(1,128)S(1)}, f32[1,32,6,384]{3,0,2,1:T(1,128)S(1)}, u32[]{:S(2)}, u32[]{:S(2)}) collective-permute-start(f32[1,32,6,384]{3,0,2,1:T(1,128)S(1)} %get-tuple-element.30), channel_id=1, source_target_pairs={{0,8},{8,16},{16,24},{24,32},{32,40},{40,48},{48,56},{56,64},{64,7... | collective-permute-start | bytes 884744 | tf_op jit(solution)/shard_map/ppermute | solution.py:22
  188.7 5.2 %collective-permute-start.3 = (f32[18,1,6,384]{3,0,2,1:T(8,128)}, f32[18,1,6,384]{3,0,2,1:T(8,128)}, u32[]{:S(2)}, u32[]{:S(2)}) collective-permute-start(f32[18,1,6,384]{3,0,2,1:T(8,128)} %get-tuple-element.26), channel_id=1, source_target_pairs={{0,1},{1,2},{2,3},{3,4},{4,5},{5,6},{6,7},{8,9},{9,10},{10,11},{11... | collective-permute-start | bytes 497672 | tf_op jit(solution)/shard_map/ppermute | solution.py:22
  195.3 6.3 %shard_map.66 = f32[32,5,16,128]{3,2,1,0:T(8,128)S(1)} custom-call(f32[5,5]{1,0:T(8,128)S(1)} %copy-done.5, f32[32,5,16,128]{3,2,1,0:T(8,128)S(1)} %all-to-all-done.3.lines_ref, f32[1024,512]{1,0:T(8,128)S(1)} %constant_dynamic-update-slice_fusion.mats_ref), custom_call_target="tpu_custom_call" | custom-call | tf_op jit(solution)/shard_map/pallas_call | solution.py:75
  204.2 34.0 %all-to-all-start.5 = ((f32[32,5,16,128]{3,2,1,0:T(8,128)}), f32[32,5,16,128]{3,2,1,0:T(8,128)S(1)}, u32[]{:S(2)}, u32[]{:S(2)}) async-start(f32[32,5,16,128]{3,2,1,0:T(8,128)} %copy-done.1), calls=%async_computation.5 | async-start | bytes 2621440 | tf_op jit(solution)/shard_map/all_to_all | solution.py:98
  238.2 6.2 %pad_maximum_fusion = (f32[18,33,6,384]{3,0,2,1:T(8,128)S(1)}, f32[18,33,6,384]{3,0,2,1:T(8,128)S(1)}) fusion(f32[18,1,6,384]{3,0,2,1:T(8,128)} %collective-permute-done.2, f32[1,32,6,384]{3,0,2,1:T(1,128)} %copy-done.14, f32[16,32,1,384]{3,0,2,1:T(8,128)} %bitcast.46, f32[16,32,5,384]{3,0,2,1:T(8,128)} %copy-done.6, f32[1,32,6,384]{3,0,2,1:T(1,128)} %copy-done.16, ...), kind=kLoop, calls=%fused_computation | loop fusion | flops 10948608 | bytes 16588800 | tf_op jit(solution)/shard_map/concatenate | solution.py:24
  247.4 3.3 %add_dynamic-update-slice_fusion.4 = f32[16,32,5,384]{3,0,2,1:T(8,128)S(1)} fusion(f32[16,32,5,384]{3,0,2,1:T(8,128)S(1)} %subtract_multiply_fusion, f32[]{:T(128)} %bitcast.9, f32[]{:T(128)} %bitcast.8, f32[]{:T(128)} %bitcast.7, f32[]{:T(128)} %bitcast.6, f32[]{:T(128)} %bitcast.5), kind=kLoop, calls=%fused_computation.34 | loop fusion | flops 1769471 | bytes 4718612
  250.7 3.3 %add_dynamic-update-slice_fusion.3 = f32[16,32,5,384]{3,0,2,1:T(8,128)S(1)} fusion(f32[16,32,5,384]{3,0,2,1:T(8,128)S(1)} %add_dynamic-update-slice_fusion.4, f32[16,32,5,384]{3,0,2,1:T(8,128)S(1)} %subtract_multiply_fusion, f32[]{:T(128)} %bitcast.14, f32[]{:T(128)} %bitcast.13, f32[]{:T(128)} %bitcast.12, f32[]{:T(128)} %bitcast.11, f32[]{:T(128)} %bitcast.10), kind=kLoop, calls=%fused_computation.33 | loop fusion | flops 1769472 | bytes 4718612
  254.1 3.3 %add_dynamic-update-slice_fusion.2 = f32[16,32,5,384]{3,0,2,1:T(8,128)S(1)} fusion(f32[16,32,5,384]{3,0,2,1:T(8,128)S(1)} %add_dynamic-update-slice_fusion.3, f32[16,32,5,384]{3,0,2,1:T(8,128)S(1)} %subtract_multiply_fusion, f32[]{:T(128)} %bitcast.19, f32[]{:T(128)} %bitcast.18, f32[]{:T(128)} %bitcast.17, f32[]{:T(128)} %bitcast.16, f32[]{:T(128)} %bitcast.15), kind=kLoop, calls=%fused_computation.32 | loop fusion | flops 1769472 | bytes 4718612
  257.4 4.0 %add_dynamic-update-slice_fusion.1 = f32[16,32,5,384]{3,0,2,1:T(8,128)S(1)} fusion(f32[16,32,5,384]{3,0,2,1:T(8,128)S(1)} %add_dynamic-update-slice_fusion.2, f32[16,32,5,384]{3,0,2,1:T(8,128)S(1)} %subtract_multiply_fusion, f32[]{:T(128)} %bitcast.24, f32[]{:T(128)} %bitcast.23, f32[]{:T(128)} %bitcast.22, f32[]{:T(128)} %bitcast.21, f32[]{:T(128)} %bitcast.20), kind=kLoop, calls=%fused_computation.31 | loop fusion | flops 1769472 | bytes 4718612
  261.4 3.2 %add_dynamic-update-slice_fusion = f32[16,32,5,384]{3,0,2,1:T(8,128)S(1)} fusion(f32[16,32,5,384]{3,0,2,1:T(8,128)S(1)} %add_dynamic-update-slice_fusion.1, f32[16,32,5,384]{3,0,2,1:T(8,128)S(1)} %subtract_multiply_fusion, f32[]{:T(128)} %bitcast.29, f32[]{:T(128)} %bitcast.28, f32[]{:T(128)} %bitcast.27, f32[]{:T(128)} %bitcast.26, f32[]{:T(128)} %bitcast.25), kind=kLoop, calls=%fused_computation.30 | loop fusion | flops 1769472 | bytes 4718612 | tf_op jit(solution)/shard_map/stack | solution.py:52
  268.9 3.1 %all-to-all-done.5 = f32[32,5,16,128]{3,2,1,0:T(8,128)S(1)} async-done(((f32[32,5,16,128]{3,2,1,0:T(8,128)}), f32[32,5,16,128]{3,2,1,0:T(8,128)S(1)}, u32[]{:S(2)}, u32[]{:S(2)}) %all-to-all-start.5) | async-done | bytes 1310752 | tf_op jit(solution)/shard_map/all_to_all | solution.py:98
  272.0 12.6 %fusion.6 = f32[16,32,5,384]{3,0,2,1:T(8,128)S(1)} fusion(f32[16,32,5,384]{3,0,2,1:T(8,128)} %copy-done.6, f32[1,32,6,384]{3,0,2,1:T(1,128)S(1)} %copy-done.17, f32[16,32,1,384]{3,0,2,1:T(8,128)S(1)} %bitcast.48, f32[1,32,6,384]{3,0,2,1:T(1,128)S(1)} %copy-done.15, f32[32,5,16,128]{3,2,1,0:T(8,128)S(1)} %all-to-all-done.5, ...), kind=kLoop, calls=%fused_computation.9 | loop fusion | flops 21626880 | bytes 28114944 | tf_op jit(solution)/shard_map/add | solution.py:116
  284.6 3.1 %copy.14 = f32[16,32,5,384]{3,1,2,0:T(8,128)} copy(f32[16,32,5,384]{3,0,2,1:T(8,128)S(1)} %fusion.6) | data formatting | bytes 7864320 | tf_op jit(solution)/shard_map/add | solution.py:116
  (54 shorter events, 28.8 us)
Async XLA Ops:
  4.4 2.4 copy-start.6
  91.1 7.8 %copy-start.5 = (f32[5,5]{1,0:T(8,128)S(1)}, f32[5,5]{1,0:T(8,128)}, u32[]{:S(2)}) copy-start(f32[5,5]{1,0:T(8,128)} %jac_ref.5) | copy-start | bytes 304
  91.1 34.9 %all-to-all-start.3 = ((f32[32,5,16,128]{3,2,1,0:T(8,128)}), f32[32,5,16,128]{3,2,1,0:T(8,128)S(1)}, u32[]{:S(2)}, u32[]{:S(2)}) async-start(f32[32,5,16,128]{3,2,1,0:T(8,128)} %get-tuple-element.31), calls=%async_computation.3 | async-start | bytes 2621440 | tf_op jit(solution)/shard_map/all_to_all | solution.py:98
  98.9 1.3 copy-start.3
  126.0 39.0 %all-to-all-start.2 = ((f32[32,5,16,128]{3,2,1,0:T(8,128)}), f32[32,5,16,128]{3,2,1,0:T(8,128)}, u32[]{:S(2)}, u32[]{:S(2)}) async-start(f32[32,5,16,128]{3,2,1,0:T(8,128)} %copy-done.4), calls=%async_computation.2 | async-start | bytes 2621440 | tf_op jit(solution)/shard_map/all_to_all | solution.py:98
  135.6 1.3 copy-start.2
  165.1 39.1 %all-to-all-start.4 = ((f32[32,5,16,128]{3,2,1,0:T(8,128)}), f32[32,5,16,128]{3,2,1,0:T(8,128)}, u32[]{:S(2)}, u32[]{:S(2)}) async-start(f32[32,5,16,128]{3,2,1,0:T(8,128)} %copy-done), calls=%async_computation.4 | async-start | bytes 2621440 | tf_op jit(solution)/shard_map/all_to_all | solution.py:98
  174.8 10.2 %copy-start.7 = (f32[16,32,5,384]{3,0,2,1:T(8,128)S(1)}, f32[16,32,5,384]{3,0,2,1:T(8,128)}, u32[]{:S(2)}) copy-start(f32[16,32,5,384]{3,0,2,1:T(8,128)} %copy-done.6) | copy-start | bytes 11796484
  176.6 9.3 %copy-start.11 = (f32[16,32,384]{2,0,1:T(8,128)}, f32[16,32,384]{2,0,1:T(8,128)S(1)}, u32[]{:S(2)}) copy-start(f32[16,32,384]{2,0,1:T(8,128)S(1)} %copy.18) | copy-start | bytes 2359300
  179.5 14.4 %copy-start.18 = (f32[5,5]{1,0:T(8,128)S(1)}, f32[5,5]{1,0:T(8,128)}, u32[]{:S(2)}) copy-start(f32[5,5]{1,0:T(8,128)} %param.11) | copy-start | bytes 304
  179.5 4.4 %collective-permute-start = (f32[1,32,6,384]{3,0,2,1:T(1,128)S(1)}, f32[1,32,6,384]{3,0,2,1:T(1,128)S(1)}, u32[]{:S(2)}, u32[]{:S(2)}) collective-permute-start(f32[1,32,6,384]{3,0,2,1:T(1,128)S(1)} %get-tuple-element.29), channel_id=1, source_target_pairs={{8,0},{16,8},{24,16},{32,24},{40,32},{48,40},{56,48},{64,56},{72,6... | collective-permute-start | bytes 884744 | tf_op jit(solution)/shard_map/ppermute | solution.py:23
  180.8 4.2 %collective-permute-start.1 = (f32[1,32,6,384]{3,0,2,1:T(1,128)S(1)}, f32[1,32,6,384]{3,0,2,1:T(1,128)S(1)}, u32[]{:S(2)}, u32[]{:S(2)}) collective-permute-start(f32[1,32,6,384]{3,0,2,1:T(1,128)S(1)} %get-tuple-element.30), channel_id=1, source_target_pairs={{0,8},{8,16},{16,24},{24,32},{32,40},{40,48},{48,56},{56,64},{64,7... | collective-permute-start | bytes 884744 | tf_op jit(solution)/shard_map/ppermute | solution.py:22
  183.9 10.7 %copy-start.14 = (f32[1,32,6,384]{3,0,2,1:T(1,128)}, f32[1,32,6,384]{3,0,2,1:T(1,128)S(1)}, u32[]{:S(2)}) copy-start(f32[1,32,6,384]{3,0,2,1:T(1,128)S(1)} %collective-permute-done) | copy-start | bytes 884740
  185.0 9.5 %copy-start.16 = (f32[1,32,6,384]{3,0,2,1:T(1,128)}, f32[1,32,6,384]{3,0,2,1:T(1,128)S(1)}, u32[]{:S(2)}) copy-start(f32[1,32,6,384]{3,0,2,1:T(1,128)S(1)} %collective-permute-done.1) | copy-start | bytes 884740
  186.0 52.2 %collective-permute-start.2 = (f32[18,1,6,384]{3,0,2,1:T(8,128)}, f32[18,1,6,384]{3,0,2,1:T(8,128)}, u32[]{:S(2)}, u32[]{:S(2)}) collective-permute-start(f32[18,1,6,384]{3,0,2,1:T(8,128)} %get-tuple-element.25), channel_id=1, source_target_pairs={{1,0},{2,1},{3,2},{4,3},{5,4},{6,5},{7,6},{9,8},{10,9},{11,10},{12... | collective-permute-start | bytes 497672 | tf_op jit(solution)/shard_map/ppermute | solution.py:23
  188.7 49.5 %collective-permute-start.3 = (f32[18,1,6,384]{3,0,2,1:T(8,128)}, f32[18,1,6,384]{3,0,2,1:T(8,128)}, u32[]{:S(2)}, u32[]{:S(2)}) collective-permute-start(f32[18,1,6,384]{3,0,2,1:T(8,128)} %get-tuple-element.26), channel_id=1, source_target_pairs={{0,1},{1,2},{2,3},{3,4},{4,5},{5,6},{6,7},{8,9},{9,10},{10,11},{11... | collective-permute-start | bytes 497672 | tf_op jit(solution)/shard_map/ppermute | solution.py:22
  204.2 67.8 %all-to-all-start.5 = ((f32[32,5,16,128]{3,2,1,0:T(8,128)}), f32[32,5,16,128]{3,2,1,0:T(8,128)S(1)}, u32[]{:S(2)}, u32[]{:S(2)}) async-start(f32[32,5,16,128]{3,2,1,0:T(8,128)} %copy-done.1), calls=%async_computation.5 | async-start | bytes 2621440 | tf_op jit(solution)/shard_map/all_to_all | solution.py:98
  244.4 3.0 %copy-start.9 = (f32[18,33,6,384]{3,0,2,1:T(8,128)}, f32[18,33,6,384]{3,0,2,1:T(8,128)S(1)}, u32[]{:S(2)}) copy-start(f32[18,33,6,384]{3,0,2,1:T(8,128)S(1)} %get-tuple-element.23) | copy-start | bytes 16422916
  244.4 13.0 %copy-start.10 = (f32[18,33,6,384]{3,0,2,1:T(8,128)}, f32[18,33,6,384]{3,0,2,1:T(8,128)S(1)}, u32[]{:S(2)}) copy-start(f32[18,33,6,384]{3,0,2,1:T(8,128)S(1)} %get-tuple-element.24) | copy-start | bytes 16422916
  257.4 9.1 %copy-start.8 = (f32[16,32,5,384]{3,0,2,1:T(8,128)S(1)}, f32[16,32,5,384]{3,0,2,1:T(8,128)}, u32[]{:S(2)}) copy-start(f32[16,32,5,384]{3,0,2,1:T(8,128)} %copy-done.6) | copy-start | bytes 11796484
  257.4 9.1 %copy-start.12 = (f32[16,32,384]{2,0,1:T(8,128)S(1)}, f32[16,32,384]{2,0,1:T(8,128)}, u32[]{:S(2)}) copy-start(f32[16,32,384]{2,0,1:T(8,128)} %copy-done.11) | copy-start | bytes 2359300
  257.4 9.1 %copy-start.15 = (f32[1,32,6,384]{3,0,2,1:T(1,128)S(1)}, f32[1,32,6,384]{3,0,2,1:T(1,128)}, u32[]{:S(2)}) copy-start(f32[1,32,6,384]{3,0,2,1:T(1,128)} %copy-done.14) | copy-start | bytes 884740
  257.4 9.1 %copy-start.17 = (f32[1,32,6,384]{3,0,2,1:T(1,128)S(1)}, f32[1,32,6,384]{3,0,2,1:T(1,128)}, u32[]{:S(2)}) copy-start(f32[1,32,6,384]{3,0,2,1:T(1,128)} %copy-done.16) | copy-start | bytes 884740
  264.6 1.9 copy-start.13
  (3 other events, 3.2 us)

commit v4 on v2

v4 whole, which is shorter than its diff:
```python
import functools

import jax
import jax.numpy as jnp
from jax import lax
from jax.experimental import pallas as pl
from jax.experimental.pallas import tpu as pltpu
from jax.sharding import PartitionSpec as P

section_step = 0.25
viscosity = 0.5


def halos(x, axis, dim):
    peers, length = (lax.axis_size(axis), x.shape[dim])
    up = [(i, (i + 1) % peers) for i in range(peers - 1)]
    down = [(j, i) for i, j in up]
    last = lax.slice_in_dim(x, length - 1, length, axis=dim)
    leading = lax.slice_in_dim(x, 0, 1, axis=dim)
    return lax.ppermute(last, axis, up), lax.ppermute(leading, axis, down)


def viscous(field, weight, before, after, wbefore, wafter, dim):
    up_f = jnp.concatenate([lax.slice_in_dim(field, 1, field.shape[dim], axis=dim), after], axis=dim)
    dn_f = jnp.concatenate([before, lax.slice_in_dim(field, 0, field.shape[dim] - 1, axis=dim)], axis=dim)
    up_w = jnp.concatenate([lax.slice_in_dim(weight, 1, weight.shape[dim], axis=dim), wafter], axis=dim)
    dn_w = jnp.concatenate([wbefore, lax.slice_in_dim(weight, 0, weight.shape[dim] - 1, axis=dim)], axis=dim)
    upper = 0.5 * (weight + up_w)
    lower = 0.5 * (weight + dn_w)
    return upper * (up_f - field) - lower * (field - dn_f), up_f, dn_f


def stencil(state, weight, ax_halo, rad_halo, jac_radial):
    nv = state.shape[2]
    (xb, xa), (rb, ra) = ax_halo, rad_halo
    visc_ax, _, _ = viscous(state, weight, xb[:, :, :nv], xa[:, :, :nv], xb[:, :, nv:], xa[:, :, nv:], 0)
    visc_rad, up_f, dn_f = viscous(state, weight, rb[:, :, :nv], ra[:, :, :nv], rb[:, :, nv:], ra[:, :, nv:], 1)
    spread = 0.5 * (up_f - dn_f)
    mixed = jac_radial[0][None, None, :, None] * spread[:, :, 0:1]
    for k in range(1, nv):
        mixed = mixed + jac_radial[k][None, None, :, None] * spread[:, :, k:k + 1]
    return viscosity * visc_ax + (mixed + viscosity * visc_rad)


def line_kernel(jac_ref, lines_ref, mats_ref, out_ref):
    S, V, XL, C = lines_ref.shape
    nx = S * XL
    cols = [lines_ref[:, v, :, :].reshape(nx, C) for v in range(V)]
    wide = jnp.concatenate(cols, axis=1)
    prod = jnp.dot(
        mats_ref[...], wide, precision=lax.Precision.HIGHEST, preferred_element_type=jnp.float32
    )
    smooth = prod[:nx]
    slope = prod[nx:]
    for v in range(V):
        mix = jac_ref[0, v] * slope[:, 0:C]
        for k in range(1, V):
            mix = mix + jac_ref[k, v] * slope[:, k * C:(k + 1) * C]
        res = cols[v] - smooth[:, v * C:(v + 1) * C] + section_step * mix
        out_ref[:, v, :, :] = res.reshape(S, XL, C)


def line_section(lines, mats, jac_axial):
    S, V, XL, C = lines.shape
    return pl.pallas_call(
        line_kernel,
        out_shape=jax.ShapeDtypeStruct(lines.shape, lines.dtype),
        in_specs=[
            pl.BlockSpec(memory_space=pltpu.SMEM),
            pl.BlockSpec(memory_space=pltpu.VMEM),
            pl.BlockSpec(memory_space=pltpu.VMEM),
        ],
        out_specs=pl.BlockSpec(memory_space=pltpu.VMEM),
        compiler_params=pltpu.CompilerParams(vmem_limit_bytes=48 * 1024 * 1024),
    )(jac_axial, lines, mats)


def body(state, metric, deriv, filt_corr, jac_axial, jac_radial):
    nx, nr, nv, na = state.shape
    peers = lax.axis_size("ax")
    assert nr == peers
    mats = jnp.concatenate([filt_corr, deriv], axis=0)
    weight = metric.reshape(metric.shape[0], metric.shape[1], 1, metric.shape[2])
    packed = jnp.concatenate([state, weight], axis=2)
    ax_halo = halos(packed, "ax", 0)
    rad_halo = halos(packed, "rad", 1)
    send = jnp.transpose(state, (1, 2, 0, 3))
    send, ax_halo, rad_halo = lax.optimization_barrier((send, ax_halo, rad_halo))
    lines = lax.all_to_all(send, "ax", split_axis=0, concat_axis=0, tiled=True)
    local = stencil(state, weight, ax_halo, rad_halo, jac_radial)
    lines, local = lax.optimization_barrier((lines, local))
    res = line_section(lines, mats, jac_axial)
    ret = lax.all_to_all(res, "ax", split_axis=0, concat_axis=0, tiled=True)
    return jnp.transpose(ret, (2, 0, 1, 3)) + section_step * local


def solution(mesh):
    in_specs = (P("ax", "rad", None, None), P("ax", "rad", None), P(), P(), P(), P())
    out_specs = P("ax", "rad", None, None)
    return jax.shard_map(body, mesh=mesh, in_specs=in_specs, out_specs=out_specs, check_vma=False)
```

time: 289 us -> 244 us (0.84)
  other arithmetic: 46.7 us -> 13.3 us
  blocking collectives: 118 us -> 96 us
  local copies, waits for them, and re-layouts: 12.7 us -> 19.6 us
  waiting for transfers between devices: 71 us -> 75.3 us
    all_to_all x1, waiting for transfers between devices: 0.01 us -> 66.5 us  [body(): lines = lax.all_to_all(send, 'ax', split_axis=0, concat_axis=0, tiled=True)]
    ppermute x4, waiting for transfers between devices: 71 us -> 8.85 us  [halos(): return (lax.ppermute(last, axis, up), lax.ppermute(leading, axis, down))]
    all_to_all x1, blocking collectives: 118 us -> 96 us  [body(): ret = lax.all_to_all(res, 'ax', split_axis=0, concat_axis=0, tiled=True)]
    unnamed x5 -> x0, other arithmetic: 17.4 us -> none
    mul x2, other arithmetic: 7.67 us -> 1.56 us  [the longest x1 0.82 us: viscous(): upper = 0.5 * (weight + up_w)]
    concatenate x1, other arithmetic: 4.98 us -> 0.02 us  [body(): packed = jnp.concatenate([state, weight], axis=2)]
    another operation x1 -> x0, other arithmetic: 4.5 us -> none  [radial_terms(): return jnp.stack(mixed, axis=2) + viscosity * flux]
    ppermute x4, starting transfers between devices: 12.4 us -> 8.89 us  [halos(): return (lax.ppermute(last, axis, up), lax.ppermute(leading, axis, down))]
  transfers between devices with their start and end apart: 5 -> 5, of which waited for: 2 -> 3; matrix products, arithmetic and copies ran while one was open for 17% -> 9% of each run, Pallas kernels for 0% -> 0%
where the time goes in v4:
time: 244 us; the launch traced here: 243 us
  blocking collectives  96 us (39%)
  waiting for transfers between devices  75.3 us (31%)
  starting transfers between devices  22.4 us (9%)
  local copies, waits for them, and re-layouts  19.6 us (8%)
  Pallas kernels  16.3 us (7%)
  other arithmetic  13.3 us (5%)
    all_to_all x1, blocking collectives, body(): ret = lax.all_to_all(res, 'ax', split_axis=0, concat_axis=0, tiled=True)  96 us
    all_to_all x1, waiting for transfers between devices, body(): lines = lax.all_to_all(send, 'ax', split_axis=0, concat_axis=0, tiled=True)  66.5 us
    pallas_call x1, Pallas kernels, line_section(): pl.pallas_call(line_kernel, out_shape=jax.ShapeDtypeStruct(lines.shape, l...  16.3 us
    all_to_all x1, starting transfers between devices, body(): lines = lax.all_to_all(send, 'ax', split_axis=0, concat_axis=0, tiled=True)  13.5 us
    add x1, other arithmetic, stencil(): return viscosity * visc_ax + (mixed + viscosity * visc_rad)  10.5 us
    ppermute x4, starting transfers between devices, halos(): return (lax.ppermute(last, axis, up), lax.ppermute(leading, axis, down))  8.89 us
    ppermute x4, waiting for transfers between devices, halos(): return (lax.ppermute(last, axis, up), lax.ppermute(leading, axis, down))  8.85 us
    unnamed x40, local copies, waits for them, and re-layouts  8.62 us
  transfers between devices with their start and end apart: 5, of which 3 were waited for; matrix products, arithmetic and copies ran while one was open for 9% of the time, Pallas kernels for 0%

profile of v4, /device:TPU:6, one launch (start us, length us, event | category | flops | bytes accessed | tf_op | source)
XLA Modules:
  0.0 243.2 jit_solution(14829692622131132613)
XLA Ops:
  0.0 4.5 %copy.38 = f32[16,32,5,384]{3,0,2,1:T(8,128)S(1)} copy(f32[16,32,5,384]{3,1,2,0:T(8,128)} %param.6) | data formatting | bytes 7864320 | tf_op args[0]
  5.4 1.8 collective-permute-start
  7.2 1.3 collective-permute-start.1
  8.5 3.7 %collective-permute-start.2 = (f32[16,1,6,384]{3,0,2,1:T(8,128)S(1)}, f32[16,1,6,384]{3,0,2,1:T(8,128)S(1)}, u32[]{:S(2)}, u32[]{:S(2)}) collective-permute-start(f32[16,1,6,384]{3,0,2,1:T(8,128)S(1)} %get-tuple-element.20), channel_id=1, source_target_pairs={{0,1},{1,2},{2,3},{3,4},{4,5},{5,6},{6,7},{8,9},{9,10},{10,11},{11... | collective-permute-start | bytes 442376 | tf_op jit(solution)/shard_map/ppermute | solution.py:20
  12.3 2.1 collective-permute-start.3
  14.4 2.9 %collective-permute-done.2 = f32[16,1,6,384]{3,0,2,1:T(8,128)S(1)} collective-permute-done((f32[16,1,6,384]{3,0,2,1:T(8,128)S(1)}, f32[16,1,6,384]{3,0,2,1:T(8,128)S(1)}, u32[]{:S(2)}, u32[]{:S(2)}) %collective-permute-start.2) | collective-permute-done | bytes 147488 | tf_op jit(solution)/shard_map/ppermute | solution.py:20
  17.2 6.0 %collective-permute-done.3 = f32[16,1,6,384]{3,0,2,1:T(8,128)S(1)} collective-permute-done((f32[16,1,6,384]{3,0,2,1:T(8,128)S(1)}, f32[16,1,6,384]{3,0,2,1:T(8,128)S(1)}, u32[]{:S(2)}, u32[]{:S(2)}) %collective-permute-start.3) | collective-permute-done | bytes 147488 | tf_op jit(solution)/shard_map/ppermute | solution.py:20
  23.3 0.6 copy-done.15
  23.9 13.5 %all-to-all-start = ((f32[32,5,16,384]{3,2,1,0:T(8,128)}), f32[32,5,16,384]{3,2,1,0:T(8,128)}, u32[]{:S(2)}, u32[]{:S(2)}) async-start(f32[32,5,16,384]{3,2,1,0:T(8,128)} %bitcast.42), calls=%async_computation | async-start | bytes 7864320 | tf_op jit(solution)/shard_map/all_to_all | solution.py:89
  39.1 1.0 slice_bitcast_fusion.5
  40.1 0.9 slice_bitcast_fusion.6
  42.8 0.9 slice.99
  43.6 0.9 slice.102
  44.6 0.7 subtract_multiply_fusion
  45.3 0.8 slice_bitcast_fusion.9
  46.1 0.9 slice_bitcast_fusion.7
  47.0 0.8 fusion.5
  47.8 1.3 slice_bitcast_fusion.4
  49.1 1.1 copy-done.3
  50.2 10.5 %fusion.3 = f32[16,32,5,384]{3,0,2,1:T(8,128)} fusion(f32[1,32,5,384]{3,0,2,1:T(1,128)} %slice.99, f32[15,32,5,384]{3,0,2,1:T(8,128)S(1)} %get-tuple-element.31, f32[15,32,5,384]{3,0,2,1:T(8,128)S(1)} %get-tuple-element.30, f32[1,32,5,384]{3,0,2,1:T(1,128)} %slice.102, f32[16,31,5,384]{3,0,2,1:T(8,128)S(1)} %get-tuple-element.29, ...), kind=kLoop, calls=%fused_computation.4 | loop fusion | flops 26542080 | bytes 30670948 | tf_op jit(solution)/shard_map/add | solution.py:42
  60.8 66.5 %all-to-all-done.lines_ref = f32[32,5,16,384]{3,2,1,0:T(8,128)} async-done(((f32[32,5,16,384]{3,2,1,0:T(8,128)}), f32[32,5,16,384]{3,2,1,0:T(8,128)}, u32[]{:S(2)}, u32[]{:S(2)}) %all-to-all-start) | async-done | bytes 3932192 | tf_op jit(solution)/shard_map/all_to_all | solution.py:89
  127.2 16.3 %shard_map.64 = f32[32,5,16,384]{3,2,1,0:T(8,128)S(1)} custom-call(f32[5,5]{1,0:T(8,128)S(1)} %copy-done, f32[32,5,16,384]{3,2,1,0:T(8,128)} %all-to-all-done.lines_ref, f32[1024,512]{1,0:T(8,128)S(1)} %pad_maximum_fusion.2.mats_ref), custom_call_target="tpu_custom_call" | custom-call | tf_op jit(solution)/shard_map/pallas_call | solution.py:65
  143.5 96.0 %all_to_all.10 = f32[32,5,16,384]{3,2,1,0:T(8,128)S(1)} all-to-all(f32[32,5,16,384]{3,2,1,0:T(8,128)S(1)} %shard_map.64), channel_id=1, replica_groups=mesh['ax'=32,'rad'=8] {'ax'}, dimensions={0} | all-to-all | bytes 7864320 | tf_op jit(solution)/shard_map/all_to_all | solution.py:93
  240.1 3.1 %copy.25 = f32[16,32,5,384]{3,1,2,0:T(8,128)} copy(f32[16,32,5,384]{3,0,2,1:T(8,128)S(1)} %bitcast_add_fusion) | data formatting | bytes 7864320 | tf_op jit(solution)/shard_map/add | solution.py:94
  (49 shorter events, 4.9 us)
Async XLA Ops:
  0.0 4.5 %copy-start.5 = (f32[16,32,384]{2,1,0:T(8,128)S(1)}, f32[16,32,384]{2,1,0:T(8,128)}, u32[]{:S(2)}) copy-start(f32[16,32,384]{2,1,0:T(8,128)} %param.7) | copy-start | bytes 2359300
  4.5 4.0 %copy-start.1 = (f32[16,32,5,384]{3,0,2,1:T(8,128)}, f32[16,32,5,384]{3,0,2,1:T(8,128)S(1)}, u32[]{:S(2)}) copy-start(f32[16,32,5,384]{3,0,2,1:T(8,128)S(1)} %copy.38) | copy-start | bytes 11796484
  5.4 17.8 %collective-permute-start = (f32[1,32,6,384]{3,0,2,1:T(1,128)S(1)}, f32[1,32,6,384]{3,0,2,1:T(1,128)S(1)}, u32[]{:S(2)}, u32[]{:S(2)}) collective-permute-start(f32[1,32,6,384]{3,0,2,1:T(1,128)S(1)} %get-tuple-element.22), channel_id=1, source_target_pairs={{0,8},{8,16},{16,24},{24,32},{32,40},{40,48},{48,56},{56,64},{64,7... | collective-permute-start | bytes 884744 | tf_op jit(solution)/shard_map/ppermute | solution.py:20
  7.2 16.1 %collective-permute-start.1 = (f32[1,32,6,384]{3,0,2,1:T(1,128)S(1)}, f32[1,32,6,384]{3,0,2,1:T(1,128)S(1)}, u32[]{:S(2)}, u32[]{:S(2)}) collective-permute-start(f32[1,32,6,384]{3,0,2,1:T(1,128)S(1)} %get-tuple-element.21), channel_id=1, source_target_pairs={{8,0},{16,8},{24,16},{32,24},{40,32},{48,40},{56,48},{64,56},{72,6... | collective-permute-start | bytes 884744 | tf_op jit(solution)/shard_map/ppermute | solution.py:20
  8.5 8.7 %collective-permute-start.2 = (f32[16,1,6,384]{3,0,2,1:T(8,128)S(1)}, f32[16,1,6,384]{3,0,2,1:T(8,128)S(1)}, u32[]{:S(2)}, u32[]{:S(2)}) collective-permute-start(f32[16,1,6,384]{3,0,2,1:T(8,128)S(1)} %get-tuple-element.20), channel_id=1, source_target_pairs={{0,1},{1,2},{2,3},{3,4},{4,5},{5,6},{6,7},{8,9},{9,10},{10,11},{11... | collective-permute-start | bytes 442376 | tf_op jit(solution)/shard_map/ppermute | solution.py:20
  12.3 11.0 %collective-permute-start.3 = (f32[16,1,6,384]{3,0,2,1:T(8,128)S(1)}, f32[16,1,6,384]{3,0,2,1:T(8,128)S(1)}, u32[]{:S(2)}, u32[]{:S(2)}) collective-permute-start(f32[16,1,6,384]{3,0,2,1:T(8,128)S(1)} %get-tuple-element.19), channel_id=1, source_target_pairs={{1,0},{2,1},{3,2},{4,3},{5,4},{6,5},{7,6},{9,8},{10,9},{11,10},{12... | collective-permute-start | bytes 442376 | tf_op jit(solution)/shard_map/ppermute | solution.py:20
  17.2 6.0 %copy-start.13 = (f32[16,1,6,384]{3,0,2,1:T(8,128)}, f32[16,1,6,384]{3,0,2,1:T(8,128)S(1)}, u32[]{:S(2)}) copy-start(f32[16,1,6,384]{3,0,2,1:T(8,128)S(1)} %collective-permute-done.2) | copy-start | bytes 442372
  23.2 0.7 copy-start.15
  23.2 20.4 %copy-start.11 = (f32[1,32,6,384]{3,0,2,1:T(1,128)}, f32[1,32,6,384]{3,0,2,1:T(1,128)S(1)}, u32[]{:S(2)}) copy-start(f32[1,32,6,384]{3,0,2,1:T(1,128)S(1)} %collective-permute-done) | copy-start | bytes 884740
  23.2 19.5 %copy-start.12 = (f32[1,32,6,384]{3,0,2,1:T(1,128)}, f32[1,32,6,384]{3,0,2,1:T(1,128)S(1)}, u32[]{:S(2)}) copy-start(f32[1,32,6,384]{3,0,2,1:T(1,128)S(1)} %collective-permute-done.1) | copy-start | bytes 884740
  23.9 103.4 %all-to-all-start = ((f32[32,5,16,384]{3,2,1,0:T(8,128)}), f32[32,5,16,384]{3,2,1,0:T(8,128)}, u32[]{:S(2)}, u32[]{:S(2)}) async-start(f32[32,5,16,384]{3,2,1,0:T(8,128)} %bitcast.42), calls=%async_computation | async-start | bytes 7864320 | tf_op jit(solution)/shard_map/all_to_all | solution.py:89
  37.4 1.2 copy-start.9
  37.4 1.5 copy-start.10
  37.6 1.5 copy-start.17
  38.9 2.7 %copy-start.2 = (f32[16,32,5,384]{3,0,2,1:T(8,128)S(1)}, f32[16,32,5,384]{3,0,2,1:T(8,128)}, u32[]{:S(2)}) copy-start(f32[16,32,5,384]{3,0,2,1:T(8,128)} %copy-done.1) | copy-start | bytes 11796484
  42.1 2.4 copy-start.14
  42.2 2.4 copy-start.16
  44.5 2.4 copy-start.6
  44.6 2.4 copy-start.7
  44.6 2.4 copy-start.8
  47.8 2.4 copy-start.3
  50.2 77.0 %copy-start = (f32[5,5]{1,0:T(8,128)S(1)}, f32[5,5]{1,0:T(8,128)}, u32[]{:S(2)}) copy-start(f32[5,5]{1,0:T(8,128)} %jac_ref.1) | copy-start | bytes 304
  143.5 96.0 %copy-start.4 = (f32[16,32,5,384]{3,0,2,1:T(8,128)S(1)}, f32[16,32,5,384]{3,0,2,1:T(8,128)}, u32[]{:S(2)}) copy-start(f32[16,32,5,384]{3,0,2,1:T(8,128)} %fusion.3) | copy-start | bytes 11796484

commit v5 on v4

--- a/solution.py
+++ b/solution.py
@@ -82,15 +82,16 @@
     mats = jnp.concatenate([filt_corr, deriv], axis=0)
     weight = metric.reshape(metric.shape[0], metric.shape[1], 1, metric.shape[2])
     packed = jnp.concatenate([state, weight], axis=2)
+    send = jnp.transpose(state, (1, 2, 0, 3))
+    lines = lax.all_to_all(send, "ax", split_axis=0, concat_axis=0, tiled=True)
+    lines, packed = lax.optimization_barrier((lines, packed))
     ax_halo = halos(packed, "ax", 0)
     rad_halo = halos(packed, "rad", 1)
-    send = jnp.transpose(state, (1, 2, 0, 3))
-    send, ax_halo, rad_halo = lax.optimization_barrier((send, ax_halo, rad_halo))
-    lines = lax.all_to_all(send, "ax", split_axis=0, concat_axis=0, tiled=True)
+    res = line_section(lines, mats, jac_axial)
+    res, ax_halo, rad_halo = lax.optimization_barrier((res, ax_halo, rad_halo))
+    ret = lax.all_to_all(res, "ax", split_axis=0, concat_axis=0, tiled=True)
     local = stencil(state, weight, ax_halo, rad_halo, jac_radial)
-    lines, local = lax.optimization_barrier((lines, local))
-    res = line_section(lines, mats, jac_axial)
-    ret = lax.all_to_all(res, "ax", split_axis=0, concat_axis=0, tiled=True)
+    ret, local = lax.optimization_barrier((ret, local))
     return jnp.transpose(ret, (2, 0, 1, 3)) + section_step * local
 
 

time: 244 us -> 251 us (1.029)
  blocking collectives: 96 us -> 0 us
  waiting for transfers between devices: 75.3 us -> 161 us
  other arithmetic: 13.3 us -> 21.3 us
  starting transfers between devices: 22.4 us -> 30.1 us
    all_to_all x1 -> x0, blocking collectives: 96 us -> none  [body(): ret = lax.all_to_all(res, 'ax', split_axis=0, concat_axis=0, tiled=True)]
    all_to_all x0 -> x1, waiting for transfers between devices: none -> 75.1 us  [body(): ret = lax.all_to_all(res, 'ax', split_axis=0, concat_axis=0, tiled=True)]
    all_to_all x1, waiting for transfers between devices: 66.5 us -> 85.7 us  [body(): lines = lax.all_to_all(send, 'ax', split_axis=0, concat_axis=0, tiled=True)]
    all_to_all x0 -> x1, starting transfers between devices: none -> 9.79 us  [body(): ret = lax.all_to_all(res, 'ax', split_axis=0, concat_axis=0, tiled=True)]
    ppermute x4, waiting for transfers between devices: 8.85 us -> 0.01 us  [halos(): return (lax.ppermute(last, axis, up), lax.ppermute(leading, axis, down))]
    concatenate x1, other arithmetic: 0.02 us -> 4.9 us  [body(): packed = jnp.concatenate([state, weight], axis=2)]
    slice x0 -> x2, local copies, waits for them, and re-layouts: none -> 3.78 us  [halos(): leading = lax.slice_in_dim(x, 0, 1, axis=dim)]
    unnamed x40 -> x32, local copies, waits for them, and re-layouts: 8.62 us -> 12.2 us
  transfers between devices with their start and end apart: 5 -> 6, of which waited for: 3 -> 2; matrix products, arithmetic and copies ran while one was open for 9% -> 9% of each run, Pallas kernels for 0% -> 7%
where the time goes in v5:
time: 251 us
  waiting for transfers between devices  161 us (64%)
  starting transfers between devices  30.1 us (12%)
  local copies, waits for them, and re-layouts  21.5 us (9%)
  other arithmetic  21.3 us (8%)
  Pallas kernels  16.5 us (7%)
    all_to_all x1, waiting for transfers between devices, body(): lines = lax.all_to_all(send, 'ax', split_axis=0, concat_axis=0, tiled=True)  85.7 us
    all_to_all x1, waiting for transfers between devices, body(): ret = lax.all_to_all(res, 'ax', split_axis=0, concat_axis=0, tiled=True)  75.1 us
    pallas_call x1, Pallas kernels, line_section(): pl.pallas_call(line_kernel, out_shape=jax.ShapeDtypeStruct(lines.shape, l...  16.5 us
    unnamed x32, local copies, waits for them, and re-layouts  12.2 us
    all_to_all x1, starting transfers between devices, body(): lines = lax.all_to_all(send, 'ax', split_axis=0, concat_axis=0, tiled=True)  11.7 us
    all_to_all x1, starting transfers between devices, body(): ret = lax.all_to_all(res, 'ax', split_axis=0, concat_axis=0, tiled=True)  9.79 us
    add x1, other arithmetic, stencil(): return viscosity * visc_ax + (mixed + viscosity * visc_rad)  9.54 us
    ppermute x4, starting transfers between devices, halos(): return (lax.ppermute(last, axis, up), lax.ppermute(leading, axis, down))  8.62 us
  transfers between devices with their start and end apart: 6, of which 2 were waited for; matrix products, arithmetic and copies ran while one was open for 9% of the time, Pallas kernels for 7%

profile of v5, /device:TPU:6, one launch (start us, length us, event | category | flops | bytes accessed | tf_op | source)
XLA Modules:
  0.0 250.6 jit_solution(5707597750784267166)
XLA Ops:
  0.0 6.3 %copy.38 = f32[16,32,5,384]{3,0,2,1:T(8,128)} copy(f32[16,32,5,384]{3,1,2,0:T(8,128)} %param.6) | data formatting | bytes 7864320 | tf_op args[0]
  6.3 11.7 %all-to-all-start = ((f32[32,5,16,384]{3,2,1,0:T(8,128)}), f32[32,5,16,384]{3,2,1,0:T(8,128)}, u32[]{:S(2)}, u32[]{:S(2)}) async-start(f32[32,5,16,384]{3,2,1,0:T(8,128)} %bitcast.42), calls=%async_computation | async-start | bytes 7864320 | tf_op jit(solution)/shard_map/all_to_all | solution.py:86
  18.5 4.9 %pad_maximum_fusion = f32[16,32,6,384]{3,0,2,1:T(8,128)} fusion(f32[16,32,1,384]{3,0,2,1:T(8,128)S(1)} %bitcast.43, f32[16,32,5,384]{3,0,2,1:T(8,128)} %copy.38), kind=kLoop, calls=%fused_computation | loop fusion | flops 1179648 | bytes 9437184 | tf_op jit(solution)/shard_map/concatenate | solution.py:84
  23.4 85.7 %all-to-all-done.lines_ref = f32[32,5,16,384]{3,2,1,0:T(8,128)} async-done(((f32[32,5,16,384]{3,2,1,0:T(8,128)}), f32[32,5,16,384]{3,2,1,0:T(8,128)}, u32[]{:S(2)}, u32[]{:S(2)}) %all-to-all-start) | async-done | bytes 3932192 | tf_op jit(solution)/shard_map/all_to_all | solution.py:86
  109.2 2.8 %fusion.10 = (f32[1,32,6,384]{3,0,2,1:T(1,128)S(1)}, f32[1,32,6,384]{3,0,2,1:T(1,128)S(1)}) fusion(f32[16,32,6,384]{3,0,2,1:T(8,128)} %pad_maximum_fusion), kind=kLoop, calls=%fused_computation.41 | loop fusion | bytes 1179648 | tf_op jit(solution)/shard_map/slice | solution.py:19
  112.0 1.3 collective-permute-start
  113.3 1.3 collective-permute-start.1
  114.6 1.0 fusion.9
  115.6 3.6 %collective-permute-start.2 = (f32[16,1,6,384]{3,0,2,1:T(8,128)S(1)}, f32[16,1,6,384]{3,0,2,1:T(8,128)S(1)}, u32[]{:S(2)}, u32[]{:S(2)}) collective-permute-start(f32[16,1,6,384]{3,0,2,1:T(8,128)S(1)} %get-tuple-element.24), channel_id=1, source_target_pairs={{0,1},{1,2},{2,3},{3,4},{4,5},{5,6},{6,7},{8,9},{9,10},{10,11},{11... | collective-permute-start | bytes 442376 | tf_op jit(solution)/shard_map/ppermute | solution.py:20
  119.2 2.4 collective-permute-start.3
  121.6 1.5 pad_maximum_fusion.3.mats_ref
  123.2 16.5 %shard_map.64 = f32[32,5,16,384]{3,2,1,0:T(8,128)S(1)} custom-call(f32[5,5]{1,0:T(8,128)S(1)} %copy-done.1, f32[32,5,16,384]{3,2,1,0:T(8,128)} %all-to-all-done.lines_ref, f32[1024,512]{1,0:T(8,128)S(1)} %pad_maximum_fusion.3.mats_ref), custom_call_target="tpu_custom_call" | custom-call | tf_op jit(solution)/shard_map/pallas_call | solution.py:65
  139.7 1.9 copy-done
  141.6 9.8 %all-to-all-start.1 = ((f32[32,5,16,384]{3,2,1,0:T(8,128)}), f32[32,5,16,384]{3,2,1,0:T(8,128)}, u32[]{:S(2)}, u32[]{:S(2)}) async-start(f32[32,5,16,384]{3,2,1,0:T(8,128)} %copy-done), calls=%async_computation.1 | async-start | bytes 7864320 | tf_op jit(solution)/shard_map/all_to_all | solution.py:92
  152.5 0.5 slice_bitcast_fusion.15
  153.5 0.5 fusion.11
  154.1 0.6 fusion.12
  155.0 0.7 subtract_multiply_fusion
  156.1 0.8 fusion.5
  157.3 1.7 copy-done.3
  159.1 9.5 %fusion.3 = f32[16,32,5,384]{3,0,2,1:T(8,128)} fusion(f32[1,32,5,384]{3,0,2,1:T(1,128)S(1)} %slice-done, f32[15,32,5,384]{3,0,2,1:T(8,128)S(1)} %get-tuple-element.35, f32[15,32,5,384]{3,0,2,1:T(8,128)S(1)} %get-tuple-element.34, f32[1,32,5,384]{3,0,2,1:T(1,128)S(1)} %slice-done.1, f32[16,31,5,384]{3,0,2,1:T(8,128)S(1)} %get-tuple-element.33, ...), kind=kLoop, calls=%fused_computation.5 | loop fusion | flops 26542080 | bytes 30670948 | tf_op jit(solution)/shard_map/add | solution.py:42
  168.6 75.1 %all-to-all-done.1 = f32[32,5,16,384]{3,2,1,0:T(8,128)} async-done(((f32[32,5,16,384]{3,2,1,0:T(8,128)}), f32[32,5,16,384]{3,2,1,0:T(8,128)}, u32[]{:S(2)}, u32[]{:S(2)}) %all-to-all-start.1) | async-done | bytes 3932192 | tf_op jit(solution)/shard_map/all_to_all | solution.py:92
  243.7 3.8 %bitcast_add_fusion = f32[16,32,5,384]{3,0,2,1:T(8,128)S(1)} fusion(f32[32,5,16,384]{3,2,1,0:T(8,128)} %all-to-all-done.1, f32[16,32,5,384]{3,0,2,1:T(8,128)} %fusion.3), kind=kLoop, calls=%fused_computation.10 | loop fusion | flops 1966080 | bytes 11796480 | tf_op jit(solution)/shard_map/add | solution.py:95
  247.5 3.1 %copy.25 = f32[16,32,5,384]{3,1,2,0:T(8,128)} copy(f32[16,32,5,384]{3,0,2,1:T(8,128)S(1)} %bitcast_add_fusion) | data formatting | bytes 7864320 | tf_op jit(solution)/shard_map/add | solution.py:95
  (45 shorter events, 3.1 us)
Async XLA Ops:
  6.3 11.7 %copy-start.4 = (f32[16,32,384]{2,1,0:T(8,128)S(1)}, f32[16,32,384]{2,1,0:T(8,128)}, u32[]{:S(2)}) copy-start(f32[16,32,384]{2,1,0:T(8,128)} %param.7) | copy-start | bytes 2359300
  6.3 102.9 %all-to-all-start = ((f32[32,5,16,384]{3,2,1,0:T(8,128)}), f32[32,5,16,384]{3,2,1,0:T(8,128)}, u32[]{:S(2)}, u32[]{:S(2)}) async-start(f32[32,5,16,384]{3,2,1,0:T(8,128)} %bitcast.42), calls=%async_computation | async-start | bytes 7864320 | tf_op jit(solution)/shard_map/all_to_all | solution.py:86
  18.5 103.1 %copy-start.5 = (f32[512,512]{1,0:T(8,128)S(1)}, f32[512,512]{1,0:T(8,128)}, u32[]{:S(2)}) copy-start(f32[512,512]{1,0:T(8,128)} %param.8) | copy-start | bytes 3145732
  23.4 99.7 %copy-start.1 = (f32[5,5]{1,0:T(8,128)S(1)}, f32[5,5]{1,0:T(8,128)}, u32[]{:S(2)}) copy-start(f32[5,5]{1,0:T(8,128)} %jac_ref.1) | copy-start | bytes 304
  112.0 29.6 %collective-permute-start = (f32[1,32,6,384]{3,0,2,1:T(1,128)S(1)}, f32[1,32,6,384]{3,0,2,1:T(1,128)S(1)}, u32[]{:S(2)}, u32[]{:S(2)}) collective-permute-start(f32[1,32,6,384]{3,0,2,1:T(1,128)S(1)} %get-tuple-element.26), channel_id=1, source_target_pairs={{0,8},{8,16},{16,24},{24,32},{32,40},{40,48},{48,56},{56,64},{64,7... | collective-permute-start | bytes 884744 | tf_op jit(solution)/shard_map/ppermute | solution.py:20
  113.3 28.3 %collective-permute-start.1 = (f32[1,32,6,384]{3,0,2,1:T(1,128)S(1)}, f32[1,32,6,384]{3,0,2,1:T(1,128)S(1)}, u32[]{:S(2)}, u32[]{:S(2)}) collective-permute-start(f32[1,32,6,384]{3,0,2,1:T(1,128)S(1)} %get-tuple-element.25), channel_id=1, source_target_pairs={{8,0},{16,8},{24,16},{32,24},{40,32},{48,40},{56,48},{64,56},{72,6... | collective-permute-start | bytes 884744 | tf_op jit(solution)/shard_map/ppermute | solution.py:20
  115.6 25.9 %collective-permute-start.2 = (f32[16,1,6,384]{3,0,2,1:T(8,128)S(1)}, f32[16,1,6,384]{3,0,2,1:T(8,128)S(1)}, u32[]{:S(2)}, u32[]{:S(2)}) collective-permute-start(f32[16,1,6,384]{3,0,2,1:T(8,128)S(1)} %get-tuple-element.24), channel_id=1, source_target_pairs={{0,1},{1,2},{2,3},{3,4},{4,5},{5,6},{6,7},{8,9},{9,10},{10,11},{11... | collective-permute-start | bytes 442376 | tf_op jit(solution)/shard_map/ppermute | solution.py:20
  119.2 22.3 %collective-permute-start.3 = (f32[16,1,6,384]{3,0,2,1:T(8,128)S(1)}, f32[16,1,6,384]{3,0,2,1:T(8,128)S(1)}, u32[]{:S(2)}, u32[]{:S(2)}) collective-permute-start(f32[16,1,6,384]{3,0,2,1:T(8,128)S(1)} %get-tuple-element.23), channel_id=1, source_target_pairs={{1,0},{2,1},{3,2},{4,3},{5,4},{6,5},{7,6},{9,8},{10,9},{11,10},{12... | collective-permute-start | bytes 442376 | tf_op jit(solution)/shard_map/ppermute | solution.py:20
  139.7 1.9 copy-start
  141.5 10.0 %copy-start.10 = (f32[16,1,6,384]{3,0,2,1:T(8,128)}, f32[16,1,6,384]{3,0,2,1:T(8,128)S(1)}, u32[]{:S(2)}) copy-start(f32[16,1,6,384]{3,0,2,1:T(8,128)S(1)} %collective-permute-done.3) | copy-start | bytes 442372
  141.6 10.0 %copy-start.8 = (f32[1,32,6,384]{3,0,2,1:T(1,128)}, f32[1,32,6,384]{3,0,2,1:T(1,128)S(1)}, u32[]{:S(2)}) copy-start(f32[1,32,6,384]{3,0,2,1:T(1,128)S(1)} %collective-permute-done) | copy-start | bytes 884740
  141.6 13.1 %copy-start.6 = (f32[1,32,6,384]{3,0,2,1:T(1,128)}, f32[1,32,6,384]{3,0,2,1:T(1,128)S(1)}, u32[]{:S(2)}) copy-start(f32[1,32,6,384]{3,0,2,1:T(1,128)S(1)} %collective-permute-done.1) | copy-start | bytes 884740
  141.6 102.1 %all-to-all-start.1 = ((f32[32,5,16,384]{3,2,1,0:T(8,128)}), f32[32,5,16,384]{3,2,1,0:T(8,128)}, u32[]{:S(2)}, u32[]{:S(2)}) async-start(f32[32,5,16,384]{3,2,1,0:T(8,128)} %copy-done), calls=%async_computation.1 | async-start | bytes 7864320 | tf_op jit(solution)/shard_map/all_to_all | solution.py:92
  151.4 1.1 copy-start.13
  151.4 2.1 copy-start.2
  154.1 0.9 copy-start.11
  155.0 1.0 copy-start.7
  155.0 1.0 copy-start.9
  156.9 2.1 copy-start.3
  156.9 2.1 slice-start
  156.9 2.2 slice-start.1
  156.9 2.2 copy-start.12

commit v6 on v5

--- a/solution.py
+++ b/solution.py
@@ -84,7 +84,6 @@
     packed = jnp.concatenate([state, weight], axis=2)
     send = jnp.transpose(state, (1, 2, 0, 3))
     lines = lax.all_to_all(send, "ax", split_axis=0, concat_axis=0, tiled=True)
-    lines, packed = lax.optimization_barrier((lines, packed))
     ax_halo = halos(packed, "ax", 0)
     rad_halo = halos(packed, "rad", 1)
     res = line_section(lines, mats, jac_axial)

time: 251 us -> 235 us (0.936)
  waiting for transfers between devices: 161 us -> 147 us
  other arithmetic: 21.3 us -> 18.7 us
    all_to_all x1, waiting for transfers between devices: 85.7 us -> 77 us  [body(): lines = lax.all_to_all(send, 'ax', split_axis=0, concat_axis=0, tiled=True)]
    concatenate x1, other arithmetic: 4.9 us -> 0.02 us  [body(): packed = jnp.concatenate([state, weight], axis=2)]
    all_to_all x1, waiting for transfers between devices: 75.1 us -> 70.3 us  [body(): ret = lax.all_to_all(res, 'ax', split_axis=0, concat_axis=0, tiled=True)]
    slice x2 -> x0, local copies, waits for them, and re-layouts: 3.78 us -> none  [halos(): leading = lax.slice_in_dim(x, 0, 1, axis=dim)]
    slice x0 -> x1, other arithmetic: none -> 3.65 us  [halos(): leading = lax.slice_in_dim(x, 0, 1, axis=dim)]
    unnamed x32 -> x30, local copies, waits for them, and re-layouts: 12.2 us -> 12.3 us
  transfers between devices with their start and end apart: 6 -> 6, of which waited for: 2 -> 2; matrix products, arithmetic and copies ran while one was open for 9% -> 10% of each run, Pallas kernels for 7% -> 7%
where the time goes in v6:
time: 235 us
  waiting for transfers between devices  147 us (63%)
  starting transfers between devices  29.5 us (13%)
  local copies, waits for them, and re-layouts  22.4 us (10%)
  other arithmetic  18.7 us (8%)
  Pallas kernels  16.5 us (7%)
    all_to_all x1, waiting for transfers between devices, body(): lines = lax.all_to_all(send, 'ax', split_axis=0, concat_axis=0, tiled=True)  77 us
    all_to_all x1, waiting for transfers between devices, body(): ret = lax.all_to_all(res, 'ax', split_axis=0, concat_axis=0, tiled=True)  70.3 us
    pallas_call x1, Pallas kernels, line_section(): pl.pallas_call(line_kernel, out_shape=jax.ShapeDtypeStruct(lines.shape, l...  16.5 us
    unnamed x30, local copies, waits for them, and re-layouts  12.3 us
    all_to_all x1, starting transfers between devices, body(): lines = lax.all_to_all(send, 'ax', split_axis=0, concat_axis=0, tiled=True)  11.7 us
    ppermute x4, starting transfers between devices, halos(): return (lax.ppermute(last, axis, up), lax.ppermute(leading, axis, down))  10.3 us
    add x1, other arithmetic, stencil(): return viscosity * visc_ax + (mixed + viscosity * visc_rad)  9.49 us
    all_to_all x1, starting transfers between devices, body(): ret = lax.all_to_all(res, 'ax', split_axis=0, concat_axis=0, tiled=True)  7.48 us
  transfers between devices with their start and end apart: 6, of which 2 were waited for; matrix products, arithmetic and copies ran while one was open for 10% of the time, Pallas kernels for 7%

profile of v6, /device:TPU:6, one launch (start us, length us, event | category | flops | bytes accessed | tf_op | source)
XLA Modules:
  0.0 234.7 jit_solution(872705645884297216)
XLA Ops:
  0.0 6.3 %copy.38 = f32[16,32,5,384]{3,0,2,1:T(8,128)} copy(f32[16,32,5,384]{3,1,2,0:T(8,128)} %param.6) | data formatting | bytes 7864320 | tf_op args[0]
  6.3 11.7 %all-to-all-start = ((f32[32,5,16,384]{3,2,1,0:T(8,128)}), f32[32,5,16,384]{3,2,1,0:T(8,128)}, u32[]{:S(2)}, u32[]{:S(2)}) async-start(f32[32,5,16,384]{3,2,1,0:T(8,128)} %bitcast.42), calls=%async_computation | async-start | bytes 7864320 | tf_op jit(solution)/shard_map/all_to_all | solution.py:86
  18.6 3.6 %pad_maximum_fusion.3 = (f32[1,32,6,384]{3,0,2,1:T(1,128)}, f32[1,32,6,384]{3,0,2,1:T(1,128)}) fusion(f32[16,32,1,384]{3,0,2,1:T(8,128)S(1)} %bitcast.43, f32[16,32,5,384]{3,0,2,1:T(8,128)} %copy.38), kind=kLoop, calls=%fused_computation.27 | loop fusion | flops 147456 | bytes 5308416 | tf_op jit(solution)/shard_map/slice | solution.py:19
  22.2 2.8 %collective-permute-start = (f32[1,32,6,384]{3,0,2,1:T(1,128)}, f32[1,32,6,384]{3,0,2,1:T(1,128)}, u32[]{:S(2)}, u32[]{:S(2)}) collective-permute-start(f32[1,32,6,384]{3,0,2,1:T(1,128)} %get-tuple-element.22), channel_id=1, source_target_pairs={{0,8},{8,16},{16,24},{24,32},{32,40},{40,48},{48,56},{56,64},{64,7... | collective-permute-start | bytes 884744 | tf_op jit(solution)/shard_map/ppermute | solution.py:20
  25.1 1.4 collective-permute-start.1
  26.5 2.8 %collective-permute-start.2 = (f32[16,1,6,384]{3,0,2,1:T(8,128)S(1)}, f32[16,1,6,384]{3,0,2,1:T(8,128)}, u32[]{:S(2)}, u32[]{:S(2)}) collective-permute-start(f32[16,1,6,384]{3,0,2,1:T(8,128)S(1)} %get-tuple-element.20), channel_id=1, source_target_pairs={{0,1},{1,2},{2,3},{3,4},{4,5},{5,6},{6,7},{8,9},{9,10},{10,11},{11... | collective-permute-start | bytes 442376 | tf_op jit(solution)/shard_map/ppermute | solution.py:20
  29.4 3.2 %collective-permute-start.3 = (f32[16,1,6,384]{3,0,2,1:T(8,128)S(1)}, f32[16,1,6,384]{3,0,2,1:T(8,128)}, u32[]{:S(2)}, u32[]{:S(2)}) collective-permute-start(f32[16,1,6,384]{3,0,2,1:T(8,128)S(1)} %get-tuple-element.19), channel_id=1, source_target_pairs={{1,0},{2,1},{3,2},{4,3},{5,4},{6,5},{7,6},{9,8},{10,9},{11,10},{12... | collective-permute-start | bytes 442376 | tf_op jit(solution)/shard_map/ppermute | solution.py:20
  32.8 77.0 %all-to-all-done.lines_ref = f32[32,5,16,384]{3,2,1,0:T(8,128)} async-done(((f32[32,5,16,384]{3,2,1,0:T(8,128)}), f32[32,5,16,384]{3,2,1,0:T(8,128)}, u32[]{:S(2)}, u32[]{:S(2)}) %all-to-all-start) | async-done | bytes 3932192 | tf_op jit(solution)/shard_map/all_to_all | solution.py:86
  109.8 16.5 %shard_map.64 = f32[32,5,16,384]{3,2,1,0:T(8,128)S(1)} custom-call(f32[5,5]{1,0:T(8,128)S(1)} %copy-done.1, f32[32,5,16,384]{3,2,1,0:T(8,128)} %all-to-all-done.lines_ref, f32[1024,512]{1,0:T(8,128)S(1)} %pad_maximum_fusion.2.mats_ref), custom_call_target="tpu_custom_call" | custom-call | tf_op jit(solution)/shard_map/pallas_call | solution.py:65
  126.3 1.9 copy-done
  128.2 7.5 %all-to-all-start.1 = ((f32[32,5,16,384]{3,2,1,0:T(8,128)}), f32[32,5,16,384]{3,2,1,0:T(8,128)}, u32[]{:S(2)}, u32[]{:S(2)}) async-start(f32[32,5,16,384]{3,2,1,0:T(8,128)} %copy-done), calls=%async_computation.1 | async-start | bytes 7864320 | tf_op jit(solution)/shard_map/all_to_all | solution.py:91
  136.9 0.9 copy-done.3
  139.0 1.8 slice.102
  140.8 0.9 slice.107
  141.7 0.9 slice.106
  142.6 0.7 subtract_multiply_fusion
  143.4 0.8 slice_bitcast_fusion.9
  144.1 0.8 slice_bitcast_fusion.7
  145.0 0.8 fusion.5
  146.2 1.7 copy-done.4
  148.0 9.5 %fusion.3 = f32[16,32,5,384]{3,0,2,1:T(8,128)} fusion(f32[1,32,5,384]{3,0,2,1:T(1,128)S(1)} %slice-done, f32[15,32,5,384]{3,0,2,1:T(8,128)S(1)} %get-tuple-element.31, f32[15,32,5,384]{3,0,2,1:T(8,128)S(1)} %get-tuple-element.30, f32[1,32,5,384]{3,0,2,1:T(1,128)S(1)} %copy-done.11, f32[16,31,5,384]{3,0,2,1:T(8,128)S(1)} %get-tuple-element.29, ...), kind=kLoop, calls=%fused_computation.4 | loop fusion | flops 26542080 | bytes 30670948 | tf_op jit(solution)/shard_map/add | solution.py:42
  157.5 70.3 %all-to-all-done.1 = f32[32,5,16,384]{3,2,1,0:T(8,128)} async-done(((f32[32,5,16,384]{3,2,1,0:T(8,128)}), f32[32,5,16,384]{3,2,1,0:T(8,128)}, u32[]{:S(2)}, u32[]{:S(2)}) %all-to-all-start.1) | async-done | bytes 3932192 | tf_op jit(solution)/shard_map/all_to_all | solution.py:91
  227.8 3.8 %bitcast_add_fusion = f32[16,32,5,384]{3,0,2,1:T(8,128)S(1)} fusion(f32[32,5,16,384]{3,2,1,0:T(8,128)} %all-to-all-done.1, f32[16,32,5,384]{3,0,2,1:T(8,128)} %fusion.3), kind=kLoop, calls=%fused_computation.9 | loop fusion | flops 1966080 | bytes 11796480 | tf_op jit(solution)/shard_map/add | solution.py:94
  231.6 3.1 %copy.25 = f32[16,32,5,384]{3,1,2,0:T(8,128)} copy(f32[16,32,5,384]{3,0,2,1:T(8,128)S(1)} %bitcast_add_fusion) | data formatting | bytes 7864320 | tf_op jit(solution)/shard_map/add | solution.py:94
  (41 shorter events, 3.4 us)
Async XLA Ops:
  6.3 11.7 %copy-start.5 = (f32[16,32,384]{2,1,0:T(8,128)S(1)}, f32[16,32,384]{2,1,0:T(8,128)}, u32[]{:S(2)}) copy-start(f32[16,32,384]{2,1,0:T(8,128)} %param.7) | copy-start | bytes 2359300
  6.3 103.5 %all-to-all-start = ((f32[32,5,16,384]{3,2,1,0:T(8,128)}), f32[32,5,16,384]{3,2,1,0:T(8,128)}, u32[]{:S(2)}, u32[]{:S(2)}) async-start(f32[32,5,16,384]{3,2,1,0:T(8,128)} %bitcast.42), calls=%async_computation | async-start | bytes 7864320 | tf_op jit(solution)/shard_map/all_to_all | solution.py:86
  18.1 8.4 %copy-start.2 = (f32[16,32,5,384]{3,0,2,1:T(8,128)S(1)}, f32[16,32,5,384]{3,0,2,1:T(8,128)}, u32[]{:S(2)}) copy-start(f32[16,32,5,384]{3,0,2,1:T(8,128)} %copy.38) | copy-start | bytes 11796484
  18.5 14.0 %copy-start.7 = (f32[512,512]{1,0:T(8,128)S(1)}, f32[512,512]{1,0:T(8,128)}, u32[]{:S(2)}) copy-start(f32[512,512]{1,0:T(8,128)} %param.8) | copy-start | bytes 3145732
  18.6 14.0 %copy-start.8 = (f32[512,512]{1,0:T(8,128)S(1)}, f32[512,512]{1,0:T(8,128)}, u32[]{:S(2)}) copy-start(f32[512,512]{1,0:T(8,128)} %param.9) | copy-start | bytes 3145732
  22.2 106.0 %collective-permute-start = (f32[1,32,6,384]{3,0,2,1:T(1,128)}, f32[1,32,6,384]{3,0,2,1:T(1,128)}, u32[]{:S(2)}, u32[]{:S(2)}) collective-permute-start(f32[1,32,6,384]{3,0,2,1:T(1,128)} %get-tuple-element.22), channel_id=1, source_target_pairs={{0,8},{8,16},{16,24},{24,32},{32,40},{40,48},{48,56},{56,64},{64,7... | collective-permute-start | bytes 884744 | tf_op jit(solution)/shard_map/ppermute | solution.py:20
  25.1 84.7 %copy-start.1 = (f32[5,5]{1,0:T(8,128)S(1)}, f32[5,5]{1,0:T(8,128)}, u32[]{:S(2)}) copy-start(f32[5,5]{1,0:T(8,128)} %jac_ref.1) | copy-start | bytes 304
  25.1 103.1 %collective-permute-start.1 = (f32[1,32,6,384]{3,0,2,1:T(1,128)}, f32[1,32,6,384]{3,0,2,1:T(1,128)S(1)}, u32[]{:S(2)}, u32[]{:S(2)}) collective-permute-start(f32[1,32,6,384]{3,0,2,1:T(1,128)} %get-tuple-element.21), channel_id=1, source_target_pairs={{8,0},{16,8},{24,16},{32,24},{40,32},{48,40},{56,48},{64,56},{72,6... | collective-permute-start | bytes 884744 | tf_op jit(solution)/shard_map/ppermute | solution.py:20
  26.5 101.7 %collective-permute-start.2 = (f32[16,1,6,384]{3,0,2,1:T(8,128)S(1)}, f32[16,1,6,384]{3,0,2,1:T(8,128)}, u32[]{:S(2)}, u32[]{:S(2)}) collective-permute-start(f32[16,1,6,384]{3,0,2,1:T(8,128)S(1)} %get-tuple-element.20), channel_id=1, source_target_pairs={{0,1},{1,2},{2,3},{3,4},{4,5},{5,6},{6,7},{8,9},{9,10},{10,11},{11... | collective-permute-start | bytes 442376 | tf_op jit(solution)/shard_map/ppermute | solution.py:20
  29.4 98.8 %collective-permute-start.3 = (f32[16,1,6,384]{3,0,2,1:T(8,128)S(1)}, f32[16,1,6,384]{3,0,2,1:T(8,128)}, u32[]{:S(2)}, u32[]{:S(2)}) collective-permute-start(f32[16,1,6,384]{3,0,2,1:T(8,128)S(1)} %get-tuple-element.19), channel_id=1, source_target_pairs={{1,0},{2,1},{3,2},{4,3},{5,4},{6,5},{7,6},{9,8},{10,9},{11,10},{12... | collective-permute-start | bytes 442376 | tf_op jit(solution)/shard_map/ppermute | solution.py:20
  126.3 1.9 copy-start
  128.2 7.5 %copy-start.6 = (f32[16,32,384]{2,1,0:T(8,128)S(1)}, f32[16,32,384]{2,1,0:T(8,128)}, u32[]{:S(2)}) copy-start(f32[16,32,384]{2,1,0:T(8,128)} %param.7) | copy-start | bytes 2359300
  128.2 10.8 %copy-start.9 = (f32[1,32,6,384]{3,0,2,1:T(1,128)}, f32[1,32,6,384]{3,0,2,1:T(1,128)S(1)}, u32[]{:S(2)}) copy-start(f32[1,32,6,384]{3,0,2,1:T(1,128)S(1)} %collective-permute-done.1) | copy-start | bytes 884740
  128.2 99.5 %all-to-all-start.1 = ((f32[32,5,16,384]{3,2,1,0:T(8,128)}), f32[32,5,16,384]{3,2,1,0:T(8,128)}, u32[]{:S(2)}, u32[]{:S(2)}) async-start(f32[32,5,16,384]{3,2,1,0:T(8,128)} %copy-done), calls=%async_computation.1 | async-start | bytes 7864320 | tf_op jit(solution)/shard_map/all_to_all | solution.py:91
  135.7 1.1 copy-start.12
  135.7 2.1 copy-start.3
  142.6 1.5 copy-start.10
  145.8 2.1 copy-start.4
  145.8 2.1 slice-start
  145.8 2.2 copy-start.11

commit v7 on v6

--- a/solution.py
+++ b/solution.py
@@ -42,14 +42,22 @@
     return viscosity * visc_ax + (mixed + viscosity * visc_rad)
 
 
+def split_bf16(x):
+    t = x * 65537.0
+    hi = t - (t - x)
+    return hi.astype(jnp.bfloat16), (x - hi).astype(jnp.bfloat16)
+
+
 def line_kernel(jac_ref, lines_ref, mats_ref, out_ref):
     S, V, XL, C = lines_ref.shape
     nx = S * XL
     cols = [lines_ref[:, v, :, :].reshape(nx, C) for v in range(V)]
     wide = jnp.concatenate(cols, axis=1)
-    prod = jnp.dot(
-        mats_ref[...], wide, precision=lax.Precision.HIGHEST, preferred_element_type=jnp.float32
-    )
+    w_hi, w_lo = split_bf16(wide)
+    m_hi, m_lo = split_bf16(mats_ref[...])
+    prod = jnp.dot(m_hi, w_hi, preferred_element_type=jnp.float32)
+    prod = prod + jnp.dot(m_hi, w_lo, preferred_element_type=jnp.float32)
+    prod = prod + jnp.dot(m_lo, w_hi, preferred_element_type=jnp.float32)
     smooth = prod[:nx]
     slope = prod[nx:]
     for v in range(V):
@@ -61,16 +69,16 @@
 
 
 def line_section(lines, mats, jac_axial):
-    S, V, XL, C = lines.shape
+    S, V, XL, A = lines.shape
+    C = 128 if A % 128 == 0 else A
+    block = pl.BlockSpec((S, V, XL, C), lambda i: (0, 0, 0, i))
+    whole = pl.BlockSpec(mats.shape, lambda i: (0, 0))
     return pl.pallas_call(
         line_kernel,
         out_shape=jax.ShapeDtypeStruct(lines.shape, lines.dtype),
-        in_specs=[
-            pl.BlockSpec(memory_space=pltpu.SMEM),
-            pl.BlockSpec(memory_space=pltpu.VMEM),
-            pl.BlockSpec(memory_space=pltpu.VMEM),
-        ],
-        out_specs=pl.BlockSpec(memory_space=pltpu.VMEM),
+        grid=(A // C,),
+        in_specs=[pl.BlockSpec(memory_space=pltpu.SMEM), block, whole],
+        out_specs=block,
         compiler_params=pltpu.CompilerParams(vmem_limit_bytes=48 * 1024 * 1024),
     )(jac_axial, lines, mats)
 

time: 235 us -> 230 us (0.979)
  Pallas kernels: 16.5 us -> 10.8 us
    pallas_call x1, Pallas kernels: 16.5 us -> 10.8 us  [line_section(): pl.pallas_call(line_kernel, out_shape=jax.ShapeDtypeStruct(lines.shape, l...]
  transfers between devices with their start and end apart: 6 -> 6, of which waited for: 2 -> 2; matrix products, arithmetic and copies ran while one was open for 10% -> 10% of each run, Pallas kernels for 7% -> 5%
where the time goes in v7:
time: 230 us; the launch traced here: 229 us
  waiting for transfers between devices  147 us (64%)
  starting transfers between devices  29.5 us (13%)
  local copies, waits for them, and re-layouts  22.4 us (10%)
  other arithmetic  18.7 us (8%)
  Pallas kernels  10.8 us (5%)
    all_to_all x1, waiting for transfers between devices, body(): lines = lax.all_to_all(send, 'ax', split_axis=0, concat_axis=0, tiled=True)  77.2 us
    all_to_all x1, waiting for transfers between devices, body(): ret = lax.all_to_all(res, 'ax', split_axis=0, concat_axis=0, tiled=True)  70.1 us
    unnamed x30, local copies, waits for them, and re-layouts  12.3 us
    all_to_all x1, starting transfers between devices, body(): lines = lax.all_to_all(send, 'ax', split_axis=0, concat_axis=0, tiled=True)  11.7 us
    pallas_call x1, Pallas kernels, line_section(): pl.pallas_call(line_kernel, out_shape=jax.ShapeDtypeStruct(lines.shape, l...  10.8 us
    ppermute x4, starting transfers between devices, halos(): return (lax.ppermute(last, axis, up), lax.ppermute(leading, axis, down))  10.1 us
    add x1, other arithmetic, stencil(): return viscosity * visc_ax + (mixed + viscosity * visc_rad)  9.49 us
    all_to_all x1, starting transfers between devices, body(): ret = lax.all_to_all(res, 'ax', split_axis=0, concat_axis=0, tiled=True)  7.66 us
  transfers between devices with their start and end apart: 6, of which 2 were waited for; matrix products, arithmetic and copies ran while one was open for 10% of the time, Pallas kernels for 5%

profile of v7, /device:TPU:6, one launch (start us, length us, event | category | flops | bytes accessed | tf_op | source)
XLA Modules:
  0.0 229.0 jit_solution(4512326767540036526)
XLA Ops:
  0.0 6.3 %copy.38 = f32[16,32,5,384]{3,0,2,1:T(8,128)} copy(f32[16,32,5,384]{3,1,2,0:T(8,128)} %param.6) | data formatting | bytes 7864320 | tf_op args[0]
  6.3 11.7 %all-to-all-start = ((f32[32,5,16,384]{3,2,1,0:T(8,128)}), f32[32,5,16,384]{3,2,1,0:T(8,128)}, u32[]{:S(2)}, u32[]{:S(2)}) async-start(f32[32,5,16,384]{3,2,1,0:T(8,128)} %bitcast.42), calls=%async_computation | async-start | bytes 7864320 | tf_op jit(solution)/shard_map/all_to_all | solution.py:94
  18.6 3.6 %pad_maximum_fusion.3 = (f32[1,32,6,384]{3,0,2,1:T(1,128)}, f32[1,32,6,384]{3,0,2,1:T(1,128)}) fusion(f32[16,32,1,384]{3,0,2,1:T(8,128)S(1)} %bitcast.43, f32[16,32,5,384]{3,0,2,1:T(8,128)} %copy.38), kind=kLoop, calls=%fused_computation.27 | loop fusion | flops 147456 | bytes 5308416 | tf_op jit(solution)/shard_map/slice | solution.py:19
  22.2 2.8 %collective-permute-start = (f32[1,32,6,384]{3,0,2,1:T(1,128)}, f32[1,32,6,384]{3,0,2,1:T(1,128)}, u32[]{:S(2)}, u32[]{:S(2)}) collective-permute-start(f32[1,32,6,384]{3,0,2,1:T(1,128)} %get-tuple-element.22), channel_id=1, source_target_pairs={{0,8},{8,16},{16,24},{24,32},{32,40},{40,48},{48,56},{56,64},{64,7... | collective-permute-start | bytes 884744 | tf_op jit(solution)/shard_map/ppermute | solution.py:20
  25.1 1.4 collective-permute-start.1
  26.5 2.8 %collective-permute-start.2 = (f32[16,1,6,384]{3,0,2,1:T(8,128)S(1)}, f32[16,1,6,384]{3,0,2,1:T(8,128)}, u32[]{:S(2)}, u32[]{:S(2)}) collective-permute-start(f32[16,1,6,384]{3,0,2,1:T(8,128)S(1)} %get-tuple-element.20), channel_id=1, source_target_pairs={{0,1},{1,2},{2,3},{3,4},{4,5},{5,6},{6,7},{8,9},{9,10},{10,11},{11... | collective-permute-start | bytes 442376 | tf_op jit(solution)/shard_map/ppermute | solution.py:20
  29.4 3.0 %collective-permute-start.3 = (f32[16,1,6,384]{3,0,2,1:T(8,128)S(1)}, f32[16,1,6,384]{3,0,2,1:T(8,128)}, u32[]{:S(2)}, u32[]{:S(2)}) collective-permute-start(f32[16,1,6,384]{3,0,2,1:T(8,128)S(1)} %get-tuple-element.19), channel_id=1, source_target_pairs={{1,0},{2,1},{3,2},{4,3},{5,4},{6,5},{7,6},{9,8},{10,9},{11,10},{12... | collective-permute-start | bytes 442376 | tf_op jit(solution)/shard_map/ppermute | solution.py:20
  32.6 77.2 %all-to-all-done.lines_ref = f32[32,5,16,384]{3,2,1,0:T(8,128)} async-done(((f32[32,5,16,384]{3,2,1,0:T(8,128)}), f32[32,5,16,384]{3,2,1,0:T(8,128)}, u32[]{:S(2)}, u32[]{:S(2)}) %all-to-all-start) | async-done | bytes 3932192 | tf_op jit(solution)/shard_map/all_to_all | solution.py:94
  109.8 10.8 %shard_map.64 = f32[32,5,16,384]{3,2,1,0:T(8,128)S(1)} custom-call(f32[5,5]{1,0:T(8,128)S(1)} %copy-done.1, f32[32,5,16,384]{3,2,1,0:T(8,128)} %all-to-all-done.lines_ref, f32[1024,512]{1,0:T(8,128)S(1)} %pad_maximum_fusion.2.mats_ref), custom_call_target="tpu_custom_call" | custom-call | tf_op jit(solution)/shard_map/pallas_call | solution.py:76
  120.6 1.9 copy-done
  122.5 7.7 %all-to-all-start.1 = ((f32[32,5,16,384]{3,2,1,0:T(8,128)}), f32[32,5,16,384]{3,2,1,0:T(8,128)}, u32[]{:S(2)}, u32[]{:S(2)}) async-start(f32[32,5,16,384]{3,2,1,0:T(8,128)} %copy-done), calls=%async_computation.1 | async-start | bytes 7864320 | tf_op jit(solution)/shard_map/all_to_all | solution.py:99
  131.4 0.9 copy-done.3
  133.5 1.8 slice.102
  135.3 0.9 slice.107
  136.2 0.9 slice.106
  137.1 0.7 subtract_multiply_fusion
  137.9 0.8 slice_bitcast_fusion.9
  138.6 0.8 slice_bitcast_fusion.7
  139.5 0.8 fusion.5
  140.7 1.7 copy-done.4
  142.5 9.5 %fusion.3 = f32[16,32,5,384]{3,0,2,1:T(8,128)} fusion(f32[1,32,5,384]{3,0,2,1:T(1,128)S(1)} %slice-done, f32[15,32,5,384]{3,0,2,1:T(8,128)S(1)} %get-tuple-element.31, f32[15,32,5,384]{3,0,2,1:T(8,128)S(1)} %get-tuple-element.30, f32[1,32,5,384]{3,0,2,1:T(1,128)S(1)} %copy-done.11, f32[16,31,5,384]{3,0,2,1:T(8,128)S(1)} %get-tuple-element.29, ...), kind=kLoop, calls=%fused_computation.4 | loop fusion | flops 26542080 | bytes 30670948 | tf_op jit(solution)/shard_map/add | solution.py:42
  152.0 70.1 %all-to-all-done.1 = f32[32,5,16,384]{3,2,1,0:T(8,128)} async-done(((f32[32,5,16,384]{3,2,1,0:T(8,128)}), f32[32,5,16,384]{3,2,1,0:T(8,128)}, u32[]{:S(2)}, u32[]{:S(2)}) %all-to-all-start.1) | async-done | bytes 3932192 | tf_op jit(solution)/shard_map/all_to_all | solution.py:99
  222.1 3.8 %bitcast_add_fusion = f32[16,32,5,384]{3,0,2,1:T(8,128)S(1)} fusion(f32[32,5,16,384]{3,2,1,0:T(8,128)} %all-to-all-done.1, f32[16,32,5,384]{3,0,2,1:T(8,128)} %fusion.3), kind=kLoop, calls=%fused_computation.9 | loop fusion | flops 1966080 | bytes 11796480 | tf_op jit(solution)/shard_map/add | solution.py:102
  225.9 3.1 %copy.25 = f32[16,32,5,384]{3,1,2,0:T(8,128)} copy(f32[16,32,5,384]{3,0,2,1:T(8,128)S(1)} %bitcast_add_fusion) | data formatting | bytes 7864320 | tf_op jit(solution)/shard_map/add | solution.py:102
  (41 shorter events, 3.4 us)
Async XLA Ops:
  6.3 11.7 %copy-start.5 = (f32[16,32,384]{2,1,0:T(8,128)S(1)}, f32[16,32,384]{2,1,0:T(8,128)}, u32[]{:S(2)}) copy-start(f32[16,32,384]{2,1,0:T(8,128)} %param.7) | copy-start | bytes 2359300
  6.3 103.5 %all-to-all-start = ((f32[32,5,16,384]{3,2,1,0:T(8,128)}), f32[32,5,16,384]{3,2,1,0:T(8,128)}, u32[]{:S(2)}, u32[]{:S(2)}) async-start(f32[32,5,16,384]{3,2,1,0:T(8,128)} %bitcast.42), calls=%async_computation | async-start | bytes 7864320 | tf_op jit(solution)/shard_map/all_to_all | solution.py:94
  18.1 8.4 %copy-start.2 = (f32[16,32,5,384]{3,0,2,1:T(8,128)S(1)}, f32[16,32,5,384]{3,0,2,1:T(8,128)}, u32[]{:S(2)}) copy-start(f32[16,32,5,384]{3,0,2,1:T(8,128)} %copy.38) | copy-start | bytes 11796484
  18.5 13.8 %copy-start.7 = (f32[512,512]{1,0:T(8,128)S(1)}, f32[512,512]{1,0:T(8,128)}, u32[]{:S(2)}) copy-start(f32[512,512]{1,0:T(8,128)} %param.8) | copy-start | bytes 3145732
  18.6 13.8 %copy-start.8 = (f32[512,512]{1,0:T(8,128)S(1)}, f32[512,512]{1,0:T(8,128)}, u32[]{:S(2)}) copy-start(f32[512,512]{1,0:T(8,128)} %param.9) | copy-start | bytes 3145732
  22.2 100.3 %collective-permute-start = (f32[1,32,6,384]{3,0,2,1:T(1,128)}, f32[1,32,6,384]{3,0,2,1:T(1,128)}, u32[]{:S(2)}, u32[]{:S(2)}) collective-permute-start(f32[1,32,6,384]{3,0,2,1:T(1,128)} %get-tuple-element.22), channel_id=1, source_target_pairs={{0,8},{8,16},{16,24},{24,32},{32,40},{40,48},{48,56},{56,64},{64,7... | collective-permute-start | bytes 884744 | tf_op jit(solution)/shard_map/ppermute | solution.py:20
  25.1 84.7 %copy-start.1 = (f32[5,5]{1,0:T(8,128)S(1)}, f32[5,5]{1,0:T(8,128)}, u32[]{:S(2)}) copy-start(f32[5,5]{1,0:T(8,128)} %jac_ref.1) | copy-start | bytes 304
  25.1 97.5 %collective-permute-start.1 = (f32[1,32,6,384]{3,0,2,1:T(1,128)}, f32[1,32,6,384]{3,0,2,1:T(1,128)S(1)}, u32[]{:S(2)}, u32[]{:S(2)}) collective-permute-start(f32[1,32,6,384]{3,0,2,1:T(1,128)} %get-tuple-element.21), channel_id=1, source_target_pairs={{8,0},{16,8},{24,16},{32,24},{40,32},{48,40},{56,48},{64,56},{72,6... | collective-permute-start | bytes 884744 | tf_op jit(solution)/shard_map/ppermute | solution.py:20
  26.5 96.0 %collective-permute-start.2 = (f32[16,1,6,384]{3,0,2,1:T(8,128)S(1)}, f32[16,1,6,384]{3,0,2,1:T(8,128)}, u32[]{:S(2)}, u32[]{:S(2)}) collective-permute-start(f32[16,1,6,384]{3,0,2,1:T(8,128)S(1)} %get-tuple-element.20), channel_id=1, source_target_pairs={{0,1},{1,2},{2,3},{3,4},{4,5},{5,6},{6,7},{8,9},{9,10},{10,11},{11... | collective-permute-start | bytes 442376 | tf_op jit(solution)/shard_map/ppermute | solution.py:20
  29.4 93.1 %collective-permute-start.3 = (f32[16,1,6,384]{3,0,2,1:T(8,128)S(1)}, f32[16,1,6,384]{3,0,2,1:T(8,128)}, u32[]{:S(2)}, u32[]{:S(2)}) collective-permute-start(f32[16,1,6,384]{3,0,2,1:T(8,128)S(1)} %get-tuple-element.19), channel_id=1, source_target_pairs={{1,0},{2,1},{3,2},{4,3},{5,4},{6,5},{7,6},{9,8},{10,9},{11,10},{12... | collective-permute-start | bytes 442376 | tf_op jit(solution)/shard_map/ppermute | solution.py:20
  120.6 1.9 copy-start
  122.5 7.7 %copy-start.6 = (f32[16,32,384]{2,1,0:T(8,128)S(1)}, f32[16,32,384]{2,1,0:T(8,128)}, u32[]{:S(2)}) copy-start(f32[16,32,384]{2,1,0:T(8,128)} %param.7) | copy-start | bytes 2359300
  122.5 10.9 %copy-start.9 = (f32[1,32,6,384]{3,0,2,1:T(1,128)}, f32[1,32,6,384]{3,0,2,1:T(1,128)S(1)}, u32[]{:S(2)}) copy-start(f32[1,32,6,384]{3,0,2,1:T(1,128)S(1)} %collective-permute-done.1) | copy-start | bytes 884740
  122.5 99.5 %all-to-all-start.1 = ((f32[32,5,16,384]{3,2,1,0:T(8,128)}), f32[32,5,16,384]{3,2,1,0:T(8,128)}, u32[]{:S(2)}, u32[]{:S(2)}) async-start(f32[32,5,16,384]{3,2,1,0:T(8,128)} %copy-done), calls=%async_computation.1 | async-start | bytes 7864320 | tf_op jit(solution)/shard_map/all_to_all | solution.py:99
  130.2 1.1 copy-start.12
  130.2 2.1 copy-start.3
  137.1 1.5 copy-start.10
  140.3 2.1 copy-start.4
  140.3 2.1 slice-start
  140.3 2.2 copy-start.11

commit v8 on v7

--- a/solution.py
+++ b/solution.py
@@ -5,6 +5,7 @@
 from jax import lax
 from jax.experimental import pallas as pl
 from jax.experimental.pallas import tpu as pltpu
+from jax.experimental.layout import Layout, with_layout_constraint
 from jax.sharding import PartitionSpec as P
 
 section_step = 0.25
@@ -98,6 +99,7 @@
     res, ax_halo, rad_halo = lax.optimization_barrier((res, ax_halo, rad_halo))
     ret = lax.all_to_all(res, "ax", split_axis=0, concat_axis=0, tiled=True)
     local = stencil(state, weight, ax_halo, rad_halo, jac_radial)
+    local = with_layout_constraint(local, Layout(major_to_minor=(0, 2, 1, 3)))
     ret, local = lax.optimization_barrier((ret, local))
     return jnp.transpose(ret, (2, 0, 1, 3)) + section_step * local
 

time: 230 us -> 229 us (level)
  waiting for transfers between devices: 147 us -> 155 us
  local copies, waits for them, and re-layouts: 22.4 us -> 16 us
    all_to_all x1, waiting for transfers between devices: 70.1 us -> 76.3 us  [body(): ret = lax.all_to_all(res, 'ax', split_axis=0, concat_axis=0, tiled=True)]
    add x1, other arithmetic: 9.49 us -> 6.22 us  [stencil(): return viscosity * visc_ax + (mixed + viscosity * visc_rad)]
    add x1 -> x0, local copies, waits for them, and re-layouts: 3.12 us -> none  [body(): return jnp.transpose(ret, (2, 0, 1, 3)) + section_step * local]
    add x1, other arithmetic: 3.81 us -> 6.63 us  [body(): return jnp.transpose(ret, (2, 0, 1, 3)) + section_step * local]
    unnamed x30 -> x21, local copies, waits for them, and re-layouts: 12.3 us -> 10.1 us
  transfers between devices with their start and end apart: 6 -> 6, of which waited for: 2 -> 2; matrix products, arithmetic and copies ran while one was open for 10% -> 7% of each run, Pallas kernels for 5% -> 5%
where the time goes in v8:
time: 229 us
  waiting for transfers between devices  155 us (68%)
  starting transfers between devices  28.6 us (12%)
  other arithmetic  17.5 us (8%)
  local copies, waits for them, and re-layouts  16 us (7%)
  Pallas kernels  10.8 us (5%)
    all_to_all x1, waiting for transfers between devices, body(): lines = lax.all_to_all(send, 'ax', split_axis=0, concat_axis=0, tiled=True)  79.1 us
    all_to_all x1, waiting for transfers between devices, body(): ret = lax.all_to_all(res, 'ax', split_axis=0, concat_axis=0, tiled=True)  76.3 us
    all_to_all x1, starting transfers between devices, body(): lines = lax.all_to_all(send, 'ax', split_axis=0, concat_axis=0, tiled=True)  11.7 us
    pallas_call x1, Pallas kernels, line_section(): pl.pallas_call(line_kernel, out_shape=jax.ShapeDtypeStruct(lines.shape, l...  10.8 us
    unnamed x21, local copies, waits for them, and re-layouts  10.1 us
    ppermute x4, starting transfers between devices, halos(): return (lax.ppermute(last, axis, up), lax.ppermute(leading, axis, down))  9.37 us
    all_to_all x1, starting transfers between devices, body(): ret = lax.all_to_all(res, 'ax', split_axis=0, concat_axis=0, tiled=True)  7.53 us
    add x1, other arithmetic, body(): return jnp.transpose(ret, (2, 0, 1, 3)) + section_step * local  6.63 us
  transfers between devices with their start and end apart: 6, of which 2 were waited for; matrix products, arithmetic and copies ran while one was open for 7% of the time, Pallas kernels for 5%

profile of v8, /device:TPU:6, one launch (start us, length us, event | category | flops | bytes accessed | tf_op | source)
XLA Modules:
  0.0 228.6 jit_solution(5202313527728024478)
XLA Ops:
  0.0 6.3 %copy.19 = f32[16,32,5,384]{3,0,2,1:T(8,128)} copy(f32[16,32,5,384]{3,1,2,0:T(8,128)} %param.6) | data formatting | bytes 7864320 | tf_op args[0]
  6.3 11.7 %all-to-all-start = ((f32[32,5,16,384]{3,2,1,0:T(8,128)}), f32[32,5,16,384]{3,2,1,0:T(8,128)}, u32[]{:S(2)}, u32[]{:S(2)}) async-start(f32[32,5,16,384]{3,2,1,0:T(8,128)} %bitcast.44), calls=%async_computation | async-start | bytes 7864320 | tf_op jit(solution)/shard_map/all_to_all | solution.py:95
  18.1 2.1 pad_maximum_fusion.3
  20.2 2.2 collective-permute-start
  22.4 1.3 collective-permute-start.1
  23.7 0.9 pad_maximum_fusion.5
  24.7 2.8 %collective-permute-start.2 = (f32[16,1,6,384]{3,1,2,0:T(1,128)}, f32[16,1,6,384]{3,1,2,0:T(1,128)}, u32[]{:S(2)}, u32[]{:S(2)}) collective-permute-start(f32[16,1,6,384]{3,1,2,0:T(1,128)} %get-tuple-element.20), channel_id=1, source_target_pairs={{0,1},{1,2},{2,3},{3,4},{4,5},{5,6},{6,7},{8,9},{9,10},{10,11},{11... | collective-permute-start | bytes 442376 | tf_op jit(solution)/shard_map/ppermute | solution.py:21
  27.5 3.0 %collective-permute-start.3 = (f32[16,1,6,384]{3,1,2,0:T(1,128)}, f32[16,1,6,384]{3,1,2,0:T(1,128)}, u32[]{:S(2)}, u32[]{:S(2)}) collective-permute-start(f32[16,1,6,384]{3,1,2,0:T(1,128)} %get-tuple-element.19), channel_id=1, source_target_pairs={{1,0},{2,1},{3,2},{4,3},{5,4},{6,5},{7,6},{9,8},{10,9},{11,10},{12... | collective-permute-start | bytes 442376 | tf_op jit(solution)/shard_map/ppermute | solution.py:21
  30.7 79.1 %all-to-all-done.lines_ref = f32[32,5,16,384]{3,2,1,0:T(8,128)} async-done(((f32[32,5,16,384]{3,2,1,0:T(8,128)}), f32[32,5,16,384]{3,2,1,0:T(8,128)}, u32[]{:S(2)}, u32[]{:S(2)}) %all-to-all-start) | async-done | bytes 3932192 | tf_op jit(solution)/shard_map/all_to_all | solution.py:95
  109.8 10.8 %shard_map.64 = f32[32,5,16,384]{3,2,1,0:T(8,128)S(1)} custom-call(f32[5,5]{1,0:T(8,128)S(1)} %copy-done.1, f32[32,5,16,384]{3,2,1,0:T(8,128)} %all-to-all-done.lines_ref, f32[1024,512]{1,0:T(8,128)S(1)} %pad_maximum_fusion.2.mats_ref), custom_call_target="tpu_custom_call" | custom-call | tf_op jit(solution)/shard_map/pallas_call | solution.py:77
  120.6 1.9 copy-done
  122.6 7.5 %all-to-all-start.1 = ((f32[32,5,16,384]{3,2,1,0:T(8,128)}), f32[32,5,16,384]{3,2,1,0:T(8,128)}, u32[]{:S(2)}, u32[]{:S(2)}) async-start(f32[32,5,16,384]{3,2,1,0:T(8,128)} %copy-done), calls=%async_computation.1 | async-start | bytes 7864320 | tf_op jit(solution)/shard_map/all_to_all | solution.py:100
  130.5 1.8 copy-done.3
  132.3 1.0 fusion.10
  133.3 0.8 fusion.9
  134.1 1.0 slice.107
  135.1 1.0 slice.106
  136.1 1.1 subtract_multiply_fusion
  137.1 0.8 slice_bitcast_fusion.9
  137.9 0.5 fusion.5
  138.8 0.6 slice-done
  139.5 6.2 %fusion.3 = f32[16,32,5,384]{3,1,2,0:T(8,128)} fusion(f32[16,32,5,384]{3,1,2,0:T(8,128)S(1)} %copy-done.3, f32[1,32,5,384]{3,1,2,0:T(8,128)S(1)} %slice-done, f32[15,32,5,384]{3,1,2,0:T(8,128)S(1)} %get-tuple-element.31, f32[15,32,5,384]{3,1,2,0:T(8,128)S(1)} %get-tuple-element.30, f32[1,32,5,384]{3,1,2,0:T(8,128)S(1)} %slice-done.1, ...), kind=kLoop, calls=%fused_computation.4 | loop fusion | flops 26542080 | bytes 30670948 | tf_op jit(solution)/shard_map/add | solution.py:43
  145.7 76.3 %all-to-all-done.1 = f32[32,5,16,384]{3,2,1,0:T(8,128)} async-done(((f32[32,5,16,384]{3,2,1,0:T(8,128)}), f32[32,5,16,384]{3,2,1,0:T(8,128)}, u32[]{:S(2)}, u32[]{:S(2)}) %all-to-all-start.1) | async-done | bytes 3932192 | tf_op jit(solution)/shard_map/all_to_all | solution.py:100
  222.0 6.6 %bitcast_add_fusion = f32[16,32,5,384]{3,1,2,0:T(8,128)} fusion(f32[32,5,16,384]{3,2,1,0:T(8,128)} %all-to-all-done.1, f32[16,32,5,384]{3,1,2,0:T(8,128)} %fusion.3), kind=kLoop, calls=%fused_computation.9 | loop fusion | flops 1966080 | bytes 11796480 | tf_op jit(solution)/shard_map/add | solution.py:104
  (32 shorter events, 1.0 us)
Async XLA Ops:
  6.3 11.8 %copy-start.4 = (f32[16,32,384]{2,1,0:T(8,128)S(1)}, f32[16,32,384]{2,1,0:T(8,128)}, u32[]{:S(2)}) copy-start(f32[16,32,384]{2,1,0:T(8,128)} %param.7) | copy-start | bytes 2359300
  6.3 103.5 %all-to-all-start = ((f32[32,5,16,384]{3,2,1,0:T(8,128)}), f32[32,5,16,384]{3,2,1,0:T(8,128)}, u32[]{:S(2)}, u32[]{:S(2)}) async-start(f32[32,5,16,384]{3,2,1,0:T(8,128)} %bitcast.44), calls=%async_computation | async-start | bytes 7864320 | tf_op jit(solution)/shard_map/all_to_all | solution.py:95
  18.1 5.7 %copy-start.2 = (f32[16,32,5,384]{3,1,2,0:T(8,128)S(1)}, f32[16,32,5,384]{3,1,2,0:T(8,128)}, u32[]{:S(2)}) copy-start(f32[16,32,5,384]{3,1,2,0:T(8,128)} %param.6) | copy-start | bytes 11796484
  18.1 12.4 %copy-start.5 = (f32[512,512]{1,0:T(8,128)S(1)}, f32[512,512]{1,0:T(8,128)}, u32[]{:S(2)}) copy-start(f32[512,512]{1,0:T(8,128)} %param.8) | copy-start | bytes 3145732
  18.1 12.4 %copy-start.6 = (f32[512,512]{1,0:T(8,128)S(1)}, f32[512,512]{1,0:T(8,128)}, u32[]{:S(2)}) copy-start(f32[512,512]{1,0:T(8,128)} %param.9) | copy-start | bytes 3145732
  20.2 102.4 %collective-permute-start = (f32[1,32,6,384]{3,1,2,0:T(8,128)}, f32[1,32,6,384]{3,1,2,0:T(8,128)S(1)}, u32[]{:S(2)}, u32[]{:S(2)}) collective-permute-start(f32[1,32,6,384]{3,1,2,0:T(8,128)} %get-tuple-element.22), channel_id=1, source_target_pairs={{0,8},{8,16},{16,24},{24,32},{32,40},{40,48},{48,56},{56,64},{64,7... | collective-permute-start | bytes 884744 | tf_op jit(solution)/shard_map/ppermute | solution.py:21
  22.4 87.4 %copy-start.1 = (f32[5,5]{1,0:T(8,128)S(1)}, f32[5,5]{1,0:T(8,128)}, u32[]{:S(2)}) copy-start(f32[5,5]{1,0:T(8,128)} %jac_ref.1) | copy-start | bytes 304
  22.4 100.1 %collective-permute-start.1 = (f32[1,32,6,384]{3,1,2,0:T(8,128)}, f32[1,32,6,384]{3,1,2,0:T(8,128)S(1)}, u32[]{:S(2)}, u32[]{:S(2)}) collective-permute-start(f32[1,32,6,384]{3,1,2,0:T(8,128)} %get-tuple-element.21), channel_id=1, source_target_pairs={{8,0},{16,8},{24,16},{32,24},{40,32},{48,40},{56,48},{64,56},{72,6... | collective-permute-start | bytes 884744 | tf_op jit(solution)/shard_map/ppermute | solution.py:21
  24.7 97.9 %collective-permute-start.2 = (f32[16,1,6,384]{3,1,2,0:T(1,128)}, f32[16,1,6,384]{3,1,2,0:T(1,128)}, u32[]{:S(2)}, u32[]{:S(2)}) collective-permute-start(f32[16,1,6,384]{3,1,2,0:T(1,128)} %get-tuple-element.20), channel_id=1, source_target_pairs={{0,1},{1,2},{2,3},{3,4},{4,5},{5,6},{6,7},{8,9},{9,10},{10,11},{11... | collective-permute-start | bytes 442376 | tf_op jit(solution)/shard_map/ppermute | solution.py:21
  27.5 95.0 %collective-permute-start.3 = (f32[16,1,6,384]{3,1,2,0:T(1,128)}, f32[16,1,6,384]{3,1,2,0:T(1,128)}, u32[]{:S(2)}, u32[]{:S(2)}) collective-permute-start(f32[16,1,6,384]{3,1,2,0:T(1,128)} %get-tuple-element.19), channel_id=1, source_target_pairs={{1,0},{2,1},{3,2},{4,3},{5,4},{6,5},{7,6},{9,8},{10,9},{11,10},{12... | collective-permute-start | bytes 442376 | tf_op jit(solution)/shard_map/ppermute | solution.py:21
  120.6 1.9 copy-start
  122.5 7.6 %copy-start.9 = (f32[5,5]{1,0:T(8,128)S(1)}, f32[5,5]{1,0:T(8,128)}, u32[]{:S(2)}) copy-start(f32[5,5]{1,0:T(8,128)} %param.11) | copy-start | bytes 304
  122.6 15.3 %copy-start.8 = (f32[1,32,6,384]{3,1,2,0:T(8,128)}, f32[1,32,6,384]{3,1,2,0:T(8,128)S(1)}, u32[]{:S(2)}) copy-start(f32[1,32,6,384]{3,1,2,0:T(8,128)S(1)} %collective-permute-done) | copy-start | bytes 884740
  122.6 15.3 %copy-start.7 = (f32[1,32,6,384]{3,1,2,0:T(8,128)}, f32[1,32,6,384]{3,1,2,0:T(8,128)S(1)}, u32[]{:S(2)}) copy-start(f32[1,32,6,384]{3,1,2,0:T(8,128)S(1)} %collective-permute-done.1) | copy-start | bytes 884740
  122.6 99.4 %all-to-all-start.1 = ((f32[32,5,16,384]{3,2,1,0:T(8,128)}), f32[32,5,16,384]{3,2,1,0:T(8,128)}, u32[]{:S(2)}, u32[]{:S(2)}) async-start(f32[32,5,16,384]{3,2,1,0:T(8,128)} %copy-done), calls=%async_computation.1 | async-start | bytes 7864320 | tf_op jit(solution)/shard_map/all_to_all | solution.py:100
  130.1 2.1 copy-start.3
  138.4 0.9 slice-start
  138.4 1.1 slice-start.1

commit v9 on v8

--- a/solution.py
+++ b/solution.py
@@ -95,13 +95,23 @@
     lines = lax.all_to_all(send, "ax", split_axis=0, concat_axis=0, tiled=True)
     ax_halo = halos(packed, "ax", 0)
     rad_halo = halos(packed, "rad", 1)
-    res = line_section(lines, mats, jac_axial)
-    res, ax_halo, rad_halo = lax.optimization_barrier((res, ax_halo, rad_halo))
-    ret = lax.all_to_all(res, "ax", split_axis=0, concat_axis=0, tiled=True)
+    cut = (na // 3 // 128) * 256 if na % 384 == 0 else na
+    first = line_section(lines[..., :cut], mats, jac_axial)
+    first, ax_halo, rad_halo = lax.optimization_barrier((first, ax_halo, rad_halo))
+    rets = [lax.all_to_all(first, "ax", split_axis=0, concat_axis=0, tiled=True)]
+    if cut < na:
+        second = line_section(lines[..., cut:], mats, jac_axial)
+        rets[0], second = lax.optimization_barrier((rets[0], second))
+        rets.append(lax.all_to_all(second, "ax", split_axis=0, concat_axis=0, tiled=True))
     local = stencil(state, weight, ax_halo, rad_halo, jac_radial)
     local = with_layout_constraint(local, Layout(major_to_minor=(0, 2, 1, 3)))
-    ret, local = lax.optimization_barrier((ret, local))
-    return jnp.transpose(ret, (2, 0, 1, 3)) + section_step * local
+    rets, local = lax.optimization_barrier((rets, local))
+    bounds = [0, cut, na][:len(rets) + 1]
+    parts = [
+        jnp.transpose(r, (2, 0, 1, 3)) + section_step * local[..., lo:hi]
+        for r, lo, hi in zip(rets, bounds[:-1], bounds[1:])
+    ]
+    return jnp.concatenate(parts, axis=3)
 
 
 def solution(mesh):

time: 229 us -> 243 us (1.061)
  waiting for transfers between devices: 155 us -> 135 us
  local copies, waits for them, and re-layouts: 16 us -> 35 us
  other arithmetic: 17.5 us -> 24.6 us
  starting transfers between devices: 28.6 us -> 34.1 us
    all_to_all x1 -> x2, waiting for transfers between devices: 76.3 us -> 56.7 us  [the longest x1 42.6 us: body(): lax.all_to_all(first, 'ax', split_axis=0, concat_axis=0, tiled=True)]
    slice x0 -> x2, local copies, waits for them, and re-layouts: none -> 4.88 us  [the longest x1 3.48 us: body(): first = line_section(lines[..., :cut], mats, jac_axial)]
    all_to_all x1 -> x2, starting transfers between devices: 7.53 us -> 12.3 us  [the longest x1 7.53 us: body(): lax.all_to_all(first, 'ax', split_axis=0, concat_axis=0, tiled=True)]
    mul x1, other arithmetic: 1.07 us -> 4.36 us  [stencil(): spread = 0.5 * (up_f - dn_f)]
    slice x1, local copies, waits for them, and re-layouts: 0.85 us -> 3.96 us  [viscous(): lax.slice_in_dim(field, 1, field.shape[dim], axis=dim)]
    slice x1, local copies, waits for them, and re-layouts: 1 us -> 4.05 us  [viscous(): lax.slice_in_dim(field, 0, field.shape[dim] - 1, axis=dim)]
    add x1, other arithmetic: 6.22 us -> 9.09 us  [stencil(): return viscosity * visc_ax + (mixed + viscosity * visc_rad)]
    concatenate x3, local copies, waits for them, and re-layouts: 0.84 us -> 3.28 us  [viscous(): jnp.concatenate([wbefore, lax.slice_in_dim(weight, 0, weight.shape[dim] -...]
  transfers between devices with their start and end apart: 6 -> 7, of which waited for: 2 -> 3; matrix products, arithmetic and copies ran while one was open for 7% -> 17% of each run, Pallas kernels for 5% -> 5%
where the time goes in v9:
time: 243 us; the launch traced here: 242 us
  waiting for transfers between devices  135 us (56%)
  local copies, waits for them, and re-layouts  35 us (14%)
  starting transfers between devices  34.1 us (14%)
  other arithmetic  24.6 us (10%)
  Pallas kernels  12.4 us (5%)
    all_to_all x1, waiting for transfers between devices, body(): lines = lax.all_to_all(send, 'ax', split_axis=0, concat_axis=0, tiled=True)  78.4 us
    all_to_all x1, waiting for transfers between devices, body(): lax.all_to_all(first, 'ax', split_axis=0, concat_axis=0, tiled=True)  42.6 us
    all_to_all x1, waiting for transfers between devices, body(): lax.all_to_all(second, 'ax', split_axis=0, concat_axis=0, tiled=True)  14.1 us
    pallas_call x2, Pallas kernels, line_section(): pl.pallas_call(line_kernel, out_shape=jax.ShapeDtypeStruct(lines.shape, l...  12.4 us
    all_to_all x1, starting transfers between devices, body(): lines = lax.all_to_all(send, 'ax', split_axis=0, concat_axis=0, tiled=True)  11.7 us
    unnamed x40, local copies, waits for them, and re-layouts  11.7 us
    ppermute x4, starting transfers between devices, halos(): return (lax.ppermute(last, axis, up), lax.ppermute(leading, axis, down))  10.1 us
    add x1, other arithmetic, stencil(): return viscosity * visc_ax + (mixed + viscosity * visc_rad)  9.09 us
  transfers between devices with their start and end apart: 7, of which 3 were waited for; matrix products, arithmetic and copies ran while one was open for 17% of the time, Pallas kernels for 5%

profile of v9, /device:TPU:6, one launch (start us, length us, event | category | flops | bytes accessed | tf_op | source)
XLA Modules:
  0.0 241.5 jit_solution(1565349035449229331)
XLA Ops:
  0.0 6.3 %copy.24 = f32[16,32,5,384]{3,0,2,1:T(8,128)} copy(f32[16,32,5,384]{3,1,2,0:T(8,128)} %param.6) | data formatting | bytes 7864320 | tf_op args[0]
  6.3 11.7 %all-to-all-start = ((f32[32,5,16,384]{3,2,1,0:T(8,128)}), f32[32,5,16,384]{3,2,1,0:T(8,128)}, u32[]{:S(2)}, u32[]{:S(2)}) async-start(f32[32,5,16,384]{3,2,1,0:T(8,128)} %bitcast.46), calls=%async_computation | async-start | bytes 7864320 | tf_op jit(solution)/shard_map/all_to_all | solution.py:95
  18.1 2.1 pad_maximum_fusion.3
  20.2 2.9 %collective-permute-start = (f32[1,32,6,384]{3,1,2,0:T(8,128)}, f32[1,32,6,384]{3,1,2,0:T(8,128)}, u32[]{:S(2)}, u32[]{:S(2)}) collective-permute-start(f32[1,32,6,384]{3,1,2,0:T(8,128)} %get-tuple-element.28), channel_id=1, source_target_pairs={{0,8},{8,16},{16,24},{24,32},{32,40},{40,48},{48,56},{56,64},{64,7... | collective-permute-start | bytes 884744 | tf_op jit(solution)/shard_map/ppermute | solution.py:21
  25.3 2.8 %collective-permute-start.2 = (f32[16,1,6,384]{3,1,2,0:T(1,128)}, f32[16,1,6,384]{3,1,2,0:T(1,128)}, u32[]{:S(2)}, u32[]{:S(2)}) collective-permute-start(f32[16,1,6,384]{3,1,2,0:T(1,128)} %get-tuple-element.26), channel_id=1, source_target_pairs={{0,1},{1,2},{2,3},{3,4},{4,5},{5,6},{6,7},{8,9},{9,10},{10,11},{11... | collective-permute-start | bytes 442376 | tf_op jit(solution)/shard_map/ppermute | solution.py:21
  28.1 3.0 %collective-permute-start.3 = (f32[16,1,6,384]{3,1,2,0:T(1,128)S(1)}, f32[16,1,6,384]{3,1,2,0:T(1,128)}, u32[]{:S(2)}, u32[]{:S(2)}) collective-permute-start(f32[16,1,6,384]{3,1,2,0:T(1,128)S(1)} %get-tuple-element.25), channel_id=1, source_target_pairs={{1,0},{2,1},{3,2},{4,3},{5,4},{6,5},{7,6},{9,8},{10,9},{11,10},{12... | collective-permute-start | bytes 442376 | tf_op jit(solution)/shard_map/ppermute | solution.py:21
  31.3 78.4 %all-to-all-done = f32[32,5,16,384]{3,2,1,0:T(8,128)} async-done(((f32[32,5,16,384]{3,2,1,0:T(8,128)}), f32[32,5,16,384]{3,2,1,0:T(8,128)}, u32[]{:S(2)}, u32[]{:S(2)}) %all-to-all-start) | async-done | bytes 3932192 | tf_op jit(solution)/shard_map/all_to_all | solution.py:95
  109.8 3.5 %slice.138.lines_ref = f32[32,5,16,256]{3,2,1,0:T(8,128)} slice(f32[32,5,16,384]{3,2,1,0:T(8,128)} %all-to-all-done), slice={[0:32], [0:5], [0:16], [0:256]} | slice | bytes 5242880 | tf_op jit(solution)/shard_map/slice | solution.py:99
  113.3 7.6 %shard_map.64 = f32[32,5,16,256]{3,2,1,0:T(8,128)S(1)} custom-call(f32[5,5]{1,0:T(8,128)S(1)} %copy-done.1, f32[32,5,16,256]{3,2,1,0:T(8,128)} %slice.138.lines_ref, f32[1024,512]{1,0:T(8,128)S(1)} %constant_dynamic-update-slice_fusion.mats_ref), custom_call_target="tpu_custom_call" | custom-call | tf_op jit(solution)/shard_map/pallas_call | solution.py:77
  120.9 1.5 copy-done
  122.4 7.5 %all-to-all-start.1 = ((f32[32,5,16,256]{3,2,1,0:T(8,128)}), f32[32,5,16,256]{3,2,1,0:T(8,128)}, u32[]{:S(2)}, u32[]{:S(2)}) async-start(f32[32,5,16,256]{3,2,1,0:T(8,128)} %copy-done), calls=%async_computation.1 | async-start | bytes 5242880 | tf_op jit(solution)/shard_map/all_to_all | solution.py:101
  133.3 4.0 %fusion.10 = (f32[15,32,5,384]{3,1,2,0:T(8,128)}, f32[15,32,5,384]{3,1,2,0:T(8,128)}) fusion(f32[16,32,5,384]{3,1,2,0:T(8,128)S(1)} %copy-done.3), kind=kLoop, calls=%fused_computation.45 | loop fusion | bytes 14745600 | tf_op jit(solution)/shard_map/slice | solution.py:26
  137.3 4.0 %fusion.9 = (f32[16,31,5,384]{3,1,2,0:T(8,128)}, f32[16,31,5,384]{3,1,2,0:T(8,128)}) fusion(f32[16,32,5,384]{3,1,2,0:T(8,128)S(1)} %copy-done.3), kind=kLoop, calls=%fused_computation.44 | loop fusion | bytes 15237120 | tf_op jit(solution)/shard_map/slice | solution.py:25
  142.7 4.7 %shard_map.65 = f32[32,5,16,128]{3,2,1,0:T(8,128)} custom-call(f32[5,5]{1,0:T(8,128)S(1)} %copy-done.1, f32[32,5,16,128]{3,2,1,0:T(8,128)S(1)} %slice.139.lines_ref, f32[1024,512]{1,0:T(8,128)S(1)} %constant_dynamic-update-slice_fusion.mats_ref), custom_call_target="tpu_custom_call" | custom-call | tf_op jit(solution)/shard_map/pallas_call | solution.py:77
  147.4 1.7 slice.116
  151.0 42.6 %all-to-all-done.1 = f32[32,5,16,256]{3,2,1,0:T(8,128)} async-done(((f32[32,5,16,256]{3,2,1,0:T(8,128)}), f32[32,5,16,256]{3,2,1,0:T(8,128)}, u32[]{:S(2)}, u32[]{:S(2)}) %all-to-all-start.1) | async-done | bytes 2621472 | tf_op jit(solution)/shard_map/all_to_all | solution.py:101
  193.6 4.8 %all-to-all-start.2 = ((f32[32,5,16,128]{3,2,1,0:T(8,128)}), f32[32,5,16,128]{3,2,1,0:T(8,128)S(1)}, u32[]{:S(2)}, u32[]{:S(2)}) async-start(f32[32,5,16,128]{3,2,1,0:T(8,128)} %shard_map.65), calls=%async_computation.2 | async-start | bytes 2621440 | tf_op jit(solution)/shard_map/all_to_all | solution.py:105
  198.5 4.4 %subtract_multiply_fusion = f32[16,32,5,384]{3,1,2,0:T(8,128)S(1)} fusion(f32[16,31,5,384]{3,1,2,0:T(8,128)} %get-tuple-element.35, f32[16,1,5,384]{3,1,2,0:T(1,128)S(1)} %slice.121, f32[16,1,5,384]{3,1,2,0:T(1,128)S(1)} %slice.120, f32[16,31,5,384]{3,1,2,0:T(8,128)} %get-tuple-element.34), kind=kLoop, calls=%fused_computation.11 | loop fusion | flops 3932160 | bytes 11796480 | tf_op jit(solution)/shard_map/mul | solution.py:39
  202.8 1.5 slice_bitcast_fusion.9
  210.2 9.1 %fusion.3 = f32[16,32,5,384]{3,1,2,0:T(8,128)} fusion(f32[16,32,5,384]{3,1,2,0:T(8,128)S(1)} %copy-done.4, f32[1,32,5,384]{3,1,2,0:T(8,128)S(1)} %slice-done, f32[15,32,5,384]{3,1,2,0:T(8,128)S(1)} %copy-done.10, f32[15,32,5,384]{3,1,2,0:T(8,128)S(1)} %copy-done.9, f32[1,32,5,384]{3,1,2,0:T(8,128)} %slice.116, f32[16,31,5,384]{3,1,2,0:T(8,128)S(1)} %copy-done.7, ...), kind=kLoop, calls=%fused_computation.4 | loop fusion | flops 26542080 | bytes 30670948 | tf_op jit(solution)/shard_map/add | solution.py:43
  219.2 14.1 %all-to-all-done.2 = f32[32,5,16,128]{3,2,1,0:T(8,128)S(1)} async-done(((f32[32,5,16,128]{3,2,1,0:T(8,128)}), f32[32,5,16,128]{3,2,1,0:T(8,128)S(1)}, u32[]{:S(2)}, u32[]{:S(2)}) %all-to-all-start.2) | async-done | bytes 1310752 | tf_op jit(solution)/shard_map/all_to_all | solution.py:105
  233.3 1.9 bitcast_add_fusion.1
  235.9 3.4 %bitcast_add_fusion = f32[16,32,5,256]{3,1,2,0:T(8,128)S(1)} fusion(f32[32,5,16,256]{3,2,1,0:T(8,128)} %all-to-all-done.1, f32[16,32,5,384]{3,1,2,0:T(8,128)S(1)} %copy-done.8), kind=kLoop, calls=%fused_computation.12 | loop fusion | flops 1310720 | bytes 7864320 | tf_op jit(solution)/shard_map/add | solution.py:111
  239.3 2.3 pad_maximum_fusion.2
  (57 shorter events, 15.2 us)
Async XLA Ops:
  6.3 11.8 %copy-start.5 = (f32[16,32,384]{2,1,0:T(8,128)S(1)}, f32[16,32,384]{2,1,0:T(8,128)}, u32[]{:S(2)}) copy-start(f32[16,32,384]{2,1,0:T(8,128)} %param.7) | copy-start | bytes 2359300
  6.3 103.5 %all-to-all-start = ((f32[32,5,16,384]{3,2,1,0:T(8,128)}), f32[32,5,16,384]{3,2,1,0:T(8,128)}, u32[]{:S(2)}, u32[]{:S(2)}) async-start(f32[32,5,16,384]{3,2,1,0:T(8,128)} %bitcast.46), calls=%async_computation | async-start | bytes 7864320 | tf_op jit(solution)/shard_map/all_to_all | solution.py:95
  18.1 6.4 %copy-start.2 = (f32[16,32,5,384]{3,1,2,0:T(8,128)S(1)}, f32[16,32,5,384]{3,1,2,0:T(8,128)}, u32[]{:S(2)}) copy-start(f32[16,32,5,384]{3,1,2,0:T(8,128)} %param.6) | copy-start | bytes 11796484
  18.1 13.1 %copy-start.15 = (f32[512,512]{1,0:T(8,128)S(1)}, f32[512,512]{1,0:T(8,128)}, u32[]{:S(2)}) copy-start(f32[512,512]{1,0:T(8,128)} %param.9) | copy-start | bytes 3145732
  20.2 11.1 %copy-start.16 = (f32[512,512]{1,0:T(8,128)S(1)}, f32[512,512]{1,0:T(8,128)}, u32[]{:S(2)}) copy-start(f32[512,512]{1,0:T(8,128)} %param.8) | copy-start | bytes 3145732
  20.2 102.2 %collective-permute-start = (f32[1,32,6,384]{3,1,2,0:T(8,128)}, f32[1,32,6,384]{3,1,2,0:T(8,128)}, u32[]{:S(2)}, u32[]{:S(2)}) collective-permute-start(f32[1,32,6,384]{3,1,2,0:T(8,128)} %get-tuple-element.28), channel_id=1, source_target_pairs={{0,8},{8,16},{16,24},{24,32},{32,40},{40,48},{48,56},{56,64},{64,7... | collective-permute-start | bytes 884744 | tf_op jit(solution)/shard_map/ppermute | solution.py:21
  23.1 99.3 %collective-permute-start.1 = (f32[1,32,6,384]{3,1,2,0:T(8,128)}, f32[1,32,6,384]{3,1,2,0:T(8,128)S(1)}, u32[]{:S(2)}, u32[]{:S(2)}) collective-permute-start(f32[1,32,6,384]{3,1,2,0:T(8,128)} %get-tuple-element.27), channel_id=1, source_target_pairs={{8,0},{16,8},{24,16},{32,24},{40,32},{48,40},{56,48},{64,56},{72,6... | collective-permute-start | bytes 884744 | tf_op jit(solution)/shard_map/ppermute | solution.py:21
  25.3 97.1 %collective-permute-start.2 = (f32[16,1,6,384]{3,1,2,0:T(1,128)}, f32[16,1,6,384]{3,1,2,0:T(1,128)}, u32[]{:S(2)}, u32[]{:S(2)}) collective-permute-start(f32[16,1,6,384]{3,1,2,0:T(1,128)} %get-tuple-element.26), channel_id=1, source_target_pairs={{0,1},{1,2},{2,3},{3,4},{4,5},{5,6},{6,7},{8,9},{9,10},{10,11},{11... | collective-permute-start | bytes 442376 | tf_op jit(solution)/shard_map/ppermute | solution.py:21
  28.1 94.3 %collective-permute-start.3 = (f32[16,1,6,384]{3,1,2,0:T(1,128)S(1)}, f32[16,1,6,384]{3,1,2,0:T(1,128)}, u32[]{:S(2)}, u32[]{:S(2)}) collective-permute-start(f32[16,1,6,384]{3,1,2,0:T(1,128)S(1)} %get-tuple-element.25), channel_id=1, source_target_pairs={{1,0},{2,1},{3,2},{4,3},{5,4},{6,5},{7,6},{9,8},{10,9},{11,10},{12... | collective-permute-start | bytes 442376 | tf_op jit(solution)/shard_map/ppermute | solution.py:21
  31.3 82.0 %copy-start.1 = (f32[5,5]{1,0:T(8,128)S(1)}, f32[5,5]{1,0:T(8,128)}, u32[]{:S(2)}) copy-start(f32[5,5]{1,0:T(8,128)} %jac_ref.3) | copy-start | bytes 304
  122.4 7.6 %copy-start.18 = (f32[5,5]{1,0:T(8,128)S(1)}, f32[5,5]{1,0:T(8,128)}, u32[]{:S(2)}) copy-start(f32[5,5]{1,0:T(8,128)} %param.11) | copy-start | bytes 304
  122.4 81.9 %copy-start.17 = (f32[1,32,6,384]{3,1,2,0:T(8,128)}, f32[1,32,6,384]{3,1,2,0:T(8,128)S(1)}, u32[]{:S(2)}) copy-start(f32[1,32,6,384]{3,1,2,0:T(8,128)S(1)} %collective-permute-done.1) | copy-start | bytes 884740
  122.4 71.2 %all-to-all-start.1 = ((f32[32,5,16,256]{3,2,1,0:T(8,128)}), f32[32,5,16,256]{3,2,1,0:T(8,128)}, u32[]{:S(2)}, u32[]{:S(2)}) async-start(f32[32,5,16,256]{3,2,1,0:T(8,128)} %copy-done), calls=%async_computation.1 | async-start | bytes 5242880 | tf_op jit(solution)/shard_map/all_to_all | solution.py:101
  130.0 3.3 %copy-start.3 = (f32[16,32,5,384]{3,1,2,0:T(8,128)S(1)}, f32[16,32,5,384]{3,1,2,0:T(8,128)}, u32[]{:S(2)}) copy-start(f32[16,32,5,384]{3,1,2,0:T(8,128)} %param.6) | copy-start | bytes 11796484
  193.6 39.7 %all-to-all-start.2 = ((f32[32,5,16,128]{3,2,1,0:T(8,128)}), f32[32,5,16,128]{3,2,1,0:T(8,128)S(1)}, u32[]{:S(2)}, u32[]{:S(2)}) async-start(f32[32,5,16,128]{3,2,1,0:T(8,128)} %shard_map.65), calls=%async_computation.2 | async-start | bytes 2621440 | tf_op jit(solution)/shard_map/all_to_all | solution.py:105
  198.4 6.8 %copy-start.11 = (f32[16,31,384]{2,1,0:T(8,128)S(1)}, f32[16,31,384]{2,1,0:T(8,128)}, u32[]{:S(2)}) copy-start(f32[16,31,384]{2,1,0:T(8,128)} %slice_bitcast_fusion) | copy-start | bytes 2285572
  198.4 6.8 %copy-start.12 = (f32[16,31,384]{2,1,0:T(8,128)S(1)}, f32[16,31,384]{2,1,0:T(8,128)}, u32[]{:S(2)}) copy-start(f32[16,31,384]{2,1,0:T(8,128)} %slice_bitcast_fusion.1) | copy-start | bytes 2285572
  198.4 6.8 %copy-start.13 = (f32[15,32,384]{2,1,0:T(8,128)S(1)}, f32[15,32,384]{2,1,0:T(8,128)}, u32[]{:S(2)}) copy-start(f32[15,32,384]{2,1,0:T(8,128)} %get-tuple-element.42) | copy-start | bytes 2211844
  198.4 6.8 %copy-start.14 = (f32[15,32,384]{2,1,0:T(8,128)S(1)}, f32[15,32,384]{2,1,0:T(8,128)}, u32[]{:S(2)}) copy-start(f32[15,32,384]{2,1,0:T(8,128)} %get-tuple-element.43) | copy-start | bytes 2211844
  198.5 8.5 %copy-start.9 = (f32[15,32,5,384]{3,1,2,0:T(8,128)S(1)}, f32[15,32,5,384]{3,1,2,0:T(8,128)}, u32[]{:S(2)}) copy-start(f32[15,32,5,384]{3,1,2,0:T(8,128)} %get-tuple-element.36) | copy-start | bytes 11059204
  198.5 8.5 %copy-start.10 = (f32[15,32,5,384]{3,1,2,0:T(8,128)S(1)}, f32[15,32,5,384]{3,1,2,0:T(8,128)}, u32[]{:S(2)}) copy-start(f32[15,32,5,384]{3,1,2,0:T(8,128)} %get-tuple-element.37) | copy-start | bytes 11059204
  205.8 3.3 %copy-start.4 = (f32[16,32,5,384]{3,1,2,0:T(8,128)S(1)}, f32[16,32,5,384]{3,1,2,0:T(8,128)}, u32[]{:S(2)}) copy-start(f32[16,32,5,384]{3,1,2,0:T(8,128)} %param.6) | copy-start | bytes 11796484
  205.8 4.4 %copy-start.6 = (f32[16,31,5,384]{3,1,2,0:T(8,128)S(1)}, f32[16,31,5,384]{3,1,2,0:T(8,128)}, u32[]{:S(2)}) copy-start(f32[16,31,5,384]{3,1,2,0:T(8,128)} %get-tuple-element.34) | copy-start | bytes 11427844
  233.3 2.5 %copy-start.8 = (f32[16,32,5,384]{3,1,2,0:T(8,128)S(1)}, f32[16,32,5,384]{3,1,2,0:T(8,128)}, u32[]{:S(2)}) copy-start(f32[16,32,5,384]{3,1,2,0:T(8,128)} %fusion.3) | copy-start | bytes 11796484
  (3 other events, 6.3 us)

commit v10 on v8

--- a/solution.py
+++ b/solution.py
@@ -80,6 +80,7 @@
         grid=(A // C,),
         in_specs=[pl.BlockSpec(memory_space=pltpu.SMEM), block, whole],
         out_specs=block,
+        input_output_aliases={1: 0},
         compiler_params=pltpu.CompilerParams(vmem_limit_bytes=48 * 1024 * 1024),
     )(jac_axial, lines, mats)
 

time: 229 us -> 228 us (level)
    unnamed x21 -> x19, local copies, waits for them, and re-layouts: 10.1 us -> 8.14 us
where the time goes in v10:
time: 228 us
  waiting for transfers between devices  155 us (68%)
  starting transfers between devices  28.6 us (13%)
  other arithmetic  17.6 us (8%)
  local copies, waits for them, and re-layouts  14 us (6%)
  Pallas kernels  11.7 us (5%)
    all_to_all x1, waiting for transfers between devices, body(): lines = lax.all_to_all(send, 'ax', split_axis=0, concat_axis=0, tiled=True)  79 us
    all_to_all x1, waiting for transfers between devices, body(): ret = lax.all_to_all(res, 'ax', split_axis=0, concat_axis=0, tiled=True)  76.3 us
    all_to_all x1, starting transfers between devices, body(): lines = lax.all_to_all(send, 'ax', split_axis=0, concat_axis=0, tiled=True)  11.7 us
    pallas_call x1, Pallas kernels, line_section(): pl.pallas_call(line_kernel, out_shape=jax.ShapeDtypeStruct(lines.shape, l...  11.7 us
    ppermute x4, starting transfers between devices, halos(): return (lax.ppermute(last, axis, up), lax.ppermute(leading, axis, down))  9.37 us
    unnamed x19, local copies, waits for them, and re-layouts  8.14 us
    all_to_all x1, starting transfers between devices, body(): ret = lax.all_to_all(res, 'ax', split_axis=0, concat_axis=0, tiled=True)  7.53 us
    add x1, other arithmetic, body(): return jnp.transpose(ret, (2, 0, 1, 3)) + section_step * local  6.63 us
  transfers between devices with their start and end apart: 6, of which 2 were waited for; matrix products, arithmetic and copies ran while one was open for 7% of the time, Pallas kernels for 5%

profile of v10, /device:TPU:6, one launch (start us, length us, event | category | flops | bytes accessed | tf_op | source)
XLA Modules:
  0.0 227.6 jit_solution(4882357243106668453)
XLA Ops:
  0.0 6.3 %copy.20 = f32[16,32,5,384]{3,0,2,1:T(8,128)} copy(f32[16,32,5,384]{3,1,2,0:T(8,128)} %param.6) | data formatting | bytes 7864320 | tf_op args[0]
  6.3 11.7 %all-to-all-start = ((f32[32,5,16,384]{3,2,1,0:T(8,128)}), f32[32,5,16,384]{3,2,1,0:T(8,128)}, u32[]{:S(2)}, u32[]{:S(2)}) async-start(f32[32,5,16,384]{3,2,1,0:T(8,128)} %bitcast.44), calls=%async_computation | async-start | bytes 7864320 | tf_op jit(solution)/shard_map/all_to_all | solution.py:96
  18.1 2.1 pad_maximum_fusion.3
  20.2 2.2 collective-permute-start
  22.4 1.3 collective-permute-start.1
  23.8 0.9 pad_maximum_fusion.5
  24.7 2.8 %collective-permute-start.2 = (f32[16,1,6,384]{3,1,2,0:T(1,128)}, f32[16,1,6,384]{3,1,2,0:T(1,128)}, u32[]{:S(2)}, u32[]{:S(2)}) collective-permute-start(f32[16,1,6,384]{3,1,2,0:T(1,128)} %get-tuple-element.20), channel_id=1, source_target_pairs={{0,1},{1,2},{2,3},{3,4},{4,5},{5,6},{6,7},{8,9},{9,10},{10,11},{11... | collective-permute-start | bytes 442376 | tf_op jit(solution)/shard_map/ppermute | solution.py:21
  27.5 3.0 %collective-permute-start.3 = (f32[16,1,6,384]{3,1,2,0:T(1,128)}, f32[16,1,6,384]{3,1,2,0:T(1,128)}, u32[]{:S(2)}, u32[]{:S(2)}) collective-permute-start(f32[16,1,6,384]{3,1,2,0:T(1,128)} %get-tuple-element.19), channel_id=1, source_target_pairs={{1,0},{2,1},{3,2},{4,3},{5,4},{6,5},{7,6},{9,8},{10,9},{11,10},{12... | collective-permute-start | bytes 442376 | tf_op jit(solution)/shard_map/ppermute | solution.py:21
  30.7 79.0 %all-to-all-done.lines_ref = f32[32,5,16,384]{3,2,1,0:T(8,128)} async-done(((f32[32,5,16,384]{3,2,1,0:T(8,128)}), f32[32,5,16,384]{3,2,1,0:T(8,128)}, u32[]{:S(2)}, u32[]{:S(2)}) %all-to-all-start) | async-done | bytes 3932192 | tf_op jit(solution)/shard_map/all_to_all | solution.py:96
  109.8 11.7 %shard_map.64 = f32[32,5,16,384]{3,2,1,0:T(8,128)} custom-call(f32[5,5]{1,0:T(8,128)S(1)} %copy-done, f32[32,5,16,384]{3,2,1,0:T(8,128)} %all-to-all-done.lines_ref, f32[1024,512]{1,0:T(8,128)S(1)} %pad_maximum_fusion.2.mats_ref), custom_call_target="tpu_custom_call", output_to_operand_aliasing={{}: (1, {})} | custom-call | tf_op jit(solution)/shard_map/pallas_call | solution.py:77
  121.6 7.5 %all-to-all-start.1 = ((f32[32,5,16,384]{3,2,1,0:T(8,128)}), f32[32,5,16,384]{3,2,1,0:T(8,128)}, u32[]{:S(2)}, u32[]{:S(2)}) async-start(f32[32,5,16,384]{3,2,1,0:T(8,128)} %shard_map.64), calls=%async_computation.1 | async-start | bytes 7864320 | tf_op jit(solution)/shard_map/all_to_all | solution.py:101
  129.5 1.8 copy-done.2
  131.2 1.0 fusion.10
  132.2 0.8 fusion.9
  133.1 1.0 slice.107
  134.1 1.0 slice.106
  135.0 1.1 subtract_multiply_fusion
  136.1 0.8 slice_bitcast_fusion.9
  136.9 0.5 fusion.5
  137.4 0.3 slice_bitcast_fusion.6
  137.8 0.6 slice-done
  138.5 6.2 %fusion.3 = f32[16,32,5,384]{3,1,2,0:T(8,128)} fusion(f32[16,32,5,384]{3,1,2,0:T(8,128)S(1)} %copy-done.2, f32[1,32,5,384]{3,1,2,0:T(8,128)S(1)} %slice-done, f32[15,32,5,384]{3,1,2,0:T(8,128)S(1)} %get-tuple-element.31, f32[15,32,5,384]{3,1,2,0:T(8,128)S(1)} %get-tuple-element.30, f32[1,32,5,384]{3,1,2,0:T(8,128)S(1)} %slice-done.1, ...), kind=kLoop, calls=%fused_computation.4 | loop fusion | flops 26542080 | bytes 30670948 | tf_op jit(solution)/shard_map/add | solution.py:43
  144.7 76.3 %all-to-all-done.1 = f32[32,5,16,384]{3,2,1,0:T(8,128)} async-done(((f32[32,5,16,384]{3,2,1,0:T(8,128)}), f32[32,5,16,384]{3,2,1,0:T(8,128)}, u32[]{:S(2)}, u32[]{:S(2)}) %all-to-all-start.1) | async-done | bytes 3932192 | tf_op jit(solution)/shard_map/all_to_all | solution.py:101
  221.0 6.6 %bitcast_add_fusion = f32[16,32,5,384]{3,1,2,0:T(8,128)} fusion(f32[32,5,16,384]{3,2,1,0:T(8,128)} %all-to-all-done.1, f32[16,32,5,384]{3,1,2,0:T(8,128)} %fusion.3), kind=kLoop, calls=%fused_computation.9 | loop fusion | flops 1966080 | bytes 11796480 | tf_op jit(solution)/shard_map/add | solution.py:105
  (30 shorter events, 0.7 us)
Async XLA Ops:
  6.3 11.8 %copy-start.3 = (f32[16,32,384]{2,1,0:T(8,128)S(1)}, f32[16,32,384]{2,1,0:T(8,128)}, u32[]{:S(2)}) copy-start(f32[16,32,384]{2,1,0:T(8,128)} %param.7) | copy-start | bytes 2359300
  6.3 103.5 %all-to-all-start = ((f32[32,5,16,384]{3,2,1,0:T(8,128)}), f32[32,5,16,384]{3,2,1,0:T(8,128)}, u32[]{:S(2)}, u32[]{:S(2)}) async-start(f32[32,5,16,384]{3,2,1,0:T(8,128)} %bitcast.44), calls=%async_computation | async-start | bytes 7864320 | tf_op jit(solution)/shard_map/all_to_all | solution.py:96
  18.1 5.7 %copy-start.1 = (f32[16,32,5,384]{3,1,2,0:T(8,128)S(1)}, f32[16,32,5,384]{3,1,2,0:T(8,128)}, u32[]{:S(2)}) copy-start(f32[16,32,5,384]{3,1,2,0:T(8,128)} %param.6) | copy-start | bytes 11796484
  18.1 12.5 %copy-start.4 = (f32[512,512]{1,0:T(8,128)S(1)}, f32[512,512]{1,0:T(8,128)}, u32[]{:S(2)}) copy-start(f32[512,512]{1,0:T(8,128)} %param.8) | copy-start | bytes 3145732
  18.1 12.5 %copy-start.5 = (f32[512,512]{1,0:T(8,128)S(1)}, f32[512,512]{1,0:T(8,128)}, u32[]{:S(2)}) copy-start(f32[512,512]{1,0:T(8,128)} %param.9) | copy-start | bytes 3145732
  20.2 101.3 %collective-permute-start = (f32[1,32,6,384]{3,1,2,0:T(8,128)}, f32[1,32,6,384]{3,1,2,0:T(8,128)S(1)}, u32[]{:S(2)}, u32[]{:S(2)}) collective-permute-start(f32[1,32,6,384]{3,1,2,0:T(8,128)} %get-tuple-element.22), channel_id=1, source_target_pairs={{0,8},{8,16},{16,24},{24,32},{32,40},{40,48},{48,56},{56,64},{64,7... | collective-permute-start | bytes 884744 | tf_op jit(solution)/shard_map/ppermute | solution.py:21
  22.4 87.3 %copy-start = (f32[5,5]{1,0:T(8,128)S(1)}, f32[5,5]{1,0:T(8,128)}, u32[]{:S(2)}) copy-start(f32[5,5]{1,0:T(8,128)} %jac_ref.1) | copy-start | bytes 304
  22.4 99.1 %collective-permute-start.1 = (f32[1,32,6,384]{3,1,2,0:T(8,128)}, f32[1,32,6,384]{3,1,2,0:T(8,128)S(1)}, u32[]{:S(2)}, u32[]{:S(2)}) collective-permute-start(f32[1,32,6,384]{3,1,2,0:T(8,128)} %get-tuple-element.21), channel_id=1, source_target_pairs={{8,0},{16,8},{24,16},{32,24},{40,32},{48,40},{56,48},{64,56},{72,6... | collective-permute-start | bytes 884744 | tf_op jit(solution)/shard_map/ppermute | solution.py:21
  24.7 96.8 %collective-permute-start.2 = (f32[16,1,6,384]{3,1,2,0:T(1,128)}, f32[16,1,6,384]{3,1,2,0:T(1,128)}, u32[]{:S(2)}, u32[]{:S(2)}) collective-permute-start(f32[16,1,6,384]{3,1,2,0:T(1,128)} %get-tuple-element.20), channel_id=1, source_target_pairs={{0,1},{1,2},{2,3},{3,4},{4,5},{5,6},{6,7},{8,9},{9,10},{10,11},{11... | collective-permute-start | bytes 442376 | tf_op jit(solution)/shard_map/ppermute | solution.py:21
  27.5 94.0 %collective-permute-start.3 = (f32[16,1,6,384]{3,1,2,0:T(1,128)}, f32[16,1,6,384]{3,1,2,0:T(1,128)}, u32[]{:S(2)}, u32[]{:S(2)}) collective-permute-start(f32[16,1,6,384]{3,1,2,0:T(1,128)} %get-tuple-element.19), channel_id=1, source_target_pairs={{1,0},{2,1},{3,2},{4,3},{5,4},{6,5},{7,6},{9,8},{10,9},{11,10},{12... | collective-permute-start | bytes 442376 | tf_op jit(solution)/shard_map/ppermute | solution.py:21
  121.5 7.6 %copy-start.8 = (f32[5,5]{1,0:T(8,128)S(1)}, f32[5,5]{1,0:T(8,128)}, u32[]{:S(2)}) copy-start(f32[5,5]{1,0:T(8,128)} %param.11) | copy-start | bytes 304
  121.5 15.3 %copy-start.7 = (f32[1,32,6,384]{3,1,2,0:T(8,128)}, f32[1,32,6,384]{3,1,2,0:T(8,128)S(1)}, u32[]{:S(2)}) copy-start(f32[1,32,6,384]{3,1,2,0:T(8,128)S(1)} %collective-permute-done) | copy-start | bytes 884740
  121.6 15.3 %copy-start.6 = (f32[1,32,6,384]{3,1,2,0:T(8,128)}, f32[1,32,6,384]{3,1,2,0:T(8,128)S(1)}, u32[]{:S(2)}) copy-start(f32[1,32,6,384]{3,1,2,0:T(8,128)S(1)} %collective-permute-done.1) | copy-start | bytes 884740
  121.6 99.4 %all-to-all-start.1 = ((f32[32,5,16,384]{3,2,1,0:T(8,128)}), f32[32,5,16,384]{3,2,1,0:T(8,128)}, u32[]{:S(2)}, u32[]{:S(2)}) async-start(f32[32,5,16,384]{3,2,1,0:T(8,128)} %shard_map.64), calls=%async_computation.1 | async-start | bytes 7864320 | tf_op jit(solution)/shard_map/all_to_all | solution.py:101
  129.1 2.1 copy-start.2
  137.4 0.9 slice-start
  137.4 1.1 slice-start.1

commit v11 on v10

--- a/solution.py
+++ b/solution.py
@@ -85,6 +85,24 @@
     )(jac_axial, lines, mats)
 
 
+def swap_kernel(x_ref, o_ref):
+    for v in range(x_ref.shape[1]):
+        o_ref[:, v, :, :] = jnp.swapaxes(x_ref[:, v, :, :], 0, 1)
+
+
+def swap_outer(x):
+    X, V, R, A = x.shape
+    C = 128 if A % 128 == 0 else A
+    return pl.pallas_call(
+        swap_kernel,
+        out_shape=jax.ShapeDtypeStruct((R, V, X, A), x.dtype),
+        grid=(A // C,),
+        in_specs=[pl.BlockSpec((X, V, R, C), lambda a: (0, 0, 0, a))],
+        out_specs=pl.BlockSpec((R, V, X, C), lambda a: (0, 0, 0, a)),
+        compiler_params=pltpu.CompilerParams(vmem_limit_bytes=48 * 1024 * 1024),
+    )(x)
+
+
 def body(state, metric, deriv, filt_corr, jac_axial, jac_radial):
     nx, nr, nv, na = state.shape
     peers = lax.axis_size("ax")
@@ -92,7 +110,7 @@
     mats = jnp.concatenate([filt_corr, deriv], axis=0)
     weight = metric.reshape(metric.shape[0], metric.shape[1], 1, metric.shape[2])
     packed = jnp.concatenate([state, weight], axis=2)
-    send = jnp.transpose(state, (1, 2, 0, 3))
+    send = swap_outer(jnp.transpose(state, (0, 2, 1, 3)))
     lines = lax.all_to_all(send, "ax", split_axis=0, concat_axis=0, tiled=True)
     ax_halo = halos(packed, "ax", 0)
     rad_halo = halos(packed, "rad", 1)

time: 228 us -> 227 us (level)
  local copies, waits for them, and re-layouts: 14 us -> 9.64 us
  Pallas kernels: 11.7 us -> 15 us
    unnamed x19 -> x20, local copies, waits for them, and re-layouts: 8.14 us -> 3.74 us
    pallas_call x0 -> x1, Pallas kernels: none -> 3.31 us  [swap_outer(): pl.pallas_call(swap_kernel, out_shape=jax.ShapeDtypeStruct((R, V, X, A),...]
where the time goes in v11:
time: 227 us; the launch traced here: 226 us
  waiting for transfers between devices  156 us (69%)
  starting transfers between devices  28.5 us (13%)
  other arithmetic  17.6 us (8%)
  Pallas kernels  15 us (7%)
  local copies, waits for them, and re-layouts  9.64 us (4%)
    all_to_all x1, waiting for transfers between devices, body(): lines = lax.all_to_all(send, 'ax', split_axis=0, concat_axis=0, tiled=True)  79 us
    all_to_all x1, waiting for transfers between devices, body(): ret = lax.all_to_all(res, 'ax', split_axis=0, concat_axis=0, tiled=True)  76.5 us
    all_to_all x1, starting transfers between devices, body(): lines = lax.all_to_all(send, 'ax', split_axis=0, concat_axis=0, tiled=True)  11.7 us
    pallas_call x1, Pallas kernels, line_section(): pl.pallas_call(line_kernel, out_shape=jax.ShapeDtypeStruct(lines.shape, l...  11.7 us
    ppermute x4, starting transfers between devices, halos(): return (lax.ppermute(last, axis, up), lax.ppermute(leading, axis, down))  9.37 us
    all_to_all x1, starting transfers between devices, body(): ret = lax.all_to_all(res, 'ax', split_axis=0, concat_axis=0, tiled=True)  7.35 us
    add x1, other arithmetic, body(): return jnp.transpose(ret, (2, 0, 1, 3)) + section_step * local  6.63 us
    add x1, other arithmetic, stencil(): return viscosity * visc_ax + (mixed + viscosity * visc_rad)  6.21 us
  transfers between devices with their start and end apart: 6, of which 2 were waited for; matrix products, arithmetic and copies ran while one was open for 7% of the time, Pallas kernels for 5%

profile of v11, /device:TPU:6, one launch (start us, length us, event | category | flops | bytes accessed | tf_op | source)
XLA Modules:
  0.0 226.5 jit_solution(4847139525594438658)
XLA Ops:
  0.0 3.3 %shard_map.64 = f32[32,5,16,384]{3,2,1,0:T(8,128)S(1)} custom-call(f32[16,5,32,384]{3,2,1,0:T(8,128)} %bitcast.38), custom_call_target="tpu_custom_call" | custom-call | tf_op jit(solution)/shard_map/pallas_call | solution.py:96
  3.3 1.9 copy-done
  5.2 11.7 %all-to-all-start = ((f32[32,5,16,384]{3,2,1,0:T(8,128)}), f32[32,5,16,384]{3,2,1,0:T(8,128)}, u32[]{:S(2)}, u32[]{:S(2)}) async-start(f32[32,5,16,384]{3,2,1,0:T(8,128)} %copy-done), calls=%async_computation | async-start | bytes 7864320 | tf_op jit(solution)/shard_map/all_to_all | solution.py:114
  17.0 2.1 pad_maximum_fusion.3
  19.1 2.2 collective-permute-start
  21.4 1.3 collective-permute-start.1
  22.7 0.9 pad_maximum_fusion.5
  23.6 2.8 %collective-permute-start.2 = (f32[16,1,6,384]{3,1,2,0:T(1,128)}, f32[16,1,6,384]{3,1,2,0:T(1,128)}, u32[]{:S(2)}, u32[]{:S(2)}) collective-permute-start(f32[16,1,6,384]{3,1,2,0:T(1,128)} %get-tuple-element.20), channel_id=1, source_target_pairs={{0,1},{1,2},{2,3},{3,4},{4,5},{5,6},{6,7},{8,9},{9,10},{10,11},{11... | collective-permute-start | bytes 442376 | tf_op jit(solution)/shard_map/ppermute | solution.py:21
  26.5 3.0 %collective-permute-start.3 = (f32[16,1,6,384]{3,1,2,0:T(1,128)}, f32[16,1,6,384]{3,1,2,0:T(1,128)}, u32[]{:S(2)}, u32[]{:S(2)}) collective-permute-start(f32[16,1,6,384]{3,1,2,0:T(1,128)} %get-tuple-element.19), channel_id=1, source_target_pairs={{1,0},{2,1},{3,2},{4,3},{5,4},{6,5},{7,6},{9,8},{10,9},{11,10},{12... | collective-permute-start | bytes 442376 | tf_op jit(solution)/shard_map/ppermute | solution.py:21
  29.7 79.0 %all-to-all-done.lines_ref = f32[32,5,16,384]{3,2,1,0:T(8,128)} async-done(((f32[32,5,16,384]{3,2,1,0:T(8,128)}), f32[32,5,16,384]{3,2,1,0:T(8,128)}, u32[]{:S(2)}, u32[]{:S(2)}) %all-to-all-start) | async-done | bytes 3932192 | tf_op jit(solution)/shard_map/all_to_all | solution.py:114
  108.7 11.7 %shard_map.65 = f32[32,5,16,384]{3,2,1,0:T(8,128)} custom-call(f32[5,5]{1,0:T(8,128)S(1)} %copy-done.1, f32[32,5,16,384]{3,2,1,0:T(8,128)} %all-to-all-done.lines_ref, f32[1024,512]{1,0:T(8,128)S(1)} %pad_maximum_fusion.2.mats_ref), custom_call_target="tpu_custom_call", output_to_operand_aliasing={{}: (1, {})} | custom-call | tf_op jit(solution)/shard_map/pallas_call | solution.py:77
  120.4 7.3 %all-to-all-start.1 = ((f32[32,5,16,384]{3,2,1,0:T(8,128)}), f32[32,5,16,384]{3,2,1,0:T(8,128)}, u32[]{:S(2)}, u32[]{:S(2)}) async-start(f32[32,5,16,384]{3,2,1,0:T(8,128)} %shard_map.65), calls=%async_computation.1 | async-start | bytes 7864320 | tf_op jit(solution)/shard_map/all_to_all | solution.py:119
  128.1 1.8 copy-done.3
  129.9 1.0 fusion.10
  130.9 0.8 fusion.9
  131.8 1.0 slice.107
  132.8 1.0 slice.106
  133.7 1.1 subtract_multiply_fusion
  134.8 0.8 slice_bitcast_fusion.9
  135.6 0.5 fusion.5
  136.5 0.6 slice-done
  137.2 6.2 %fusion.3 = f32[16,32,5,384]{3,1,2,0:T(8,128)} fusion(f32[16,32,5,384]{3,1,2,0:T(8,128)S(1)} %copy-done.3, f32[1,32,5,384]{3,1,2,0:T(8,128)S(1)} %slice-done, f32[15,32,5,384]{3,1,2,0:T(8,128)S(1)} %get-tuple-element.31, f32[15,32,5,384]{3,1,2,0:T(8,128)S(1)} %get-tuple-element.30, f32[1,32,5,384]{3,1,2,0:T(8,128)S(1)} %slice-done.1, ...), kind=kLoop, calls=%fused_computation.4 | loop fusion | flops 26542080 | bytes 30670948 | tf_op jit(solution)/shard_map/add | solution.py:43
  143.4 76.5 %all-to-all-done.1 = f32[32,5,16,384]{3,2,1,0:T(8,128)} async-done(((f32[32,5,16,384]{3,2,1,0:T(8,128)}), f32[32,5,16,384]{3,2,1,0:T(8,128)}, u32[]{:S(2)}, u32[]{:S(2)}) %all-to-all-start.1) | async-done | bytes 3932192 | tf_op jit(solution)/shard_map/all_to_all | solution.py:119
  219.8 6.6 %bitcast_add_fusion = f32[16,32,5,384]{3,1,2,0:T(8,128)} fusion(f32[32,5,16,384]{3,2,1,0:T(8,128)} %all-to-all-done.1, f32[16,32,5,384]{3,1,2,0:T(8,128)} %fusion.3), kind=kLoop, calls=%fused_computation.9 | loop fusion | flops 1966080 | bytes 11796480 | tf_op jit(solution)/shard_map/add | solution.py:123
  (32 shorter events, 1.0 us)
Async XLA Ops:
  3.3 1.9 copy-start
  5.2 11.8 %copy-start.4 = (f32[16,32,384]{2,1,0:T(8,128)S(1)}, f32[16,32,384]{2,1,0:T(8,128)}, u32[]{:S(2)}) copy-start(f32[16,32,384]{2,1,0:T(8,128)} %param.7) | copy-start | bytes 2359300
  5.2 103.5 %all-to-all-start = ((f32[32,5,16,384]{3,2,1,0:T(8,128)}), f32[32,5,16,384]{3,2,1,0:T(8,128)}, u32[]{:S(2)}, u32[]{:S(2)}) async-start(f32[32,5,16,384]{3,2,1,0:T(8,128)} %copy-done), calls=%async_computation | async-start | bytes 7864320 | tf_op jit(solution)/shard_map/all_to_all | solution.py:114
  17.0 5.7 %copy-start.2 = (f32[16,32,5,384]{3,1,2,0:T(8,128)S(1)}, f32[16,32,5,384]{3,1,2,0:T(8,128)}, u32[]{:S(2)}) copy-start(f32[16,32,5,384]{3,1,2,0:T(8,128)} %param.6) | copy-start | bytes 11796484
  17.0 12.5 %copy-start.5 = (f32[512,512]{1,0:T(8,128)S(1)}, f32[512,512]{1,0:T(8,128)}, u32[]{:S(2)}) copy-start(f32[512,512]{1,0:T(8,128)} %param.8) | copy-start | bytes 3145732
  17.0 12.5 %copy-start.6 = (f32[512,512]{1,0:T(8,128)S(1)}, f32[512,512]{1,0:T(8,128)}, u32[]{:S(2)}) copy-start(f32[512,512]{1,0:T(8,128)} %param.9) | copy-start | bytes 3145732
  19.1 101.3 %collective-permute-start = (f32[1,32,6,384]{3,1,2,0:T(8,128)}, f32[1,32,6,384]{3,1,2,0:T(8,128)S(1)}, u32[]{:S(2)}, u32[]{:S(2)}) collective-permute-start(f32[1,32,6,384]{3,1,2,0:T(8,128)} %get-tuple-element.22), channel_id=1, source_target_pairs={{0,8},{8,16},{16,24},{24,32},{32,40},{40,48},{48,56},{56,64},{64,7... | collective-permute-start | bytes 884744 | tf_op jit(solution)/shard_map/ppermute | solution.py:21
  21.4 87.4 %copy-start.1 = (f32[5,5]{1,0:T(8,128)S(1)}, f32[5,5]{1,0:T(8,128)}, u32[]{:S(2)}) copy-start(f32[5,5]{1,0:T(8,128)} %jac_ref.1) | copy-start | bytes 304
  21.4 99.0 %collective-permute-start.1 = (f32[1,32,6,384]{3,1,2,0:T(8,128)}, f32[1,32,6,384]{3,1,2,0:T(8,128)S(1)}, u32[]{:S(2)}, u32[]{:S(2)}) collective-permute-start(f32[1,32,6,384]{3,1,2,0:T(8,128)} %get-tuple-element.21), channel_id=1, source_target_pairs={{8,0},{16,8},{24,16},{32,24},{40,32},{48,40},{56,48},{64,56},{72,6... | collective-permute-start | bytes 884744 | tf_op jit(solution)/shard_map/ppermute | solution.py:21
  23.6 96.8 %collective-permute-start.2 = (f32[16,1,6,384]{3,1,2,0:T(1,128)}, f32[16,1,6,384]{3,1,2,0:T(1,128)}, u32[]{:S(2)}, u32[]{:S(2)}) collective-permute-start(f32[16,1,6,384]{3,1,2,0:T(1,128)} %get-tuple-element.20), channel_id=1, source_target_pairs={{0,1},{1,2},{2,3},{3,4},{4,5},{5,6},{6,7},{8,9},{9,10},{10,11},{11... | collective-permute-start | bytes 442376 | tf_op jit(solution)/shard_map/ppermute | solution.py:21
  26.5 93.9 %collective-permute-start.3 = (f32[16,1,6,384]{3,1,2,0:T(1,128)}, f32[16,1,6,384]{3,1,2,0:T(1,128)}, u32[]{:S(2)}, u32[]{:S(2)}) collective-permute-start(f32[16,1,6,384]{3,1,2,0:T(1,128)} %get-tuple-element.19), channel_id=1, source_target_pairs={{1,0},{2,1},{3,2},{4,3},{5,4},{6,5},{7,6},{9,8},{10,9},{11,10},{12... | collective-permute-start | bytes 442376 | tf_op jit(solution)/shard_map/ppermute | solution.py:21
  120.4 7.4 %copy-start.9 = (f32[5,5]{1,0:T(8,128)S(1)}, f32[5,5]{1,0:T(8,128)}, u32[]{:S(2)}) copy-start(f32[5,5]{1,0:T(8,128)} %param.11) | copy-start | bytes 304
  120.4 15.2 %copy-start.8 = (f32[1,32,6,384]{3,1,2,0:T(8,128)}, f32[1,32,6,384]{3,1,2,0:T(8,128)S(1)}, u32[]{:S(2)}) copy-start(f32[1,32,6,384]{3,1,2,0:T(8,128)S(1)} %collective-permute-done) | copy-start | bytes 884740
  120.4 15.2 %copy-start.7 = (f32[1,32,6,384]{3,1,2,0:T(8,128)}, f32[1,32,6,384]{3,1,2,0:T(8,128)S(1)}, u32[]{:S(2)}) copy-start(f32[1,32,6,384]{3,1,2,0:T(8,128)S(1)} %collective-permute-done.1) | copy-start | bytes 884740
  120.4 99.4 %all-to-all-start.1 = ((f32[32,5,16,384]{3,2,1,0:T(8,128)}), f32[32,5,16,384]{3,2,1,0:T(8,128)}, u32[]{:S(2)}, u32[]{:S(2)}) async-start(f32[32,5,16,384]{3,2,1,0:T(8,128)} %shard_map.65), calls=%async_computation.1 | async-start | bytes 7864320 | tf_op jit(solution)/shard_map/all_to_all | solution.py:119
  127.8 2.1 copy-start.3
  136.1 0.9 slice-start
  136.1 1.1 slice-start.1

commit v12 on v11

--- a/solution.py
+++ b/solution.py
@@ -103,6 +103,27 @@
     )(x)
 
 
+def finish_kernel(ret_ref, local_ref, o_ref):
+    for v in range(ret_ref.shape[1]):
+        o_ref[:, v, :, :] = jnp.swapaxes(ret_ref[:, v, :, :], 0, 1) + section_step * local_ref[:, v, :, :]
+
+
+def finish(ret, local_t):
+    R, V, X, A = ret.shape
+    C = 128 if A % 128 == 0 else A
+    return pl.pallas_call(
+        finish_kernel,
+        out_shape=jax.ShapeDtypeStruct(local_t.shape, local_t.dtype),
+        grid=(A // C,),
+        in_specs=[
+            pl.BlockSpec((R, V, X, C), lambda a: (0, 0, 0, a)),
+            pl.BlockSpec((X, V, R, C), lambda a: (0, 0, 0, a)),
+        ],
+        out_specs=pl.BlockSpec((X, V, R, C), lambda a: (0, 0, 0, a)),
+        compiler_params=pltpu.CompilerParams(vmem_limit_bytes=48 * 1024 * 1024),
+    )(ret, local_t)
+
+
 def body(state, metric, deriv, filt_corr, jac_axial, jac_radial):
     nx, nr, nv, na = state.shape
     peers = lax.axis_size("ax")
@@ -120,7 +141,8 @@
     local = stencil(state, weight, ax_halo, rad_halo, jac_radial)
     local = with_layout_constraint(local, Layout(major_to_minor=(0, 2, 1, 3)))
     ret, local = lax.optimization_barrier((ret, local))
-    return jnp.transpose(ret, (2, 0, 1, 3)) + section_step * local
+    out = finish(ret, jnp.transpose(local, (0, 2, 1, 3)))
+    return jnp.transpose(out, (0, 2, 1, 3))
 
 
 def solution(mesh):

time: 227 us -> 227 us (level)
  other arithmetic: 17.6 us -> 10.9 us
  Pallas kernels: 15 us -> 21.2 us
    add x1 -> x0, other arithmetic: 6.63 us -> none  [body(): return jnp.transpose(ret, (2, 0, 1, 3)) + section_step * local]
    pallas_call x0 -> x1, Pallas kernels: none -> 6.22 us  [finish(): pl.pallas_call(finish_kernel, out_shape=jax.ShapeDtypeStruct(local_t.shap...]
where the time goes in v12:
time: 227 us; the launch traced here: 226 us
  waiting for transfers between devices  156 us (69%)
  starting transfers between devices  28.5 us (13%)
  Pallas kernels  21.2 us (9%)
  other arithmetic  10.9 us (5%)
  local copies, waits for them, and re-layouts  9.64 us (4%)
    all_to_all x1, waiting for transfers between devices, body(): lines = lax.all_to_all(send, 'ax', split_axis=0, concat_axis=0, tiled=True)  79 us
    all_to_all x1, waiting for transfers between devices, body(): ret = lax.all_to_all(res, 'ax', split_axis=0, concat_axis=0, tiled=True)  76.5 us
    all_to_all x1, starting transfers between devices, body(): lines = lax.all_to_all(send, 'ax', split_axis=0, concat_axis=0, tiled=True)  11.7 us
    pallas_call x1, Pallas kernels, line_section(): pl.pallas_call(line_kernel, out_shape=jax.ShapeDtypeStruct(lines.shape, l...  11.7 us
    ppermute x4, starting transfers between devices, halos(): return (lax.ppermute(last, axis, up), lax.ppermute(leading, axis, down))  9.37 us
    all_to_all x1, starting transfers between devices, body(): ret = lax.all_to_all(res, 'ax', split_axis=0, concat_axis=0, tiled=True)  7.35 us
    pallas_call x1, Pallas kernels, finish(): pl.pallas_call(finish_kernel, out_shape=jax.ShapeDtypeStruct(local_t.shap...  6.22 us
    add x1, other arithmetic, stencil(): return viscosity * visc_ax + (mixed + viscosity * visc_rad)  6.21 us
  transfers between devices with their start and end apart: 6, of which 2 were waited for; matrix products, arithmetic and copies ran while one was open for 7% of the time, Pallas kernels for 5%

profile of v12, /device:TPU:6, one launch (start us, length us, event | category | flops | bytes accessed | tf_op | source)
XLA Modules:
  0.0 226.1 jit_solution(17512013545531110931)
XLA Ops:
  0.0 3.3 %shard_map.64 = f32[32,5,16,384]{3,2,1,0:T(8,128)S(1)} custom-call(f32[16,5,32,384]{3,2,1,0:T(8,128)} %bitcast.38), custom_call_target="tpu_custom_call" | custom-call | tf_op jit(solution)/shard_map/pallas_call | solution.py:96
  3.3 1.9 copy-done
  5.2 11.7 %all-to-all-start = ((f32[32,5,16,384]{3,2,1,0:T(8,128)}), f32[32,5,16,384]{3,2,1,0:T(8,128)}, u32[]{:S(2)}, u32[]{:S(2)}) async-start(f32[32,5,16,384]{3,2,1,0:T(8,128)} %copy-done), calls=%async_computation | async-start | bytes 7864320 | tf_op jit(solution)/shard_map/all_to_all | solution.py:135
  17.0 2.1 pad_maximum_fusion.3
  19.1 2.2 collective-permute-start
  21.4 1.3 collective-permute-start.1
  22.7 0.9 pad_maximum_fusion.5
  23.6 2.8 %collective-permute-start.2 = (f32[16,1,6,384]{3,1,2,0:T(1,128)}, f32[16,1,6,384]{3,1,2,0:T(1,128)}, u32[]{:S(2)}, u32[]{:S(2)}) collective-permute-start(f32[16,1,6,384]{3,1,2,0:T(1,128)} %get-tuple-element.20), channel_id=1, source_target_pairs={{0,1},{1,2},{2,3},{3,4},{4,5},{5,6},{6,7},{8,9},{9,10},{10,11},{11... | collective-permute-start | bytes 442376 | tf_op jit(solution)/shard_map/ppermute | solution.py:21
  26.5 3.0 %collective-permute-start.3 = (f32[16,1,6,384]{3,1,2,0:T(1,128)}, f32[16,1,6,384]{3,1,2,0:T(1,128)}, u32[]{:S(2)}, u32[]{:S(2)}) collective-permute-start(f32[16,1,6,384]{3,1,2,0:T(1,128)} %get-tuple-element.19), channel_id=1, source_target_pairs={{1,0},{2,1},{3,2},{4,3},{5,4},{6,5},{7,6},{9,8},{10,9},{11,10},{12... | collective-permute-start | bytes 442376 | tf_op jit(solution)/shard_map/ppermute | solution.py:21
  29.7 79.0 %all-to-all-done.lines_ref = f32[32,5,16,384]{3,2,1,0:T(8,128)} async-done(((f32[32,5,16,384]{3,2,1,0:T(8,128)}), f32[32,5,16,384]{3,2,1,0:T(8,128)}, u32[]{:S(2)}, u32[]{:S(2)}) %all-to-all-start) | async-done | bytes 3932192 | tf_op jit(solution)/shard_map/all_to_all | solution.py:135
  108.7 11.7 %shard_map.65 = f32[32,5,16,384]{3,2,1,0:T(8,128)} custom-call(f32[5,5]{1,0:T(8,128)S(1)} %copy-done.1, f32[32,5,16,384]{3,2,1,0:T(8,128)} %all-to-all-done.lines_ref, f32[1024,512]{1,0:T(8,128)S(1)} %pad_maximum_fusion.2.mats_ref), custom_call_target="tpu_custom_call", output_to_operand_aliasing={{}: (1, {})} | custom-call | tf_op jit(solution)/shard_map/pallas_call | solution.py:77
  120.4 7.3 %all-to-all-start.1 = ((f32[32,5,16,384]{3,2,1,0:T(8,128)}), f32[32,5,16,384]{3,2,1,0:T(8,128)}, u32[]{:S(2)}, u32[]{:S(2)}) async-start(f32[32,5,16,384]{3,2,1,0:T(8,128)} %shard_map.65), calls=%async_computation.1 | async-start | bytes 7864320 | tf_op jit(solution)/shard_map/all_to_all | solution.py:140
  128.1 1.8 copy-done.3
  129.9 1.0 fusion.10
  130.9 0.8 fusion.9
  131.8 1.0 slice.107
  132.8 1.0 slice.106
  133.7 1.1 subtract_multiply_fusion
  134.8 0.8 slice_bitcast_fusion.9
  135.6 0.5 fusion.5
  136.5 0.6 slice-done
  137.2 6.2 %fusion.3 = f32[16,32,5,384]{3,1,2,0:T(8,128)} fusion(f32[16,32,5,384]{3,1,2,0:T(8,128)S(1)} %copy-done.3, f32[1,32,5,384]{3,1,2,0:T(8,128)S(1)} %slice-done, f32[15,32,5,384]{3,1,2,0:T(8,128)S(1)} %get-tuple-element.31, f32[15,32,5,384]{3,1,2,0:T(8,128)S(1)} %get-tuple-element.30, f32[1,32,5,384]{3,1,2,0:T(8,128)S(1)} %slice-done.1, ...), kind=kLoop, calls=%fused_computation.4 | loop fusion | flops 26542080 | bytes 30670948 | tf_op jit(solution)/shard_map/add | solution.py:43
  143.4 76.5 %all-to-all-done.1.ret_ref = f32[32,5,16,384]{3,2,1,0:T(8,128)} async-done(((f32[32,5,16,384]{3,2,1,0:T(8,128)}), f32[32,5,16,384]{3,2,1,0:T(8,128)}, u32[]{:S(2)}, u32[]{:S(2)}) %all-to-all-start.1) | async-done | bytes 3932192 | tf_op jit(solution)/shard_map/all_to_all | solution.py:140
  219.8 6.2 %shard_map.66 = f32[16,5,32,384]{3,2,1,0:T(8,128)} custom-call(f32[32,5,16,384]{3,2,1,0:T(8,128)} %all-to-all-done.1.ret_ref, f32[16,5,32,384]{3,2,1,0:T(8,128)} %bitcast.43), custom_call_target="tpu_custom_call" | custom-call | tf_op jit(solution)/shard_map/pallas_call | solution.py:114
  (32 shorter events, 1.0 us)
Async XLA Ops:
  3.3 1.9 copy-start
  5.2 11.8 %copy-start.4 = (f32[16,32,384]{2,1,0:T(8,128)S(1)}, f32[16,32,384]{2,1,0:T(8,128)}, u32[]{:S(2)}) copy-start(f32[16,32,384]{2,1,0:T(8,128)} %param.7) | copy-start | bytes 2359300
  5.2 103.5 %all-to-all-start = ((f32[32,5,16,384]{3,2,1,0:T(8,128)}), f32[32,5,16,384]{3,2,1,0:T(8,128)}, u32[]{:S(2)}, u32[]{:S(2)}) async-start(f32[32,5,16,384]{3,2,1,0:T(8,128)} %copy-done), calls=%async_computation | async-start | bytes 7864320 | tf_op jit(solution)/shard_map/all_to_all | solution.py:135
  17.0 5.7 %copy-start.2 = (f32[16,32,5,384]{3,1,2,0:T(8,128)S(1)}, f32[16,32,5,384]{3,1,2,0:T(8,128)}, u32[]{:S(2)}) copy-start(f32[16,32,5,384]{3,1,2,0:T(8,128)} %param.6) | copy-start | bytes 11796484
  17.0 12.5 %copy-start.5 = (f32[512,512]{1,0:T(8,128)S(1)}, f32[512,512]{1,0:T(8,128)}, u32[]{:S(2)}) copy-start(f32[512,512]{1,0:T(8,128)} %param.8) | copy-start | bytes 3145732
  17.0 12.5 %copy-start.6 = (f32[512,512]{1,0:T(8,128)S(1)}, f32[512,512]{1,0:T(8,128)}, u32[]{:S(2)}) copy-start(f32[512,512]{1,0:T(8,128)} %param.9) | copy-start | bytes 3145732
  19.1 101.3 %collective-permute-start = (f32[1,32,6,384]{3,1,2,0:T(8,128)}, f32[1,32,6,384]{3,1,2,0:T(8,128)S(1)}, u32[]{:S(2)}, u32[]{:S(2)}) collective-permute-start(f32[1,32,6,384]{3,1,2,0:T(8,128)} %get-tuple-element.22), channel_id=1, source_target_pairs={{0,8},{8,16},{16,24},{24,32},{32,40},{40,48},{48,56},{56,64},{64,7... | collective-permute-start | bytes 884744 | tf_op jit(solution)/shard_map/ppermute | solution.py:21
  21.4 87.4 %copy-start.1 = (f32[5,5]{1,0:T(8,128)S(1)}, f32[5,5]{1,0:T(8,128)}, u32[]{:S(2)}) copy-start(f32[5,5]{1,0:T(8,128)} %jac_ref.1) | copy-start | bytes 304
  21.4 99.0 %collective-permute-start.1 = (f32[1,32,6,384]{3,1,2,0:T(8,128)}, f32[1,32,6,384]{3,1,2,0:T(8,128)S(1)}, u32[]{:S(2)}, u32[]{:S(2)}) collective-permute-start(f32[1,32,6,384]{3,1,2,0:T(8,128)} %get-tuple-element.21), channel_id=1, source_target_pairs={{8,0},{16,8},{24,16},{32,24},{40,32},{48,40},{56,48},{64,56},{72,6... | collective-permute-start | bytes 884744 | tf_op jit(solution)/shard_map/ppermute | solution.py:21
  23.6 96.8 %collective-permute-start.2 = (f32[16,1,6,384]{3,1,2,0:T(1,128)}, f32[16,1,6,384]{3,1,2,0:T(1,128)}, u32[]{:S(2)}, u32[]{:S(2)}) collective-permute-start(f32[16,1,6,384]{3,1,2,0:T(1,128)} %get-tuple-element.20), channel_id=1, source_target_pairs={{0,1},{1,2},{2,3},{3,4},{4,5},{5,6},{6,7},{8,9},{9,10},{10,11},{11... | collective-permute-start | bytes 442376 | tf_op jit(solution)/shard_map/ppermute | solution.py:21
  26.5 93.9 %collective-permute-start.3 = (f32[16,1,6,384]{3,1,2,0:T(1,128)}, f32[16,1,6,384]{3,1,2,0:T(1,128)}, u32[]{:S(2)}, u32[]{:S(2)}) collective-permute-start(f32[16,1,6,384]{3,1,2,0:T(1,128)} %get-tuple-element.19), channel_id=1, source_target_pairs={{1,0},{2,1},{3,2},{4,3},{5,4},{6,5},{7,6},{9,8},{10,9},{11,10},{12... | collective-permute-start | bytes 442376 | tf_op jit(solution)/shard_map/ppermute | solution.py:21
  120.4 7.4 %copy-start.9 = (f32[5,5]{1,0:T(8,128)S(1)}, f32[5,5]{1,0:T(8,128)}, u32[]{:S(2)}) copy-start(f32[5,5]{1,0:T(8,128)} %param.11) | copy-start | bytes 304
  120.4 15.2 %copy-start.8 = (f32[1,32,6,384]{3,1,2,0:T(8,128)}, f32[1,32,6,384]{3,1,2,0:T(8,128)S(1)}, u32[]{:S(2)}) copy-start(f32[1,32,6,384]{3,1,2,0:T(8,128)S(1)} %collective-permute-done) | copy-start | bytes 884740
  120.4 15.2 %copy-start.7 = (f32[1,32,6,384]{3,1,2,0:T(8,128)}, f32[1,32,6,384]{3,1,2,0:T(8,128)S(1)}, u32[]{:S(2)}) copy-start(f32[1,32,6,384]{3,1,2,0:T(8,128)S(1)} %collective-permute-done.1) | copy-start | bytes 884740
  120.4 99.4 %all-to-all-start.1 = ((f32[32,5,16,384]{3,2,1,0:T(8,128)}), f32[32,5,16,384]{3,2,1,0:T(8,128)}, u32[]{:S(2)}, u32[]{:S(2)}) async-start(f32[32,5,16,384]{3,2,1,0:T(8,128)} %shard_map.65), calls=%async_computation.1 | async-start | bytes 7864320 | tf_op jit(solution)/shard_map/all_to_all | solution.py:140
  127.8 2.1 copy-start.3
  136.1 0.9 slice-start
  136.1 1.1 slice-start.1

commit v13 on v12

--- a/solution.py
+++ b/solution.py
@@ -49,13 +49,25 @@
     return hi.astype(jnp.bfloat16), (x - hi).astype(jnp.bfloat16)
 
 
-def line_kernel(jac_ref, lines_ref, mats_ref, out_ref):
+def split_kernel(m_ref, hi_ref, lo_ref):
+    hi, lo = split_bf16(m_ref[...])
+    hi_ref[...] = hi
+    lo_ref[...] = lo
+
+
+def split_mats(mats):
+    part = jax.ShapeDtypeStruct(mats.shape, jnp.bfloat16)
+    return pl.pallas_call(split_kernel, out_shape=(part, part))(mats)
+
+
+def line_kernel(jac_ref, lines_ref, hi_ref, lo_ref, out_ref):
     S, V, XL, C = lines_ref.shape
     nx = S * XL
     cols = [lines_ref[:, v, :, :].reshape(nx, C) for v in range(V)]
     wide = jnp.concatenate(cols, axis=1)
     w_hi, w_lo = split_bf16(wide)
-    m_hi, m_lo = split_bf16(mats_ref[...])
+    m_hi = hi_ref[...]
+    m_lo = lo_ref[...]
     prod = jnp.dot(m_hi, w_hi, preferred_element_type=jnp.float32)
     prod = prod + jnp.dot(m_hi, w_lo, preferred_element_type=jnp.float32)
     prod = prod + jnp.dot(m_lo, w_hi, preferred_element_type=jnp.float32)
@@ -78,11 +90,11 @@
         line_kernel,
         out_shape=jax.ShapeDtypeStruct(lines.shape, lines.dtype),
         grid=(A // C,),
-        in_specs=[pl.BlockSpec(memory_space=pltpu.SMEM), block, whole],
+        in_specs=[pl.BlockSpec(memory_space=pltpu.SMEM), block, whole, whole],
         out_specs=block,
         input_output_aliases={1: 0},
         compiler_params=pltpu.CompilerParams(vmem_limit_bytes=48 * 1024 * 1024),
-    )(jac_axial, lines, mats)
+    )(jac_axial, lines, *split_mats(mats))
 
 
 def swap_kernel(x_ref, o_ref):

time: 227 us -> 229 us (level)
  Pallas kernels: 21.2 us -> 24.1 us
    pallas_call x0 -> x1, Pallas kernels: none -> 3.19 us  [split_mats(): return pl.pallas_call(split_kernel, out_shape=(part, part))(mats)]
    all_to_all x1, waiting for transfers between devices: 79 us -> 76 us  [body(): lines = lax.all_to_all(send, 'ax', split_axis=0, concat_axis=0, tiled=True)]
    all_to_all x1, waiting for transfers between devices: 76.5 us -> 79 us  [body(): ret = lax.all_to_all(res, 'ax', split_axis=0, concat_axis=0, tiled=True)]
    unnamed x20 -> x24, local copies, waits for them, and re-layouts: 3.74 us -> 6.2 us
  transfers between devices with their start and end apart: 6 -> 6, of which waited for: 2 -> 2; matrix products, arithmetic and copies ran while one was open for 7% -> 6% of each run, Pallas kernels for 5% -> 6%
where the time goes in v13:
time: 229 us; the launch traced here: 228 us
  waiting for transfers between devices  155 us (68%)
  starting transfers between devices  28.5 us (12%)
  Pallas kernels  24.1 us (11%)
  other arithmetic  10.8 us (5%)
  local copies, waits for them, and re-layouts  9.53 us (4%)
    all_to_all x1, waiting for transfers between devices, body(): ret = lax.all_to_all(res, 'ax', split_axis=0, concat_axis=0, tiled=True)  79 us
    all_to_all x1, waiting for transfers between devices, body(): lines = lax.all_to_all(send, 'ax', split_axis=0, concat_axis=0, tiled=True)  76 us
    all_to_all x1, starting transfers between devices, body(): lines = lax.all_to_all(send, 'ax', split_axis=0, concat_axis=0, tiled=True)  11.7 us
    pallas_call x1, Pallas kernels, line_section(): pl.pallas_call(line_kernel, out_shape=jax.ShapeDtypeStruct(lines.shape, l...  11.4 us
    ppermute x4, starting transfers between devices, halos(): return (lax.ppermute(last, axis, up), lax.ppermute(leading, axis, down))  9.4 us
    all_to_all x1, starting transfers between devices, body(): ret = lax.all_to_all(res, 'ax', split_axis=0, concat_axis=0, tiled=True)  7.35 us
    add x1, other arithmetic, stencil(): return viscosity * visc_ax + (mixed + viscosity * visc_rad)  6.23 us
    pallas_call x1, Pallas kernels, finish(): pl.pallas_call(finish_kernel, out_shape=jax.ShapeDtypeStruct(local_t.shap...  6.21 us
  transfers between devices with their start and end apart: 6, of which 2 were waited for; matrix products, arithmetic and copies ran while one was open for 6% of the time, Pallas kernels for 6%

profile of v13, /device:TPU:6, one launch (start us, length us, event | category | flops | bytes accessed | tf_op | source)
XLA Modules:
  0.0 228.2 jit_solution(11636352583417329545)
XLA Ops:
  0.0 3.3 %shard_map.64 = f32[32,5,16,384]{3,2,1,0:T(8,128)S(1)} custom-call(f32[16,5,32,384]{3,2,1,0:T(8,128)} %bitcast.38), custom_call_target="tpu_custom_call" | custom-call | tf_op jit(solution)/shard_map/pallas_call | solution.py:108
  3.3 1.9 copy-done
  5.2 11.7 %all-to-all-start = ((f32[32,5,16,384]{3,2,1,0:T(8,128)}), f32[32,5,16,384]{3,2,1,0:T(8,128)}, u32[]{:S(2)}, u32[]{:S(2)}) async-start(f32[32,5,16,384]{3,2,1,0:T(8,128)} %copy-done), calls=%async_computation | async-start | bytes 7864320 | tf_op jit(solution)/shard_map/all_to_all | solution.py:147
  17.0 1.3 pad_maximum_fusion.3
  18.3 2.3 collective-permute-start
  20.6 1.3 collective-permute-start.1
  22.1 2.8 %collective-permute-start.2 = (f32[16,1,6,384]{3,1,2,0:T(1,128)S(1)}, f32[16,1,6,384]{3,1,2,0:T(1,128)S(1)}, u32[]{:S(2)}, u32[]{:S(2)}) collective-permute-start(f32[16,1,6,384]{3,1,2,0:T(1,128)S(1)} %get-tuple-element.24), channel_id=1, source_target_pairs={{0,1},{1,2},{2,3},{3,4},{4,5},{5,6},{6,7},{8,9},{9,10},{10,11},{11... | collective-permute-start | bytes 442376 | tf_op jit(solution)/shard_map/ppermute | solution.py:21
  24.9 3.0 %collective-permute-start.3 = (f32[16,1,6,384]{3,1,2,0:T(1,128)S(1)}, f32[16,1,6,384]{3,1,2,0:T(1,128)S(1)}, u32[]{:S(2)}, u32[]{:S(2)}) collective-permute-start(f32[16,1,6,384]{3,1,2,0:T(1,128)S(1)} %get-tuple-element.23), channel_id=1, source_target_pairs={{1,0},{2,1},{3,2},{4,3},{5,4},{6,5},{7,6},{9,8},{10,9},{11,10},{12... | collective-permute-start | bytes 442376 | tf_op jit(solution)/shard_map/ppermute | solution.py:21
  28.0 1.5 pad_maximum_fusion.2.m_ref
  29.5 3.2 %shard_map.65 = (bf16[1024,512]{1,0:T(8,128)(2,1)}, bf16[1024,512]{1,0:T(8,128)(2,1)}) custom-call(f32[1024,512]{1,0:T(8,128)} %pad_maximum_fusion.2.m_ref), custom_call_target="tpu_custom_call" | custom-call | tf_op jit(solution)/shard_map/pallas_call | solution.py:60
  32.7 76.0 %all-to-all-done.lines_ref = f32[32,5,16,384]{3,2,1,0:T(8,128)} async-done(((f32[32,5,16,384]{3,2,1,0:T(8,128)}), f32[32,5,16,384]{3,2,1,0:T(8,128)}, u32[]{:S(2)}, u32[]{:S(2)}) %all-to-all-start) | async-done | bytes 3932192 | tf_op jit(solution)/shard_map/all_to_all | solution.py:147
  108.7 1.2 copy-done.1
  109.9 1.2 copy-done.2
  111.2 11.4 %shard_map.66 = f32[32,5,16,384]{3,2,1,0:T(8,128)} custom-call(f32[5,5]{1,0:T(8,128)S(1)} %copy-done.3, f32[32,5,16,384]{3,2,1,0:T(8,128)} %all-to-all-done.lines_ref, bf16[1024,512]{1,0:T(8,128)(2,1)S(1)} %copy-done.1, bf16[1024,512]{1,0:T(8,128)(2,1)S(1)} %copy-done.2), custom_call_target="tpu_custom_call", output_to_operand_aliasing={{}: (1, {})} | custom-call | tf_op jit(solution)/shard_map/pallas_call | solution.py:89
  122.6 7.3 %all-to-all-start.1 = ((f32[32,5,16,384]{3,2,1,0:T(8,128)}), f32[32,5,16,384]{3,2,1,0:T(8,128)}, u32[]{:S(2)}, u32[]{:S(2)}) async-start(f32[32,5,16,384]{3,2,1,0:T(8,128)} %shard_map.66), calls=%async_computation.1 | async-start | bytes 7864320 | tf_op jit(solution)/shard_map/all_to_all | solution.py:152
  130.3 1.8 copy-done.5
  132.1 1.0 fusion.10
  133.1 0.8 fusion.9
  134.1 1.1 subtract_multiply_fusion
  135.3 0.5 fusion.5
  136.1 0.6 slice-done
  136.8 6.2 %fusion.3 = f32[16,32,5,384]{3,1,2,0:T(8,128)} fusion(f32[16,32,5,384]{3,1,2,0:T(8,128)S(1)} %copy-done.5, f32[1,32,5,384]{3,1,2,0:T(8,128)S(1)} %slice-done, f32[15,32,5,384]{3,1,2,0:T(8,128)S(1)} %get-tuple-element.35, f32[15,32,5,384]{3,1,2,0:T(8,128)S(1)} %get-tuple-element.34, f32[1,32,5,384]{3,1,2,0:T(8,128)S(1)} %slice-done.1, ...), kind=kLoop, calls=%fused_computation.4 | loop fusion | flops 26542080 | bytes 30670948 | tf_op jit(solution)/shard_map/add | solution.py:43
  143.1 79.0 %all-to-all-done.1.ret_ref = f32[32,5,16,384]{3,2,1,0:T(8,128)} async-done(((f32[32,5,16,384]{3,2,1,0:T(8,128)}), f32[32,5,16,384]{3,2,1,0:T(8,128)}, u32[]{:S(2)}, u32[]{:S(2)}) %all-to-all-start.1) | async-done | bytes 3932192 | tf_op jit(solution)/shard_map/all_to_all | solution.py:152
  222.0 6.2 %shard_map.67 = f32[16,5,32,384]{3,2,1,0:T(8,128)} custom-call(f32[32,5,16,384]{3,2,1,0:T(8,128)} %all-to-all-done.1.ret_ref, f32[16,5,32,384]{3,2,1,0:T(8,128)} %bitcast.43), custom_call_target="tpu_custom_call" | custom-call | tf_op jit(solution)/shard_map/pallas_call | solution.py:126
  (37 shorter events, 1.2 us)
Async XLA Ops:
  3.3 1.9 copy-start
  5.2 11.8 %copy-start.6 = (f32[16,32,384]{2,1,0:T(8,128)S(1)}, f32[16,32,384]{2,1,0:T(8,128)}, u32[]{:S(2)}) copy-start(f32[16,32,384]{2,1,0:T(8,128)} %param.7) | copy-start | bytes 2359300
  5.2 103.5 %all-to-all-start = ((f32[32,5,16,384]{3,2,1,0:T(8,128)}), f32[32,5,16,384]{3,2,1,0:T(8,128)}, u32[]{:S(2)}, u32[]{:S(2)}) async-start(f32[32,5,16,384]{3,2,1,0:T(8,128)} %copy-done), calls=%async_computation | async-start | bytes 7864320 | tf_op jit(solution)/shard_map/all_to_all | solution.py:147
  17.0 4.9 %copy-start.4 = (f32[16,32,5,384]{3,1,2,0:T(8,128)S(1)}, f32[16,32,5,384]{3,1,2,0:T(8,128)}, u32[]{:S(2)}) copy-start(f32[16,32,5,384]{3,1,2,0:T(8,128)} %param.6) | copy-start | bytes 11796484
  17.0 10.9 %copy-start.7 = (f32[512,512]{1,0:T(8,128)S(1)}, f32[512,512]{1,0:T(8,128)}, u32[]{:S(2)}) copy-start(f32[512,512]{1,0:T(8,128)} %param.8) | copy-start | bytes 3145732
  17.0 10.9 %copy-start.8 = (f32[512,512]{1,0:T(8,128)S(1)}, f32[512,512]{1,0:T(8,128)}, u32[]{:S(2)}) copy-start(f32[512,512]{1,0:T(8,128)} %param.9) | copy-start | bytes 3145732
  18.3 104.3 %collective-permute-start = (f32[1,32,6,384]{3,1,2,0:T(8,128)S(1)}, f32[1,32,6,384]{3,1,2,0:T(8,128)S(1)}, u32[]{:S(2)}, u32[]{:S(2)}) collective-permute-start(f32[1,32,6,384]{3,1,2,0:T(8,128)S(1)} %get-tuple-element.26), channel_id=1, source_target_pairs={{0,8},{8,16},{16,24},{24,32},{32,40},{40,48},{48,56},{56,64},{64,7... | collective-permute-start | bytes 884744 | tf_op jit(solution)/shard_map/ppermute | solution.py:21
  20.6 102.1 %collective-permute-start.1 = (f32[1,32,6,384]{3,1,2,0:T(8,128)S(1)}, f32[1,32,6,384]{3,1,2,0:T(8,128)S(1)}, u32[]{:S(2)}, u32[]{:S(2)}) collective-permute-start(f32[1,32,6,384]{3,1,2,0:T(8,128)S(1)} %get-tuple-element.25), channel_id=1, source_target_pairs={{8,0},{16,8},{24,16},{32,24},{40,32},{48,40},{56,48},{64,56},{72,6... | collective-permute-start | bytes 884744 | tf_op jit(solution)/shard_map/ppermute | solution.py:21
  22.1 86.6 %copy-start.3 = (f32[5,5]{1,0:T(8,128)S(1)}, f32[5,5]{1,0:T(8,128)}, u32[]{:S(2)}) copy-start(f32[5,5]{1,0:T(8,128)} %jac_ref.1) | copy-start | bytes 304
  22.1 100.5 %collective-permute-start.2 = (f32[16,1,6,384]{3,1,2,0:T(1,128)S(1)}, f32[16,1,6,384]{3,1,2,0:T(1,128)S(1)}, u32[]{:S(2)}, u32[]{:S(2)}) collective-permute-start(f32[16,1,6,384]{3,1,2,0:T(1,128)S(1)} %get-tuple-element.24), channel_id=1, source_target_pairs={{0,1},{1,2},{2,3},{3,4},{4,5},{5,6},{6,7},{8,9},{9,10},{10,11},{11... | collective-permute-start | bytes 442376 | tf_op jit(solution)/shard_map/ppermute | solution.py:21
  24.9 97.6 %collective-permute-start.3 = (f32[16,1,6,384]{3,1,2,0:T(1,128)S(1)}, f32[16,1,6,384]{3,1,2,0:T(1,128)S(1)}, u32[]{:S(2)}, u32[]{:S(2)}) collective-permute-start(f32[16,1,6,384]{3,1,2,0:T(1,128)S(1)} %get-tuple-element.23), channel_id=1, source_target_pairs={{1,0},{2,1},{3,2},{4,3},{5,4},{6,5},{7,6},{9,8},{10,9},{11,10},{12... | collective-permute-start | bytes 442376 | tf_op jit(solution)/shard_map/ppermute | solution.py:21
  108.7 1.2 copy-start.1
  109.9 1.2 copy-start.2
  122.6 7.4 %copy-start.11 = (f32[5,5]{1,0:T(8,128)S(1)}, f32[5,5]{1,0:T(8,128)}, u32[]{:S(2)}) copy-start(f32[5,5]{1,0:T(8,128)} %param.11) | copy-start | bytes 304
  122.6 12.6 %copy-start.10 = (f32[1,32,6,384]{3,1,2,0:T(8,128)}, f32[1,32,6,384]{3,1,2,0:T(8,128)S(1)}, u32[]{:S(2)}) copy-start(f32[1,32,6,384]{3,1,2,0:T(8,128)S(1)} %collective-permute-done) | copy-start | bytes 884740
  122.6 12.6 %copy-start.9 = (f32[1,32,6,384]{3,1,2,0:T(8,128)}, f32[1,32,6,384]{3,1,2,0:T(8,128)S(1)}, u32[]{:S(2)}) copy-start(f32[1,32,6,384]{3,1,2,0:T(8,128)S(1)} %collective-permute-done.1) | copy-start | bytes 884740
  122.6 99.4 %all-to-all-start.1 = ((f32[32,5,16,384]{3,2,1,0:T(8,128)}), f32[32,5,16,384]{3,2,1,0:T(8,128)}, u32[]{:S(2)}, u32[]{:S(2)}) async-start(f32[32,5,16,384]{3,2,1,0:T(8,128)} %shard_map.66), calls=%async_computation.1 | async-start | bytes 7864320 | tf_op jit(solution)/shard_map/all_to_all | solution.py:152
  130.0 2.1 copy-start.5
  135.8 0.9 slice-start
  135.8 1.1 slice-start.1
